TPU v7x, 512 devices: a whole 4x8x8 slice. The times are simulated.
512 devices in a mesh: pp: 4 (over x_lo, core), cp: 16 (over z, x_hi), tp: 8 (over y).
Axes of the slice: x: 4 (x_hi: 2, x_lo: 2; x = x_hi * 2 + x_lo), y: 8, z: 8, core: 2. Of those that a mesh axis runs over, the one named last changes fastest.
Arguments:
- query: bfloat16 [4, 2048, 16384], P('pp', 'cp', 'tp'), may hold values from -200 to 200
- key: bfloat16 [4, 2048, 1024], P('pp', 'cp', 'tp'), may hold values from -6 to 6
- value: bfloat16 [4, 2048, 1024], P('pp', 'cp', 'tp'), may hold values from -6 to 6
- out_grad: bfloat16 [4, 2048, 16384], P('pp', 'cp', 'tp'), may hold values from -24 to 24
- lengths: int32 [6], replicated, may hold values from 1 to 1024, 2048 in all
- plan: int32 [16, 16], replicated, may hold values from 0 to 15, each once within a row
Outputs:
- handed_grad: bfloat16 [4, 2048, 16384], P('pp', 'cp', 'tp')
- key_grad: bfloat16 [4, 2048, 1024], P('pp', 'cp', 'tp')
- value_grad: bfloat16 [4, 2048, 1024], P('pp', 'cp', 'tp')
Inputs may be any that keep to these rules, and one draw needn't show every extreme that they name: Row s of plan is a permutation: for each of the blocks of 8 tokens of context shard s it names the shard that takes the block.
All inputs are finite; a program needn't handle non-finite values.
Results may differ from a plain program's by a relative error of at most 0.0085.
Values may be sent and summed in bfloat16 or wider, within the bound.
No kernel may reach another device: no remote copies, remote signals or barrier semaphores. Data moves between devices by JAX's collectives and lax.ppermute only.
A program may use at most 64 MiB of HBM per device.

v0:
```python
import jax
import jax.numpy as jnp
from jax import lax
from jax.sharding import PartitionSpec as P


def passed_along(array, axis, by):
    peers = lax.axis_size(axis)
    pairs = [(i, i + by) for i in range(peers) if 0 <= i + by < peers]
    return lax.ppermute(array, axis, pairs)


def attend(query_rows, grad_rows, query_pos, key_full, value_full, owner):
    tokens = query_rows.shape[0]
    head_width = key_full.shape[1]
    head_count = query_rows.shape[1] // head_width
    key_count = key_full.shape[0]
    total_rows = tokens * head_count
    score_scale = head_width ** (-0.5)
    flat_query = query_rows.reshape(total_rows, head_width)
    flat_grad = grad_rows.reshape(total_rows, head_width)
    row_pos = jnp.repeat(query_pos, head_count)
    row_doc = jnp.repeat(jnp.take(owner, query_pos), head_count)
    block_width = min(512, key_count)
    block_count = key_count // block_width
    key_pos = jnp.arange(key_count, dtype=jnp.int32)
    blocks = (
        key_full.reshape(block_count, block_width, head_width),
        value_full.reshape(block_count, block_width, head_width),
        key_pos.reshape(block_count, block_width),
        owner.reshape(block_count, block_width),
    )

    def masked_scores(key_block, pos_block, doc_block):
        scores = jnp.dot(flat_query, key_block.T, preferred_element_type=jnp.float32) * score_scale
        seen = (doc_block[None, :] == row_doc[:, None]) & (pos_block[None, :] <= row_pos[:, None])
        return jnp.where(seen, scores, -jnp.inf)

    def first_pass(state, block):
        top, total, weighted = state
        key_block, value_block, pos_block, doc_block = block
        scores = masked_scores(key_block, pos_block, doc_block)
        new_top = jnp.maximum(top, jnp.max(scores, axis=1))
        expo = jnp.exp(scores - new_top[:, None])
        shrink = jnp.exp(top - new_top)
        dprob = jnp.dot(flat_grad, value_block.T, preferred_element_type=jnp.float32)
        total = total * shrink + jnp.sum(expo, axis=1)
        weighted = weighted * shrink + jnp.sum(expo * dprob, axis=1)
        return ((new_top, total, weighted), None)

    start = (
        jnp.full((total_rows,), -1e30, jnp.float32),
        jnp.zeros((total_rows,), jnp.float32),
        jnp.zeros((total_rows,), jnp.float32),
    )
    (top, total, weighted), unused = lax.scan(first_pass, start, blocks)
    delta = weighted / total

    def second_pass(dquery, block):
        key_block, value_block, pos_block, doc_block = block
        scores = masked_scores(key_block, pos_block, doc_block)
        probs = jnp.exp(scores - top[:, None]) / total[:, None]
        dprob = jnp.dot(flat_grad, value_block.T, preferred_element_type=jnp.float32)
        probs_low = probs.astype(jnp.bfloat16)
        dscore = (probs * (dprob - delta[:, None]) * score_scale).astype(jnp.bfloat16)
        dvalue = jnp.dot(probs_low.T, flat_grad, preferred_element_type=jnp.float32)
        dkey = jnp.dot(dscore.T, flat_query, preferred_element_type=jnp.float32)
        dquery = dquery + jnp.dot(dscore, key_block, preferred_element_type=jnp.float32)
        return (dquery, jnp.concatenate([dkey, dvalue], axis=1))

    dquery, terms = lax.scan(second_pass, jnp.zeros((total_rows, head_width), jnp.float32), blocks)
    dquery = dquery.astype(jnp.bfloat16).reshape(tokens, head_count * head_width)
    return (dquery, terms.reshape(key_count, 2 * head_width))


def body(query, key, value, out_grad, lengths, plan):
    tokens = query.shape[1]
    width = query.shape[2]
    head_width = key.shape[2]
    shards = lax.axis_size("cp")
    own_index = lax.axis_index("cp")
    block_rows = tokens // shards
    key_full, value_full = (
        lax.all_gather(key[0], "cp", axis=0, tiled=True),
        lax.all_gather(value[0], "cp", axis=0, tiled=True),
    )
    key_count = key_full.shape[0]
    ends = jnp.cumsum(lengths)
    positions = jnp.arange(key_count, dtype=jnp.int32)
    owner = jnp.sum((positions[:, None] >= ends[None, :]).astype(jnp.int32), axis=1)
    iota = jnp.arange(shards, dtype=jnp.int32)
    inverse = jnp.sum(
        (plan[:, None, :] == iota[None, :, None]).astype(jnp.int32) * iota[None, None, :], axis=2
    )
    send_order = lax.dynamic_index_in_dim(inverse, own_index, 0, keepdims=False)

    def reorder(rows):
        grouped = rows.reshape(shards, block_rows, rows.shape[1])
        return jnp.take(grouped, send_order, axis=0)

    query_sent, grad_sent = (
        lax.all_to_all(reorder(query[0]), "cp", split_axis=0, concat_axis=0, tiled=True),
        lax.all_to_all(reorder(out_grad[0]), "cp", split_axis=0, concat_axis=0, tiled=True),
    )
    taken = lax.dynamic_index_in_dim(inverse, own_index, 1, keepdims=False)
    query_pos = (
        iota[:, None] * tokens
        + taken[:, None] * block_rows
        + jnp.arange(block_rows, dtype=jnp.int32)[None, :]
    ).reshape(tokens)
    dquery, terms = attend(
        query_sent.reshape(tokens, width),
        grad_sent.reshape(tokens, width),
        query_pos,
        key_full,
        value_full,
        owner,
    )
    handed = passed_along(dquery, "pp", -1)
    summed = lax.psum_scatter(terms, "cp", scatter_dimension=0, tiled=True)
    key_grad = summed[:, :head_width].astype(jnp.bfloat16)
    value_grad = summed[:, head_width:].astype(jnp.bfloat16)
    return (handed[None], key_grad[None], value_grad[None])


def solution(mesh):
    return jax.shard_map(
        body,
        mesh=mesh,
        in_specs=(
            P("pp", "cp", "tp"),
            P("pp", "cp", "tp"),
            P("pp", "cp", "tp"),
            P("pp", "cp", "tp"),
            P(),
            P(),
        ),
        out_specs=(P("pp", "cp", "tp"), P("pp", "cp", "tp"), P("pp", "cp", "tp")),
        check_vma=False,
    )
```

profile of v0, /device:TPU:56, one launch (start us, length us, event | category | flops | bytes accessed | tf_op | source)
XLA Modules:
  0.0 425.1 jit_solution(5239354460927206662)
XLA Ops:
  7.2 1.1 select_reduce_fusion
  8.9 1.6 gather_fusion.1
  10.6 1.1 broadcast_select_fusion
  11.7 12.9 %all-to-all-start.1 = ((bf16[16,8,2048]{2,1,0:T(8,128)(2,1)}), bf16[16,8,2048]{2,1,0:T(8,128)(2,1)S(1)}, u32[]{:S(2)}, u32[]{:S(2)}) async-start(bf16[16,8,2048]{2,1,0:T(8,128)(2,1)} %get-tuple-element.306), calls=%async_computation.1 | async-start | bytes 1048576 | tf_op jit(solution)/shard_map/all_to_all | solution.py:103
  25.1 18.1 %all-to-all-done.1 = bf16[16,8,2048]{2,1,0:T(8,128)(2,1)S(1)} async-done(((bf16[16,8,2048]{2,1,0:T(8,128)(2,1)}), bf16[16,8,2048]{2,1,0:T(8,128)(2,1)S(1)}, u32[]{:S(2)}, u32[]{:S(2)}) %all-to-all-start.1) | async-done | bytes 524320 | tf_op jit(solution)/shard_map/all_to_all | solution.py:103
  43.2 3.6 all-to-all-start
  47.1 1.1 gather_fusion
  48.3 49.1 %all-gather = bf16[1,2048,128]{2,1,0:T(8,128)(2,1)} all-gather(bf16[1,128,128]{2,1,0:T(8,128)(2,1)S(1)} %copy-done.1), channel_id=2, replica_groups=mesh['pp'=4,'cp'=16,'tp'=8] {'cp'}, dimensions={1}, use_global_device_ids=true | all-gather | bytes 557056 | tf_op jit(solution)/shard_map/all_gather | solution.py:84
  97.4 43.7 %all-gather.1 = bf16[1,2048,128]{2,1,0:T(8,128)(2,1)} all-gather(bf16[1,128,128]{2,1,0:T(8,128)(2,1)S(1)} %copy-done.2), channel_id=3, replica_groups=mesh['pp'=4,'cp'=16,'tp'=8] {'cp'}, dimensions={1}, use_global_device_ids=true | all-gather | bytes 557056 | tf_op jit(solution)/shard_map/all_gather | solution.py:85
  141.4 1.0 reshape_reshape.6
  142.4 20.0 %while.28 = (s32[]{:T(128)}, f32[2048]{0:T(1024)S(1)}, f32[2048]{0:T(1024)S(1)}, f32[2048]{0:T(1024)S(1)}, s32[4,512]{1,0:T(4,128)S(1)}, /*index=5*/s32[4,512]{1...) while((s32[]{:T(128)}, f32[2048]{0:T(1024)S(1)}, ...), condition=%wide.region_7.9_spmd.clone, body=%wide.region_3.0_spmd.clone.sunk | while | flops 548419584 | bytes 14120100 | solution.py:56
  142.8 2.2 fusion.69
  145.0 1.8 fusion.70
  147.8 2.2 fusion.69
  150.0 1.8 fusion.70
  152.8 2.2 fusion.69
  155.0 1.8 fusion.70
  157.8 2.2 fusion.69
  160.0 1.8 fusion.70
  162.5 41.5 %while.29 = (s32[]{:T(128)}, f32[2048,128]{1,0:T(8,128)S(1)}, f32[4,512,256]{2,1,0:T(8,128)}, s32[4,512]{1,0:T(4,128)S(1)}, s32[4,512]{1,0:T(4,128)S(1)}, /*inde...) while((s32[]{:T(128)}, f32[2048,128]{1,0:T(8,128)S(1)}, ...), condition=%wide.region_9.11_spmd.clone, body=%wide.region_8.10_spmd.clone.sunk | while | flops 1355415552 | bytes 27235516 | solution.py:71
  162.8 2.6 fusion.83
  165.4 0.8 fusion.85
  166.3 1.6 fusion.84
  167.9 1.9 fusion.86
  169.8 2.0 convolution_add_fusion.2
  172.0 0.8 constant_dynamic-update-slice_fusion.2
  173.2 2.6 fusion.83
  175.8 0.8 fusion.85
  176.6 1.6 fusion.84
  178.3 1.9 fusion.86
  180.2 2.0 convolution_add_fusion.2
  182.4 0.8 constant_dynamic-update-slice_fusion.2
  183.6 2.6 fusion.83
  186.2 0.8 fusion.85
  187.0 1.6 fusion.84
  188.7 1.9 fusion.86
  190.6 2.0 convolution_add_fusion.2
  192.8 0.9 constant_dynamic-update-slice_fusion.2
  194.0 2.6 fusion.83
  196.6 0.8 fusion.85
  197.4 1.6 fusion.84
  199.1 1.9 fusion.86
  200.9 2.0 convolution_add_fusion.2
  203.2 0.9 constant_dynamic-update-slice_fusion.2
  204.3 1.3 collective-permute-start
  205.6 2.5 collective-permute-done
  208.1 207.8 %reduce-scatter.2.cloned.1.call-done = f32[128,256]{1,0:T(8,128)} async-done(((f32[2048,256]{1,0:T(8,128)}), f32[128,256]{1,0:T(8,128)}) %reduce-scatter.2.cloned.1.call-update) | async-done | bytes 131088 | tf_op jit(solution)/shard_map/reduce_scatter | solution.py:120
  416.0 0.9 convert.4
  (100 shorter events, 9.7 us)
Async XLA Ops:
  7.2 1.2 copy-start
  7.2 17.4 %copy-start.3 = (s32[6]{0:T(128)S(1)}, s32[6]{0:T(128)}, u32[]{:S(2)}) copy-start(s32[6]{0:T(128)} %param.16) | copy-start | bytes 76
  7.2 41.1 %copy-start.1 = (bf16[1,128,128]{2,1,0:T(8,128)(2,1)S(1)}, bf16[1,128,128]{2,1,0:T(8,128)(2,1)}, u32[]{:S(2)}) copy-start(bf16[1,128,128]{2,1,0:T(8,128)(2,1)} %param.13) | copy-start | bytes 98308
  7.2 90.2 %copy-start.2 = (bf16[1,128,128]{2,1,0:T(8,128)(2,1)S(1)}, bf16[1,128,128]{2,1,0:T(8,128)(2,1)}, u32[]{:S(2)}) copy-start(bf16[1,128,128]{2,1,0:T(8,128)(2,1)} %param.14) | copy-start | bytes 98308
  11.7 31.5 %all-to-all-start.1 = ((bf16[16,8,2048]{2,1,0:T(8,128)(2,1)}), bf16[16,8,2048]{2,1,0:T(8,128)(2,1)S(1)}, u32[]{:S(2)}, u32[]{:S(2)}) async-start(bf16[16,8,2048]{2,1,0:T(8,128)(2,1)} %get-tuple-element.306), calls=%async_computation.1 | async-start | bytes 1048576 | tf_op jit(solution)/shard_map/all_to_all | solution.py:103
  43.2 98.1 %all-to-all-start = ((bf16[16,8,2048]{2,1,0:T(8,128)(2,1)}), bf16[16,8,2048]{2,1,0:T(8,128)(2,1)S(1)}, u32[]{:S(2)}, u32[]{:S(2)}) async-start(bf16[16,8,2048]{2,1,0:T(8,128)(2,1)} %get-tuple-element.307), calls=%async_computation | async-start | bytes 1048576 | tf_op jit(solution)/shard_map/all_to_all | solution.py:102
  46.8 369.1 %reduce-scatter.2.cloned.1.call-start = ((), (), s32[]{:S(2)}) async-start(), calls=%async_computation.3 | async-start | bytes 2228224 | tf_op jit(solution)/shard_map/reduce_scatter | solution.py:120
  204.3 3.8 collective-permute-start
Sparse Core Ops, SparseCore 0:
  204.1 211.7 reduce-scatter.1
where the time goes:
time: 427 us; the launch traced here: 425 us
  waiting for transfers between devices  228 us (53%)
  blocking collectives  92.8 us (22%)
  matrix products  51.4 us (12%)
  starting transfers between devices  17.8 us (4%)
  between operations  14.3 us (3%)
  local copies, waits for them, and re-layouts  13.4 us (3%)
  other arithmetic  6.55 us (2%)
    reduce_scatter x1, waiting for transfers between devices, body(): summed = lax.psum_scatter(terms, 'cp', scatter_dimension=0, tiled=True)  208 us
    all_gather x1, blocking collectives, body(): lax.all_gather(key[0], 'cp', axis=0, tiled=True)  49.1 us
    all_gather x1, blocking collectives, body(): lax.all_gather(value[0], 'cp', axis=0, tiled=True)  43.7 us
    dot_general x8, matrix products, masked_scores(): jnp.dot(flat_query, key_block.T, preferred_element_type=jnp.float32)  19 us
    all_to_all x1, waiting for transfers between devices, body(): lax.all_to_all(reorder(out_grad[0]), 'cp', split_axis=0, concat_axis=0, t...  18.1 us
    all_to_all x1, starting transfers between devices, body(): lax.all_to_all(reorder(out_grad[0]), 'cp', split_axis=0, concat_axis=0, t...  12.9 us
  transfers between devices with their start and end apart: 4, of which 3 were waited for; matrix products, arithmetic and copies ran while one was open for 1% of the time, Pallas kernels for 0%

commit v1 on v0

--- a/solution.py
+++ b/solution.py
@@ -80,14 +80,7 @@
     shards = lax.axis_size("cp")
     own_index = lax.axis_index("cp")
     block_rows = tokens // shards
-    key_full, value_full = (
-        lax.all_gather(key[0], "cp", axis=0, tiled=True),
-        lax.all_gather(value[0], "cp", axis=0, tiled=True),
-    )
-    key_count = key_full.shape[0]
-    ends = jnp.cumsum(lengths)
-    positions = jnp.arange(key_count, dtype=jnp.int32)
-    owner = jnp.sum((positions[:, None] >= ends[None, :]).astype(jnp.int32), axis=1)
+    key_count = shards * tokens
     iota = jnp.arange(shards, dtype=jnp.int32)
     inverse = jnp.sum(
         (plan[:, None, :] == iota[None, :, None]).astype(jnp.int32) * iota[None, None, :], axis=2
@@ -98,10 +91,25 @@
         grouped = rows.reshape(shards, block_rows, rows.shape[1])
         return jnp.take(grouped, send_order, axis=0)
 
-    query_sent, grad_sent = (
-        lax.all_to_all(reorder(query[0]), "cp", split_axis=0, concat_axis=0, tiled=True),
-        lax.all_to_all(reorder(out_grad[0]), "cp", split_axis=0, concat_axis=0, tiled=True),
+    row_width = block_rows * width
+    key_width = tokens * 2 * head_width
+    own_keys = jnp.concatenate([key[0], value[0]], axis=1).reshape(1, key_width)
+    packed = jnp.concatenate(
+        [
+            reorder(query[0]).reshape(shards, row_width),
+            reorder(out_grad[0]).reshape(shards, row_width),
+            jnp.broadcast_to(own_keys, (shards, key_width)),
+        ],
+        axis=1,
     )
+    received = lax.all_to_all(packed, "cp", split_axis=0, concat_axis=0, tiled=True)
+    query_sent = received[:, :row_width]
+    grad_sent = received[:, row_width : 2 * row_width]
+    keys_all = received[:, 2 * row_width :].reshape(key_count, 2 * head_width)
+    key_full, value_full = keys_all[:, :head_width], keys_all[:, head_width:]
+    ends = jnp.cumsum(lengths)
+    positions = jnp.arange(key_count, dtype=jnp.int32)
+    owner = jnp.sum((positions[:, None] >= ends[None, :]).astype(jnp.int32), axis=1)
     taken = lax.dynamic_index_in_dim(inverse, own_index, 1, keepdims=False)
     query_pos = (
         iota[:, None] * tokens
@@ -117,7 +125,10 @@
         owner,
     )
     handed = passed_along(dquery, "pp", -1)
-    summed = lax.psum_scatter(terms, "cp", scatter_dimension=0, tiled=True)
+    partials = lax.all_to_all(
+        terms.reshape(shards, tokens, 2 * head_width), "cp", split_axis=0, concat_axis=0, tiled=True
+    )
+    summed = jnp.sum(partials, axis=0)
     key_grad = summed[:, :head_width].astype(jnp.bfloat16)
     value_grad = summed[:, head_width:].astype(jnp.bfloat16)
     return (handed[None], key_grad[None], value_grad[None])

time: 427 us -> 223 us (0.52)
  waiting for transfers between devices: 228 us -> 99.7 us
  blocking collectives: 92.8 us -> 0 us
  local copies, waits for them, and re-layouts: 13.4 us -> 40.3 us
  between operations: 14.3 us -> 0.9 us
    reduce_scatter x1 -> x0, waiting for transfers between devices: 208 us -> none  [body(): summed = lax.psum_scatter(terms, 'cp', scatter_dimension=0, tiled=True)]
    all_gather x2 -> x0, blocking collectives: 92.8 us -> none  [the longest x1 49.1 us: body(): lax.all_gather(key[0], 'cp', axis=0, tiled=True)]
    all_to_all x2, waiting for transfers between devices: 18.1 us -> 97.2 us  [the longest x1 50.1 us: body(): lax.all_to_all(packed, 'cp', split_axis=0, concat_axis=0, tiled=True)]
    unnamed x9 -> x11, local copies, waits for them, and re-layouts: 0.81 us -> 20.4 us
  transfers between devices with their start and end apart: 4 -> 3, of which waited for: 3 -> 3; matrix products, arithmetic and copies ran while one was open for 1% -> 1% of each run, Pallas kernels for 0% -> 0%
where the time goes in v1:
time: 223 us; the launch traced here: 222 us
  waiting for transfers between devices  99.7 us (45%)
  matrix products  51.4 us (23%)
  local copies, waits for them, and re-layouts  40.3 us (18%)
  starting transfers between devices  18.7 us (8%)
  other arithmetic  10.4 us (5%)
    all_to_all x1, waiting for transfers between devices, body(): lax.all_to_all(packed, 'cp', split_axis=0, concat_axis=0, tiled=True)  50.1 us
    all_to_all x1, waiting for transfers between devices, body(): lax.all_to_all(terms.reshape(shards, tokens, 2 * head_width), 'cp', split...  47.1 us
    unnamed x11, local copies, waits for them, and re-layouts  20.4 us
    dot_general x8, matrix products, masked_scores(): jnp.dot(flat_query, key_block.T, preferred_element_type=jnp.float32)  19 us
    all_to_all x1, starting transfers between devices, body(): lax.all_to_all(packed, 'cp', split_axis=0, concat_axis=0, tiled=True)  12.9 us
    dot_general x4, matrix products, second_pass(): jnp.dot(dscore, key_block, preferred_element_type=jnp.float32)  7.85 us
    dot_general x4, matrix products, second_pass(): dkey = jnp.dot(dscore.T, flat_query, preferred_element_type=jnp.float32)  7.47 us
    dot_general x4, matrix products, first_pass(): jnp.dot(flat_grad, value_block.T, preferred_element_type=jnp.float32)  7.12 us
  transfers between devices with their start and end apart: 3, of which 3 were waited for; matrix products, arithmetic and copies ran while one was open for 1% of the time, Pallas kernels for 0%

profile of v1, /device:TPU:56, one launch (start us, length us, event | category | flops | bytes accessed | tf_op | source)
XLA Modules:
  0.0 221.8 jit_solution(2269640365677569492)
XLA Ops:
  0.6 1.1 select_reduce_fusion
  3.2 1.6 gather_fusion.1
  6.5 2.9 %reduce.2 = bf16[16,65536]{1,0:T(8,128)(2,1)} reduce(bf16[16,1,65536]{2,0,1:T(8,128)(2,1)S(1)} %maximum_bitcast_fusion.1, bf16[]{:T(256)} %broadcast.153), dimensions={1}, to_apply=%copy.15.reduce_sub_computation | reduce | bytes 4194306 | tf_op jit(solution)/shard_map/all_to_all | solution.py:105
  9.3 4.1 %reshape.174 = bf16[16,2,32768]{2,1,0:T(2,128)(2,1)} reshape(bf16[16,65536]{1,0:T(8,128)(2,1)} %reduce.2) | data formatting | bytes 4194304
  13.4 12.9 %all-to-all-start = ((bf16[16,2,32768]{2,1,0:T(2,128)(2,1)}), bf16[16,2,32768]{2,1,0:T(2,128)(2,1)}, u32[]{:S(2)}, u32[]{:S(2)}) async-start(bf16[16,2,32768]{2,1,0:T(2,128)(2,1)} %reshape.174), calls=%async_computation | async-start | bytes 4194304 | tf_op jit(solution)/shard_map/all_to_all | solution.py:105
  27.2 1.1 gather_fusion
  28.3 50.1 %all-to-all-done = bf16[16,2,32768]{2,1,0:T(2,128)(2,1)} async-done(((bf16[16,2,32768]{2,1,0:T(2,128)(2,1)}), bf16[16,2,32768]{2,1,0:T(2,128)(2,1)}, u32[]{:S(2)}, u32[]{:S(2)}) %all-to-all-start) | async-done | bytes 2097184 | tf_op jit(solution)/shard_map/all_to_all | solution.py:105
  78.4 10.4 %reshape.175 = bf16[16,1,65536]{2,1,0:T(2,128)(2,1)} reshape(bf16[16,2,32768]{2,1,0:T(2,128)(2,1)} %all-to-all-done) | data formatting | bytes 4194304
  88.9 4.5 %copy.25 = bf16[16,1,65536]{2,0,1:T(8,128)(2,1)S(1)} copy(bf16[16,1,65536]{2,1,0:T(2,128)(2,1)} %reshape.175) | data formatting | bytes 4194304
  93.4 1.1 fusion.36
  94.5 1.3 reshape_reshape.10
  95.8 1.3 reshape.135
  97.1 2.3 %fusion.37 = (bf16[2048,128]{1,0:T(8,128)(2,1)}, bf16[2048,128]{1,0:T(8,128)(2,1)}) fusion(bf16[2048,256]{1,0:T(8,128)(2,1)} %reshape.135), kind=kLoop, calls=%fused_computation.73 | loop fusion | bytes 2097152 | tf_op jit(solution)/shard_map/slice | solution.py:109
  99.4 2.1 reshape_reshape.9
  101.4 20.1 %while.28 = (s32[]{:T(128)}, f32[2048]{0:T(1024)S(1)}, f32[2048]{0:T(1024)S(1)}, f32[2048]{0:T(1024)S(1)}, s32[4,512]{1,0:T(4,128)S(1)}, /*index=5*/s32[4,512]{1...) while((s32[]{:T(128)}, f32[2048]{0:T(1024)S(1)}, ...), condition=%wide.region_7.9_spmd.clone, body=%wide.region_3.8_spmd.clone.sunk | while | flops 548419584 | bytes 14120100 | solution.py:56
  101.8 2.2 fusion.71
  104.0 1.8 fusion.72
  106.8 2.2 fusion.71
  109.0 1.8 fusion.72
  111.8 2.2 fusion.71
  114.0 1.8 fusion.72
  116.8 2.2 fusion.71
  119.0 1.8 fusion.72
  121.5 41.5 %while.29 = (s32[]{:T(128)}, f32[2048,128]{1,0:T(8,128)S(1)}, f32[4,512,256]{2,1,0:T(8,128)}, s32[4,512]{1,0:T(4,128)S(1)}, s32[4,512]{1,0:T(4,128)S(1)}, /*inde...) while((s32[]{:T(128)}, f32[2048,128]{1,0:T(8,128)S(1)}, ...), condition=%wide.region_9.11_spmd.clone, body=%wide.region_8.10_spmd.clone.sunk | while | flops 1355415552 | bytes 27235516 | solution.py:71
  121.9 2.6 %fusion.85 = f32[2048,512]{0,1:T(8,128)S(1)} fusion(bf16[2048,128]{1,0:T(8,128)(2,1)} %get-tuple-element.566, f32[2048]{0:T(1024)S(1)} %get-tuple-element.568, f32[2048]{0:T(1024)S(1)} %get-tuple-element.567, s32[2048]{0:T(1024)S(1)} %le.82, s32[2048]{0:T(1024)S(1)} %eq.82, s32[512]{0:T(512)S(1)} %bitcast.136, s32[512]{0:T(512)S(1)} %bitcast.137, ...), kind=kOutput, calls=%fused_computation.32.clone.1 | convolution fusion | flops 275775488 | bytes 4886532 | tf_op jit(solution)/shard_map/while/body/eval_jaxpr/dot_general | solution.py:35
  125.3 1.6 fusion.86
  127.0 1.9 fusion.88
  128.9 2.0 convolution_add_fusion.2
  132.2 2.6 %fusion.85 = f32[2048,512]{0,1:T(8,128)S(1)} fusion(bf16[2048,128]{1,0:T(8,128)(2,1)} %get-tuple-element.566, f32[2048]{0:T(1024)S(1)} %get-tuple-element.568, f32[2048]{0:T(1024)S(1)} %get-tuple-element.567, s32[2048]{0:T(1024)S(1)} %le.82, s32[2048]{0:T(1024)S(1)} %eq.82, s32[512]{0:T(512)S(1)} %bitcast.136, s32[512]{0:T(512)S(1)} %bitcast.137, ...), kind=kOutput, calls=%fused_computation.32.clone.1 | convolution fusion | flops 275775488 | bytes 4886532 | tf_op jit(solution)/shard_map/while/body/eval_jaxpr/dot_general | solution.py:35
  135.7 1.6 fusion.86
  137.3 1.9 fusion.88
  139.2 2.0 convolution_add_fusion.2
  141.4 0.9 constant_dynamic-update-slice_fusion.2
  142.6 2.6 %fusion.85 = f32[2048,512]{0,1:T(8,128)S(1)} fusion(bf16[2048,128]{1,0:T(8,128)(2,1)} %get-tuple-element.566, f32[2048]{0:T(1024)S(1)} %get-tuple-element.568, f32[2048]{0:T(1024)S(1)} %get-tuple-element.567, s32[2048]{0:T(1024)S(1)} %le.82, s32[2048]{0:T(1024)S(1)} %eq.82, s32[512]{0:T(512)S(1)} %bitcast.136, s32[512]{0:T(512)S(1)} %bitcast.137, ...), kind=kOutput, calls=%fused_computation.32.clone.1 | convolution fusion | flops 275775488 | bytes 4886532 | tf_op jit(solution)/shard_map/while/body/eval_jaxpr/dot_general | solution.py:35
  146.0 1.6 fusion.86
  147.7 1.9 fusion.88
  149.6 2.0 convolution_add_fusion.2
  151.8 0.8 constant_dynamic-update-slice_fusion.2
  153.0 2.6 %fusion.85 = f32[2048,512]{0,1:T(8,128)S(1)} fusion(bf16[2048,128]{1,0:T(8,128)(2,1)} %get-tuple-element.566, f32[2048]{0:T(1024)S(1)} %get-tuple-element.568, f32[2048]{0:T(1024)S(1)} %get-tuple-element.567, s32[2048]{0:T(1024)S(1)} %le.82, s32[2048]{0:T(1024)S(1)} %eq.82, s32[512]{0:T(512)S(1)} %bitcast.136, s32[512]{0:T(512)S(1)} %bitcast.137, ...), kind=kOutput, calls=%fused_computation.32.clone.1 | convolution fusion | flops 275775488 | bytes 4886532 | tf_op jit(solution)/shard_map/while/body/eval_jaxpr/dot_general | solution.py:35
  156.4 1.6 fusion.86
  158.0 1.9 fusion.88
  159.9 2.0 convolution_add_fusion.2
  162.1 0.8 constant_dynamic-update-slice_fusion.2
  163.0 4.4 %all-to-all-start.1 = ((f32[16,128,256]{2,1,0:T(8,128)}), f32[16,128,256]{2,1,0:T(8,128)}, u32[]{:S(2)}, u32[]{:S(2)}) async-start(f32[16,128,256]{2,1,0:T(8,128)} %bitcast.130), calls=%async_computation.1 | async-start | bytes 4194304 | tf_op jit(solution)/shard_map/all_to_all | solution.py:128
  167.7 1.3 collective-permute-start
  169.0 2.5 %collective-permute-done = bf16[128,2048]{1,0:T(8,128)(2,1)S(1)} collective-permute-done((bf16[128,2048]{1,0:T(8,128)(2,1)S(1)}, bf16[128,2048]{1,0:T(8,128)(2,1)S(1)}, u32[]{:S(2)}, u32[]{:S(2)}) %collective-permute-start) | collective-permute-done | bytes 524320 | tf_op jit(solution)/shard_map/ppermute | solution.py:10
  171.5 47.1 %all-to-all-done.1 = f32[16,128,256]{2,1,0:T(8,128)} async-done(((f32[16,128,256]{2,1,0:T(8,128)}), f32[16,128,256]{2,1,0:T(8,128)}, u32[]{:S(2)}, u32[]{:S(2)}) %all-to-all-start.1) | async-done | bytes 2097184 | tf_op jit(solution)/shard_map/all_to_all | solution.py:128
  218.7 1.7 reduce_sum.47
  (106 shorter events, 16.0 us)
Async XLA Ops:
  0.6 2.0 copy-start
  9.3 17.5 %copy-start.1 = (s32[6]{0:T(128)S(1)}, s32[6]{0:T(128)}, u32[]{:S(2)}) copy-start(s32[6]{0:T(128)} %param.16) | copy-start | bytes 76
  13.4 65.1 %all-to-all-start = ((bf16[16,2,32768]{2,1,0:T(2,128)(2,1)}), bf16[16,2,32768]{2,1,0:T(2,128)(2,1)}, u32[]{:S(2)}, u32[]{:S(2)}) async-start(bf16[16,2,32768]{2,1,0:T(2,128)(2,1)} %reshape.174), calls=%async_computation | async-start | bytes 4194304 | tf_op jit(solution)/shard_map/all_to_all | solution.py:105
  163.0 55.7 %all-to-all-start.1 = ((f32[16,128,256]{2,1,0:T(8,128)}), f32[16,128,256]{2,1,0:T(8,128)}, u32[]{:S(2)}, u32[]{:S(2)}) async-start(f32[16,128,256]{2,1,0:T(8,128)} %bitcast.130), calls=%async_computation.1 | async-start | bytes 4194304 | tf_op jit(solution)/shard_map/all_to_all | solution.py:128
  167.7 3.8 %collective-permute-start = (bf16[128,2048]{1,0:T(8,128)(2,1)S(1)}, bf16[128,2048]{1,0:T(8,128)(2,1)S(1)}, u32[]{:S(2)}, u32[]{:S(2)}) collective-permute-start(bf16[128,2048]{1,0:T(8,128)(2,1)S(1)} %reshape.138), channel_id=1, source_target_pairs={{128,0},{256,128},{384,256},{129,1},{257,129},{385,257},{130,2},{2... | collective-permute-start | bytes 1572872 | tf_op jit(solution)/shard_map/ppermute | solution.py:10

commit v2 on v1

--- a/solution.py
+++ b/solution.py
@@ -91,22 +91,22 @@
         grouped = rows.reshape(shards, block_rows, rows.shape[1])
         return jnp.take(grouped, send_order, axis=0)
 
-    row_width = block_rows * width
-    key_width = tokens * 2 * head_width
-    own_keys = jnp.concatenate([key[0], value[0]], axis=1).reshape(1, key_width)
+    key_rows = tokens * head_width // width
+    own_keys = jnp.concatenate([key[0].reshape(key_rows, width), value[0].reshape(key_rows, width)], axis=0)
     packed = jnp.concatenate(
         [
-            reorder(query[0]).reshape(shards, row_width),
-            reorder(out_grad[0]).reshape(shards, row_width),
-            jnp.broadcast_to(own_keys, (shards, key_width)),
+            reorder(query[0]),
+            reorder(out_grad[0]),
+            jnp.broadcast_to(own_keys[None], (shards,) + own_keys.shape),
         ],
         axis=1,
     )
     received = lax.all_to_all(packed, "cp", split_axis=0, concat_axis=0, tiled=True)
-    query_sent = received[:, :row_width]
-    grad_sent = received[:, row_width : 2 * row_width]
-    keys_all = received[:, 2 * row_width :].reshape(key_count, 2 * head_width)
-    key_full, value_full = keys_all[:, :head_width], keys_all[:, head_width:]
+    query_sent = received[:, :block_rows]
+    grad_sent = received[:, block_rows : 2 * block_rows]
+    key_at = 2 * block_rows
+    key_full = received[:, key_at : key_at + key_rows].reshape(key_count, head_width)
+    value_full = received[:, key_at + key_rows :].reshape(key_count, head_width)
     ends = jnp.cumsum(lengths)
     positions = jnp.arange(key_count, dtype=jnp.int32)
     owner = jnp.sum((positions[:, None] >= ends[None, :]).astype(jnp.int32), axis=1)

time: 223 us -> 202 us (0.906)
  local copies, waits for them, and re-layouts: 40.3 us -> 21.9 us
  other arithmetic: 10.4 us -> 8.01 us
    unnamed x11 -> x5, local copies, waits for them, and re-layouts: 20.4 us -> 0.81 us
    another operation x0 -> x4, local copies, waits for them, and re-layouts: none -> 4.67 us  [the longest x1 2.08 us: attend(): value_full.reshape(block_count, block_width, head_width)]
    all_to_all x2 -> x0, other arithmetic: 3.14 us -> none  [body(): lax.all_to_all(packed, 'cp', split_axis=0, concat_axis=0, tiled=True)]
where the time goes in v2:
time: 202 us; the launch traced here: 201 us
  waiting for transfers between devices  99.7 us (49%)
  matrix products  51.4 us (25%)
  local copies, waits for them, and re-layouts  21.9 us (11%)
  starting transfers between devices  18.7 us (9%)
  other arithmetic  8.01 us (4%)
    all_to_all x1, waiting for transfers between devices, body(): lax.all_to_all(packed, 'cp', split_axis=0, concat_axis=0, tiled=True)  50.1 us
    all_to_all x1, waiting for transfers between devices, body(): lax.all_to_all(terms.reshape(shards, tokens, 2 * head_width), 'cp', split...  47.1 us
    dot_general x8, matrix products, masked_scores(): jnp.dot(flat_query, key_block.T, preferred_element_type=jnp.float32)  19.1 us
    all_to_all x1, starting transfers between devices, body(): lax.all_to_all(packed, 'cp', split_axis=0, concat_axis=0, tiled=True)  12.9 us
    dot_general x4, matrix products, second_pass(): jnp.dot(dscore, key_block, preferred_element_type=jnp.float32)  7.85 us
    dot_general x4, matrix products, second_pass(): dkey = jnp.dot(dscore.T, flat_query, preferred_element_type=jnp.float32)  7.48 us
    dot_general x4, matrix products, first_pass(): jnp.dot(flat_grad, value_block.T, preferred_element_type=jnp.float32)  7.12 us
    dot_general x4, matrix products, second_pass(): jnp.dot(flat_grad, value_block.T, preferred_element_type=jnp.float32)  6.53 us
  transfers between devices with their start and end apart: 3, of which 3 were waited for; matrix products, arithmetic and copies ran while one was open for 1% of the time, Pallas kernels for 0%

profile of v2, /device:TPU:56, one launch (start us, length us, event | category | flops | bytes accessed | tf_op | source)
XLA Modules:
  0.0 201.1 jit_solution(14366649219747702813)
XLA Ops:
  0.6 1.1 select_reduce_fusion
  3.9 1.6 gather_fusion.1
  5.9 1.6 pad_maximum_fusion
  7.5 12.9 %all-to-all-start = ((bf16[16,32,2048]{2,1,0:T(8,128)(2,1)}), bf16[16,32,2048]{2,1,0:T(8,128)(2,1)}, u32[]{:S(2)}, u32[]{:S(2)}) async-start(bf16[16,32,2048]{2,1,0:T(8,128)(2,1)} %pad_maximum_fusion), calls=%async_computation | async-start | bytes 4194304 | tf_op jit(solution)/shard_map/all_to_all | solution.py:104
  21.2 1.1 gather_fusion
  22.4 50.1 %all-to-all-done = bf16[16,32,2048]{2,1,0:T(8,128)(2,1)} async-done(((bf16[16,32,2048]{2,1,0:T(8,128)(2,1)}), bf16[16,32,2048]{2,1,0:T(8,128)(2,1)}, u32[]{:S(2)}, u32[]{:S(2)}) %all-to-all-start) | async-done | bytes 2097184 | tf_op jit(solution)/shard_map/all_to_all | solution.py:104
  72.5 2.7 %fusion.36 = (bf16[16,8,2048]{2,1,0:T(8,128)(2,1)}, bf16[16,8,2048]{2,1,0:T(8,128)(2,1)}, bf16[16,8,2048]{2,1,0:T(8,128)(2,1)S(1)}, bf16[16,8,2048]{2,1,0:T(8,128)(2,1)S(1)}) fusion(bf16[16,32,2048]{2,1,0:T(8,128)(2,1)} %all-to-all-done), kind=kLoop, calls=%fused_computation.71 | loop fusion | bytes 4194304 | tf_op jit(solution)/shard_map/slice | solution.py:106
  75.2 1.3 reshape_reshape.18
  76.5 2.1 %reshape_reshape.17 = bf16[4,512,128]{2,1,0:T(8,128)(2,1)} reshape(bf16[16,8,2048]{2,1,0:T(8,128)(2,1)} %get-tuple-element.305) | data formatting | bytes 1048576 | tf_op jit(solution)/shard_map/reshape;reshape | solution.py:29
  78.6 1.1 reshape_reshape.16
  79.6 1.0 reshape_reshape.15
  80.7 20.1 %while.28 = (s32[]{:T(128)}, f32[2048]{0:T(1024)S(1)}, f32[2048]{0:T(1024)S(1)}, f32[2048]{0:T(1024)S(1)}, s32[4,512]{1,0:T(4,128)S(1)}, /*index=5*/s32[4,512]{1...) while((s32[]{:T(128)}, f32[2048]{0:T(1024)S(1)}, ...), condition=%wide.region_7.9_spmd.clone, body=%wide.region_3.8_spmd.clone.sunk | while | flops 548419584 | bytes 14120100 | solution.py:56
  81.0 2.2 %fusion.70 = (f32[2048]{0:T(1024)S(1)}, f32[2048,512]{0,1:T(8,128)S(1)}) fusion(bf16[2048,128]{1,0:T(8,128)(2,1)} %get-tuple-element.521, bf16[4,512,128]{2,1,0:T(8,128)(2,1)} %get-tuple-element.520, s32[]{:T(128)S(6)} %copy.22, s32[2048]{0:T(1024)S(1)} %le.78, s32[512]{0:T(512)S(1)} %bitcast.111, s32[2048]{0:T(1024)S(1)} %eq.78, s32[512]{0:T(512)S(1)} %bitcast.112), kind=kOutput, calls=%fused_computation.70.clone.1 | convolution fusion | flops 274724864 | bytes 4878340 | tf_op jit(solution)/shard_map/while/body/eval_jaxpr/dot_general | solution.py:35
  83.2 1.8 fusion.71
  86.0 2.2 %fusion.70 = (f32[2048]{0:T(1024)S(1)}, f32[2048,512]{0,1:T(8,128)S(1)}) fusion(bf16[2048,128]{1,0:T(8,128)(2,1)} %get-tuple-element.521, bf16[4,512,128]{2,1,0:T(8,128)(2,1)} %get-tuple-element.520, s32[]{:T(128)S(6)} %copy.22, s32[2048]{0:T(1024)S(1)} %le.78, s32[512]{0:T(512)S(1)} %bitcast.111, s32[2048]{0:T(1024)S(1)} %eq.78, s32[512]{0:T(512)S(1)} %bitcast.112), kind=kOutput, calls=%fused_computation.70.clone.1 | convolution fusion | flops 274724864 | bytes 4878340 | tf_op jit(solution)/shard_map/while/body/eval_jaxpr/dot_general | solution.py:35
  88.2 1.8 fusion.71
  91.0 2.2 %fusion.70 = (f32[2048]{0:T(1024)S(1)}, f32[2048,512]{0,1:T(8,128)S(1)}) fusion(bf16[2048,128]{1,0:T(8,128)(2,1)} %get-tuple-element.521, bf16[4,512,128]{2,1,0:T(8,128)(2,1)} %get-tuple-element.520, s32[]{:T(128)S(6)} %copy.22, s32[2048]{0:T(1024)S(1)} %le.78, s32[512]{0:T(512)S(1)} %bitcast.111, s32[2048]{0:T(1024)S(1)} %eq.78, s32[512]{0:T(512)S(1)} %bitcast.112), kind=kOutput, calls=%fused_computation.70.clone.1 | convolution fusion | flops 274724864 | bytes 4878340 | tf_op jit(solution)/shard_map/while/body/eval_jaxpr/dot_general | solution.py:35
  93.2 1.8 fusion.71
  96.1 2.2 %fusion.70 = (f32[2048]{0:T(1024)S(1)}, f32[2048,512]{0,1:T(8,128)S(1)}) fusion(bf16[2048,128]{1,0:T(8,128)(2,1)} %get-tuple-element.521, bf16[4,512,128]{2,1,0:T(8,128)(2,1)} %get-tuple-element.520, s32[]{:T(128)S(6)} %copy.22, s32[2048]{0:T(1024)S(1)} %le.78, s32[512]{0:T(512)S(1)} %bitcast.111, s32[2048]{0:T(1024)S(1)} %eq.78, s32[512]{0:T(512)S(1)} %bitcast.112), kind=kOutput, calls=%fused_computation.70.clone.1 | convolution fusion | flops 274724864 | bytes 4878340 | tf_op jit(solution)/shard_map/while/body/eval_jaxpr/dot_general | solution.py:35
  98.3 1.8 fusion.71
  100.8 41.5 %while.29 = (s32[]{:T(128)}, f32[2048,128]{1,0:T(8,128)S(1)}, f32[4,512,256]{2,1,0:T(8,128)}, s32[4,512]{1,0:T(4,128)S(1)}, s32[4,512]{1,0:T(4,128)S(1)}, /*inde...) while((s32[]{:T(128)}, f32[2048,128]{1,0:T(8,128)S(1)}, ...), condition=%wide.region_9.11_spmd.clone, body=%wide.region_8.10_spmd.clone.sunk | while | flops 1355415552 | bytes 27235516 | solution.py:71
  101.1 2.6 %fusion.84 = f32[2048,512]{0,1:T(8,128)S(1)} fusion(bf16[2048,128]{1,0:T(8,128)(2,1)} %get-tuple-element.566, f32[2048]{0:T(1024)S(1)} %get-tuple-element.568, f32[2048]{0:T(1024)S(1)} %get-tuple-element.567, s32[2048]{0:T(1024)S(1)} %le.82, s32[2048]{0:T(1024)S(1)} %eq.82, s32[512]{0:T(512)S(1)} %bitcast.113, s32[512]{0:T(512)S(1)} %bitcast.114, ...), kind=kOutput, calls=%fused_computation.32.clone.1 | convolution fusion | flops 275775488 | bytes 4886532 | tf_op jit(solution)/shard_map/while/body/eval_jaxpr/dot_general | solution.py:35
  103.7 0.8 fusion.86
  104.6 1.6 fusion.85
  106.2 1.9 fusion.87
  108.1 2.0 convolution_add_fusion.2
  111.5 2.6 %fusion.84 = f32[2048,512]{0,1:T(8,128)S(1)} fusion(bf16[2048,128]{1,0:T(8,128)(2,1)} %get-tuple-element.566, f32[2048]{0:T(1024)S(1)} %get-tuple-element.568, f32[2048]{0:T(1024)S(1)} %get-tuple-element.567, s32[2048]{0:T(1024)S(1)} %le.82, s32[2048]{0:T(1024)S(1)} %eq.82, s32[512]{0:T(512)S(1)} %bitcast.113, s32[512]{0:T(512)S(1)} %bitcast.114, ...), kind=kOutput, calls=%fused_computation.32.clone.1 | convolution fusion | flops 275775488 | bytes 4886532 | tf_op jit(solution)/shard_map/while/body/eval_jaxpr/dot_general | solution.py:35
  114.1 0.8 fusion.86
  114.9 1.6 fusion.85
  116.5 1.9 fusion.87
  118.4 2.0 convolution_add_fusion.2
  120.6 0.8 constant_dynamic-update-slice_fusion.2
  121.8 2.6 %fusion.84 = f32[2048,512]{0,1:T(8,128)S(1)} fusion(bf16[2048,128]{1,0:T(8,128)(2,1)} %get-tuple-element.566, f32[2048]{0:T(1024)S(1)} %get-tuple-element.568, f32[2048]{0:T(1024)S(1)} %get-tuple-element.567, s32[2048]{0:T(1024)S(1)} %le.82, s32[2048]{0:T(1024)S(1)} %eq.82, s32[512]{0:T(512)S(1)} %bitcast.113, s32[512]{0:T(512)S(1)} %bitcast.114, ...), kind=kOutput, calls=%fused_computation.32.clone.1 | convolution fusion | flops 275775488 | bytes 4886532 | tf_op jit(solution)/shard_map/while/body/eval_jaxpr/dot_general | solution.py:35
  124.4 0.8 fusion.86
  125.3 1.6 fusion.85
  126.9 1.9 fusion.87
  128.8 2.0 convolution_add_fusion.2
  131.0 0.9 constant_dynamic-update-slice_fusion.2
  132.2 2.6 %fusion.84 = f32[2048,512]{0,1:T(8,128)S(1)} fusion(bf16[2048,128]{1,0:T(8,128)(2,1)} %get-tuple-element.566, f32[2048]{0:T(1024)S(1)} %get-tuple-element.568, f32[2048]{0:T(1024)S(1)} %get-tuple-element.567, s32[2048]{0:T(1024)S(1)} %le.82, s32[2048]{0:T(1024)S(1)} %eq.82, s32[512]{0:T(512)S(1)} %bitcast.113, s32[512]{0:T(512)S(1)} %bitcast.114, ...), kind=kOutput, calls=%fused_computation.32.clone.1 | convolution fusion | flops 275775488 | bytes 4886532 | tf_op jit(solution)/shard_map/while/body/eval_jaxpr/dot_general | solution.py:35
  135.7 1.6 fusion.85
  137.3 1.9 fusion.87
  139.2 2.0 convolution_add_fusion.2
  141.4 0.9 constant_dynamic-update-slice_fusion.2
  142.2 4.4 %all-to-all-start.1 = ((f32[16,128,256]{2,1,0:T(8,128)}), f32[16,128,256]{2,1,0:T(8,128)}, u32[]{:S(2)}, u32[]{:S(2)}) async-start(f32[16,128,256]{2,1,0:T(8,128)} %bitcast.108), calls=%async_computation.1 | async-start | bytes 4194304 | tf_op jit(solution)/shard_map/all_to_all | solution.py:128
  147.0 1.3 collective-permute-start
  148.3 2.5 %collective-permute-done = bf16[128,2048]{1,0:T(8,128)(2,1)S(1)} collective-permute-done((bf16[128,2048]{1,0:T(8,128)(2,1)S(1)}, bf16[128,2048]{1,0:T(8,128)(2,1)S(1)}, u32[]{:S(2)}, u32[]{:S(2)}) %collective-permute-start) | collective-permute-done | bytes 524320 | tf_op jit(solution)/shard_map/ppermute | solution.py:10
  150.8 47.1 %all-to-all-done.1 = f32[16,128,256]{2,1,0:T(8,128)} async-done(((f32[16,128,256]{2,1,0:T(8,128)}), f32[16,128,256]{2,1,0:T(8,128)}, u32[]{:S(2)}, u32[]{:S(2)}) %all-to-all-start.1) | async-done | bytes 2097184 | tf_op jit(solution)/shard_map/all_to_all | solution.py:128
  197.9 1.7 reduce_sum.47
  (99 shorter events, 12.9 us)
Async XLA Ops:
  0.6 2.7 %copy-start = (bf16[1,128,2048]{2,1,0:T(8,128)(2,1)S(1)}, bf16[1,128,2048]{2,1,0:T(8,128)(2,1)}, u32[]{:S(2)}) copy-start(bf16[1,128,2048]{2,1,0:T(8,128)(2,1)} %param.15) | copy-start | bytes 1572868
  5.9 15.0 %copy-start.1 = (s32[6]{0:T(128)S(1)}, s32[6]{0:T(128)}, u32[]{:S(2)}) copy-start(s32[6]{0:T(128)} %param.16) | copy-start | bytes 76
  7.5 65.1 %all-to-all-start = ((bf16[16,32,2048]{2,1,0:T(8,128)(2,1)}), bf16[16,32,2048]{2,1,0:T(8,128)(2,1)}, u32[]{:S(2)}, u32[]{:S(2)}) async-start(bf16[16,32,2048]{2,1,0:T(8,128)(2,1)} %pad_maximum_fusion), calls=%async_computation | async-start | bytes 4194304 | tf_op jit(solution)/shard_map/all_to_all | solution.py:104
  142.2 55.7 %all-to-all-start.1 = ((f32[16,128,256]{2,1,0:T(8,128)}), f32[16,128,256]{2,1,0:T(8,128)}, u32[]{:S(2)}, u32[]{:S(2)}) async-start(f32[16,128,256]{2,1,0:T(8,128)} %bitcast.108), calls=%async_computation.1 | async-start | bytes 4194304 | tf_op jit(solution)/shard_map/all_to_all | solution.py:128
  147.0 3.8 %collective-permute-start = (bf16[128,2048]{1,0:T(8,128)(2,1)S(1)}, bf16[128,2048]{1,0:T(8,128)(2,1)S(1)}, u32[]{:S(2)}, u32[]{:S(2)}) collective-permute-start(bf16[128,2048]{1,0:T(8,128)(2,1)S(1)} %reshape.115), channel_id=1, source_target_pairs={{128,0},{256,128},{384,256},{129,1},{257,129},{385,257},{130,2},{2... | collective-permute-start | bytes 1572872 | tf_op jit(solution)/shard_map/ppermute | solution.py:10

commit v3 on v2

v3 whole, which is shorter than its diff:
```python
import functools

import jax
import jax.numpy as jnp
from jax import lax
from jax.sharding import PartitionSpec as P
from jax.experimental import pallas as pl
from jax.experimental.pallas import tpu as pltpu


def passed_along(array, axis, by):
    peers = lax.axis_size(axis)
    pairs = [(i, i + by) for i in range(peers) if 0 <= i + by < peers]
    return lax.ppermute(array, axis, pairs)


def _doc_of(ends_ref, position):
    doc = jnp.int32(0)
    for i in range(ends_ref.shape[0]):
        doc = doc + (position >= ends_ref[i]).astype(jnp.int32)
    return doc


def _attend_kernel(heads, ends_ref, start_ref, q_ref, g_ref, k_ref, v_ref, dq_ref, dkv_ref, top_ref, total_ref, weighted_ref, dq_acc):
    rows, head_width = q_ref.shape
    keys = k_ref.shape[0]
    rb_size = rows // start_ref.shape[0]
    kb_size = 128
    row_blocks = rows // rb_size
    key_blocks = keys // kb_size
    tokens_per_block = rb_size // heads
    scale = head_width ** (-0.5)
    dkv_ref[...] = jnp.zeros_like(dkv_ref)
    row_iota = lax.broadcasted_iota(jnp.int32, (rb_size, kb_size), 0) // heads
    col_iota = lax.broadcasted_iota(jnp.int32, (rb_size, kb_size), 1)

    def vector_doc(position):
        doc = jnp.zeros(position.shape, jnp.int32)
        for i in range(ends_ref.shape[0]):
            doc = doc + (position >= ends_ref[i]).astype(jnp.int32)
        return doc

    def row_block(rb, carry):
        first = start_ref[rb]
        last = first + tokens_per_block - 1
        first_doc = _doc_of(ends_ref, first)
        last_doc = _doc_of(ends_ref, last)
        r0 = pl.multiple_of(rb * rb_size, rb_size)
        q = q_ref[pl.ds(r0, rb_size), :]
        g = g_ref[pl.ds(r0, rb_size), :]
        row_pos = first + row_iota
        row_doc = vector_doc(row_pos)
        top_ref[...] = jnp.full(top_ref.shape, -1e30, jnp.float32)
        total_ref[...] = jnp.zeros(total_ref.shape, jnp.float32)
        weighted_ref[...] = jnp.zeros(weighted_ref.shape, jnp.float32)
        dq_acc[...] = jnp.zeros(dq_acc.shape, jnp.float32)

        def seen(kb):
            k0 = kb * kb_size
            return (k0 <= last) & (_doc_of(ends_ref, k0) <= last_doc) & (_doc_of(ends_ref, k0 + kb_size - 1) >= first_doc)

        def scores_of(kb):
            k0 = pl.multiple_of(kb * kb_size, kb_size)
            k = k_ref[pl.ds(k0, kb_size), :]
            v = v_ref[pl.ds(k0, kb_size), :]
            s = lax.dot_general(q, k, (((1,), (1,)), ((), ())), preferred_element_type=jnp.float32) * scale
            key_pos = k0 + col_iota
            visible = (vector_doc(key_pos) == row_doc) & (key_pos <= row_pos)
            s = jnp.where(visible, s, -jnp.inf)
            dp = lax.dot_general(g, v, (((1,), (1,)), ((), ())), preferred_element_type=jnp.float32)
            return k0, k, s, dp

        def first_pass(kb, c):
            @pl.when(seen(kb))
            def _():
                _, _, s, dp = scores_of(kb)
                top = top_ref[...]
                new_top = jnp.maximum(top, jnp.max(s, axis=1, keepdims=True))
                expo = jnp.exp(s - new_top)
                shrink = jnp.exp(top - new_top)
                total_ref[...] = total_ref[...] * shrink + jnp.sum(expo, axis=1, keepdims=True)
                weighted_ref[...] = weighted_ref[...] * shrink + jnp.sum(expo * dp, axis=1, keepdims=True)
                top_ref[...] = new_top
            return c

        lax.fori_loop(0, key_blocks, first_pass, 0)
        top = top_ref[...]
        total = total_ref[...]
        delta = weighted_ref[...] / total

        def second_pass(kb, c):
            @pl.when(seen(kb))
            def _():
                k0, k, s, dp = scores_of(kb)
                probs = jnp.exp(s - top) / total
                probs_low = probs.astype(jnp.bfloat16)
                dscore = (probs * (dp - delta) * scale).astype(jnp.bfloat16)
                dv = lax.dot_general(probs_low, g, (((0,), (0,)), ((), ())), preferred_element_type=jnp.float32)
                dk = lax.dot_general(dscore, q, (((0,), (0,)), ((), ())), preferred_element_type=jnp.float32)
                dkv_ref[pl.ds(k0, kb_size), pl.ds(0, head_width)] += dk
                dkv_ref[pl.ds(k0, kb_size), pl.ds(head_width, head_width)] += dv
                dq_acc[...] += jnp.dot(dscore, k, preferred_element_type=jnp.float32)
            return c

        lax.fori_loop(0, key_blocks, second_pass, 0)
        dq_ref[pl.ds(r0, rb_size), :] = dq_acc[...].astype(dq_ref.dtype)
        return carry

    lax.fori_loop(0, row_blocks, row_block, 0)


def attend_kernel(flat_query, flat_grad, key_full, value_full, ends, block_start, heads):
    rows, head_width = flat_query.shape
    keys = key_full.shape[0]
    rb_size = rows // block_start.shape[0]
    vmem = pltpu.VMEM
    smem = pl.BlockSpec(memory_space=pltpu.SMEM)
    whole = pl.BlockSpec(memory_space=pltpu.VMEM)
    flops = 2 * rows * keys * head_width * 7
    return pl.pallas_call(
        functools.partial(_attend_kernel, heads),
        out_shape=(
            jax.ShapeDtypeStruct((rows, head_width), jnp.bfloat16),
            jax.ShapeDtypeStruct((keys, 2 * head_width), jnp.float32),
        ),
        in_specs=[smem, smem, whole, whole, whole, whole],
        out_specs=(whole, whole),
        scratch_shapes=[
            vmem((rb_size, 1), jnp.float32),
            vmem((rb_size, 1), jnp.float32),
            vmem((rb_size, 1), jnp.float32),
            vmem((rb_size, head_width), jnp.float32),
        ],
        compiler_params=pltpu.CompilerParams(vmem_limit_bytes=48 * 1024 * 1024),
        cost_estimate=pl.CostEstimate(flops=flops // 4, transcendentals=rows * keys // 2, bytes_accessed=rows * head_width * 6 + keys * head_width * 4 + keys * head_width * 8),
    )(ends, block_start, flat_query, flat_grad, key_full, value_full)


def body(query, key, value, out_grad, lengths, plan):
    tokens = query.shape[1]
    width = query.shape[2]
    head_width = key.shape[2]
    shards = lax.axis_size("cp")
    own_index = lax.axis_index("cp")
    block_rows = tokens // shards
    key_count = shards * tokens
    iota = jnp.arange(shards, dtype=jnp.int32)
    inverse = jnp.sum(
        (plan[:, None, :] == iota[None, :, None]).astype(jnp.int32) * iota[None, None, :], axis=2
    )
    send_order = lax.dynamic_index_in_dim(inverse, own_index, 0, keepdims=False)

    def reorder(rows):
        grouped = rows.reshape(shards, block_rows, rows.shape[1])
        return jnp.take(grouped, send_order, axis=0)

    key_rows = tokens * head_width // width
    own_keys = jnp.concatenate([key[0].reshape(key_rows, width), value[0].reshape(key_rows, width)], axis=0)
    packed = jnp.concatenate(
        [
            reorder(query[0]),
            reorder(out_grad[0]),
            jnp.broadcast_to(own_keys[None], (shards,) + own_keys.shape),
        ],
        axis=1,
    )
    received = lax.all_to_all(packed, "cp", split_axis=0, concat_axis=0, tiled=True)
    query_sent = received[:, :block_rows]
    grad_sent = received[:, block_rows : 2 * block_rows]
    key_at = 2 * block_rows
    key_full = received[:, key_at : key_at + key_rows].reshape(key_count, head_width)
    value_full = received[:, key_at + key_rows :].reshape(key_count, head_width)
    ends = jnp.cumsum(lengths).astype(jnp.int32)
    taken = lax.dynamic_index_in_dim(inverse, own_index, 1, keepdims=False)
    head_count = width // head_width
    dquery, terms = attend_kernel(
        query_sent.reshape(tokens * head_count, head_width),
        grad_sent.reshape(tokens * head_count, head_width),
        key_full,
        value_full,
        ends,
        iota * tokens + taken * block_rows,
        head_count,
    )
    dquery = dquery.reshape(tokens, width)
    handed = passed_along(dquery, "pp", -1)
    partials = lax.all_to_all(
        terms.reshape(shards, tokens, 2 * head_width), "cp", split_axis=0, concat_axis=0, tiled=True
    )
    summed = jnp.sum(partials, axis=0)
    key_grad = summed[:, :head_width].astype(jnp.bfloat16)
    value_grad = summed[:, head_width:].astype(jnp.bfloat16)
    return (handed[None], key_grad[None], value_grad[None])


def solution(mesh):
    return jax.shard_map(
        body,
        mesh=mesh,
        in_specs=(
            P("pp", "cp", "tp"),
            P("pp", "cp", "tp"),
            P("pp", "cp", "tp"),
            P("pp", "cp", "tp"),
            P(),
            P(),
        ),
        out_specs=(P("pp", "cp", "tp"), P("pp", "cp", "tp"), P("pp", "cp", "tp")),
        check_vma=False,
    )
```

time: 202 us -> 203 us (level)
  Pallas kernels: 0 us -> 57.5 us
  matrix products: 51.4 us -> 0 us
  local copies, waits for them, and re-layouts: 21.9 us -> 10.6 us
  starting transfers between devices: 18.7 us -> 28.7 us
  other arithmetic: 8.01 us -> 3.37 us
    pallas_call x0 -> x1, Pallas kernels: none -> 57.5 us  [attend_kernel(): pl.pallas_call(functools.partial(_attend_kernel, heads), out_shape=(jax.S...]
    dot_general x28 -> x0, matrix products: 51.4 us -> none  [the longest x8 19.1 us: masked_scores(): jnp.dot(flat_query, key_block.T, preferred_element_type=jnp.float32)]
    all_to_all x1, starting transfers between devices: 4.44 us -> 14.4 us  [body(): lax.all_to_all(terms.reshape(shards, tokens, 2 * head_width), 'cp', split...]
    another operation x4 -> x0, local copies, waits for them, and re-layouts: 5.45 us -> none  [the longest x1 2.08 us: attend(): value_full.reshape(block_count, block_width, head_width)]
    dynamic_update_slice x8 -> x0, local copies, waits for them, and re-layouts: 4.17 us -> none  [attend(): lax.scan(second_pass, jnp.zeros((total_rows, head_width), jnp.float32), b...]
    reshape x2 -> x5, local copies, waits for them, and re-layouts: 0.23 us -> 4.13 us  [the longest x1 1.34 us: body(): value_full = received[:, key_at + key_rows:].reshape(key_count, head_width)]
    reduce_sum x5 -> x0, other arithmetic: 2.66 us -> none  [the longest x4 2.57 us: first_pass(): total = total * shrink + jnp.sum(expo, axis=1)]
where the time goes in v3:
time: 203 us; the launch traced here: 202 us
  waiting for transfers between devices  101 us (50%)
  Pallas kernels  57.5 us (28%)
  starting transfers between devices  28.7 us (14%)
  local copies, waits for them, and re-layouts  10.6 us (5%)
  other arithmetic  3.37 us (2%)
    pallas_call x1, Pallas kernels, attend_kernel(): pl.pallas_call(functools.partial(_attend_kernel, heads), out_shape=(jax.S...  57.5 us
    all_to_all x1, waiting for transfers between devices, body(): lax.all_to_all(packed, 'cp', split_axis=0, concat_axis=0, tiled=True)  51.7 us
    all_to_all x1, waiting for transfers between devices, body(): lax.all_to_all(terms.reshape(shards, tokens, 2 * head_width), 'cp', split...  47 us
    all_to_all x1, starting transfers between devices, body(): lax.all_to_all(terms.reshape(shards, tokens, 2 * head_width), 'cp', split...  14.4 us
    all_to_all x1, starting transfers between devices, body(): lax.all_to_all(packed, 'cp', split_axis=0, concat_axis=0, tiled=True)  13 us
  transfers between devices with their start and end apart: 3, of which 3 were waited for; matrix products, arithmetic and copies ran while one was open for 1% of the time, Pallas kernels for 0%

profile of v3, /device:TPU:56, one launch (start us, length us, event | category | flops | bytes accessed | tf_op | source)
XLA Modules:
  0.0 202.3 jit_solution(7160343357519717578)
XLA Ops:
  0.6 0.0 copy-start
  0.6 1.1 select_reduce_fusion
  1.8 0.8 reshape_squeeze.14
  2.6 0.8 reshape_squeeze.15
  3.4 0.0 copy-done
  3.4 0.6 gather_fusion.1
  3.9 1.6 gather_fusion
  5.6 0.2 broadcast_select_fusion.1
  5.8 0.1 broadcast_in_dim.27
  5.9 1.6 pad_maximum_fusion
  7.5 0.0 copy-start.2
  7.5 13.0 %all-to-all-start = ((bf16[16,32,2048]{2,1,0:T(8,128)(2,1)}), bf16[16,32,2048]{2,1,0:T(8,128)(2,1)S(1)}, u32[]{:S(2)}, u32[]{:S(2)}) async-start(bf16[16,32,2048]{2,1,0:T(8,128)(2,1)} %pad_maximum_fusion), calls=%async_computation | async-start | bytes 4194304 | tf_op jit(solution)/shard_map/all_to_all | solution.py:167
  20.5 0.0 copy-done.2
  20.5 0.2 reduce-window.9
  20.7 0.2 multiply_reduce_fusion
  20.9 51.7 %all-to-all-done = bf16[16,32,2048]{2,1,0:T(8,128)(2,1)S(1)} async-done(((bf16[16,32,2048]{2,1,0:T(8,128)(2,1)}), bf16[16,32,2048]{2,1,0:T(8,128)(2,1)S(1)}, u32[]{:S(2)}, u32[]{:S(2)}) %all-to-all-start) | async-done | bytes 2097184 | tf_op jit(solution)/shard_map/all_to_all | solution.py:167
  72.6 1.2 fusion
  73.7 0.0 copy-start.1
  73.7 1.3 reshape.64.v_ref
  75.1 1.3 reshape.63.k_ref
  76.4 0.2 reshape.62.g_ref
  76.6 0.0 copy-done.1
  76.6 0.2 reshape.61.q_ref
  76.9 57.5 %shard_map.85 = (bf16[2048,128]{1,0:T(8,128)(2,1)S(1)}, f32[2048,256]{1,0:T(8,128)}) custom-call(s32[6]{0:T(128)S(1)} %bitcast.14, s32[16]{0:T(128)S(1)} %multiply_add_fusion.start_ref, bf16[2048,128]{1,0:T(8,128)(2,1)S(1)} %reshape.61.q_ref, bf16[2048,128]{1,0:T(8,128)(2,1)S(1)} %reshape.62.g_ref, bf16[2048,128]{1,0:T(8,128)(2,1)S(1)} %reshape.63.k_ref, ...), custom_call_target="tpu_custom_call" | custom-call | flops 1879048192 | bytes 4718592 | tf_op jit(solution)/shard_map/pallas_call | solution.py:120
  134.3 14.4 %all-to-all-start.1 = ((f32[16,128,256]{2,1,0:T(8,128)}), f32[16,128,256]{2,1,0:T(8,128)S(1)}, u32[]{:S(2)}, u32[]{:S(2)}) async-start(f32[16,128,256]{2,1,0:T(8,128)} %bitcast.6), calls=%async_computation.1 | async-start | bytes 4194304 | tf_op jit(solution)/shard_map/all_to_all | solution.py:187
  148.7 1.0 reshape.65
  149.7 1.3 collective-permute-start
  151.0 2.7 %collective-permute-done = bf16[128,2048]{1,0:T(8,128)(2,1)S(1)} collective-permute-done((bf16[128,2048]{1,0:T(8,128)(2,1)}, bf16[128,2048]{1,0:T(8,128)(2,1)S(1)}, u32[]{:S(2)}, u32[]{:S(2)}) %collective-permute-start) | collective-permute-done | bytes 524320 | tf_op jit(solution)/shard_map/ppermute | solution.py:14
  153.7 47.0 %all-to-all-done.1 = f32[16,128,256]{2,1,0:T(8,128)S(1)} async-done(((f32[16,128,256]{2,1,0:T(8,128)}), f32[16,128,256]{2,1,0:T(8,128)S(1)}, u32[]{:S(2)}, u32[]{:S(2)}) %all-to-all-start.1) | async-done | bytes 2097184 | tf_op jit(solution)/shard_map/all_to_all | solution.py:187
  200.7 0.1 reduce_sum.19
  200.9 0.6 slice_bitcast_fusion
  201.5 0.8 copy.10
  (4 shorter events, 0.0 us)
Async XLA Ops:
  0.6 2.7 %copy-start = (bf16[1,128,2048]{2,1,0:T(8,128)(2,1)S(1)}, bf16[1,128,2048]{2,1,0:T(8,128)(2,1)}, u32[]{:S(2)}) copy-start(bf16[1,128,2048]{2,1,0:T(8,128)(2,1)} %param.11) | copy-start | bytes 1572868
  7.5 13.0 %copy-start.2 = (s32[6]{0:T(128)S(1)}, s32[6]{0:T(128)}, u32[]{:S(2)}) copy-start(s32[6]{0:T(128)} %param.12) | copy-start | bytes 76
  7.5 65.1 %all-to-all-start = ((bf16[16,32,2048]{2,1,0:T(8,128)(2,1)}), bf16[16,32,2048]{2,1,0:T(8,128)(2,1)S(1)}, u32[]{:S(2)}, u32[]{:S(2)}) async-start(bf16[16,32,2048]{2,1,0:T(8,128)(2,1)} %pad_maximum_fusion), calls=%async_computation | async-start | bytes 4194304 | tf_op jit(solution)/shard_map/all_to_all | solution.py:167
  73.7 2.9 %copy-start.1 = (bf16[16,8,2048]{2,1,0:T(8,128)(2,1)S(1)}, bf16[16,8,2048]{2,1,0:T(8,128)(2,1)}, u32[]{:S(2)}) copy-start(bf16[16,8,2048]{2,1,0:T(8,128)(2,1)} %get-tuple-element.13) | copy-start | bytes 1572868
  134.3 66.4 %all-to-all-start.1 = ((f32[16,128,256]{2,1,0:T(8,128)}), f32[16,128,256]{2,1,0:T(8,128)S(1)}, u32[]{:S(2)}, u32[]{:S(2)}) async-start(f32[16,128,256]{2,1,0:T(8,128)} %bitcast.6), calls=%async_computation.1 | async-start | bytes 4194304 | tf_op jit(solution)/shard_map/all_to_all | solution.py:187
  149.7 4.0 %collective-permute-start = (bf16[128,2048]{1,0:T(8,128)(2,1)}, bf16[128,2048]{1,0:T(8,128)(2,1)S(1)}, u32[]{:S(2)}, u32[]{:S(2)}) collective-permute-start(bf16[128,2048]{1,0:T(8,128)(2,1)} %reshape.65), channel_id=1, source_target_pairs={{128,0},{256,128},{384,256},{129,1},{257,129},{385,257},{130,2},{2... | collective-permute-start | bytes 1572872 | tf_op jit(solution)/shard_map/ppermute | solution.py:14

commit v4 on v3

--- a/solution.py
+++ b/solution.py
@@ -21,11 +21,10 @@
     return doc
 
 
-def _attend_kernel(heads, ends_ref, start_ref, q_ref, g_ref, k_ref, v_ref, dq_ref, dkv_ref, top_ref, total_ref, weighted_ref, dq_acc):
+def _attend_kernel(heads, kb_size, ends_ref, start_ref, kdoc_ref, q_ref, g_ref, k_ref, v_ref, dq_ref, dkv_ref, top_ref, total_ref, weighted_ref, dq_acc):
     rows, head_width = q_ref.shape
     keys = k_ref.shape[0]
     rb_size = rows // start_ref.shape[0]
-    kb_size = 128
     row_blocks = rows // rb_size
     key_blocks = keys // kb_size
     tokens_per_block = rb_size // heads
@@ -33,6 +32,7 @@
     dkv_ref[...] = jnp.zeros_like(dkv_ref)
     row_iota = lax.broadcasted_iota(jnp.int32, (rb_size, kb_size), 0) // heads
     col_iota = lax.broadcasted_iota(jnp.int32, (rb_size, kb_size), 1)
+    row_iota1 = lax.broadcasted_iota(jnp.int32, (rb_size, 1), 0) // heads
 
     def vector_doc(position):
         doc = jnp.zeros(position.shape, jnp.int32)
@@ -49,7 +49,7 @@
         q = q_ref[pl.ds(r0, rb_size), :]
         g = g_ref[pl.ds(r0, rb_size), :]
         row_pos = first + row_iota
-        row_doc = vector_doc(row_pos)
+        row_doc = vector_doc(first + row_iota1)
         top_ref[...] = jnp.full(top_ref.shape, -1e30, jnp.float32)
         total_ref[...] = jnp.zeros(total_ref.shape, jnp.float32)
         weighted_ref[...] = jnp.zeros(weighted_ref.shape, jnp.float32)
@@ -65,7 +65,8 @@
             v = v_ref[pl.ds(k0, kb_size), :]
             s = lax.dot_general(q, k, (((1,), (1,)), ((), ())), preferred_element_type=jnp.float32) * scale
             key_pos = k0 + col_iota
-            visible = (vector_doc(key_pos) == row_doc) & (key_pos <= row_pos)
+            key_doc = kdoc_ref[:, pl.ds(k0, kb_size)]
+            visible = (key_doc == row_doc) & (key_pos <= row_pos)
             s = jnp.where(visible, s, -jnp.inf)
             dp = lax.dot_general(g, v, (((1,), (1,)), ((), ())), preferred_element_type=jnp.float32)
             return k0, k, s, dp
@@ -87,12 +88,13 @@
         top = top_ref[...]
         total = total_ref[...]
         delta = weighted_ref[...] / total
+        inverse_total = 1.0 / total
 
         def second_pass(kb, c):
             @pl.when(seen(kb))
             def _():
                 k0, k, s, dp = scores_of(kb)
-                probs = jnp.exp(s - top) / total
+                probs = jnp.exp(s - top) * inverse_total
                 probs_low = probs.astype(jnp.bfloat16)
                 dscore = (probs * (dp - delta) * scale).astype(jnp.bfloat16)
                 dv = lax.dot_general(probs_low, g, (((0,), (0,)), ((), ())), preferred_element_type=jnp.float32)
@@ -109,7 +111,7 @@
     lax.fori_loop(0, row_blocks, row_block, 0)
 
 
-def attend_kernel(flat_query, flat_grad, key_full, value_full, ends, block_start, heads):
+def attend_kernel(flat_query, flat_grad, key_full, value_full, ends, block_start, heads, kb_size=512):
     rows, head_width = flat_query.shape
     keys = key_full.shape[0]
     rb_size = rows // block_start.shape[0]
@@ -117,13 +119,15 @@
     smem = pl.BlockSpec(memory_space=pltpu.SMEM)
     whole = pl.BlockSpec(memory_space=pltpu.VMEM)
     flops = 2 * rows * keys * head_width * 7
+    positions = jnp.arange(keys, dtype=jnp.int32)
+    key_doc = jnp.sum((positions[:, None] >= ends[None, :]).astype(jnp.int32), axis=1)[None, :]
     return pl.pallas_call(
-        functools.partial(_attend_kernel, heads),
+        functools.partial(_attend_kernel, heads, kb_size),
         out_shape=(
             jax.ShapeDtypeStruct((rows, head_width), jnp.bfloat16),
             jax.ShapeDtypeStruct((keys, 2 * head_width), jnp.float32),
         ),
-        in_specs=[smem, smem, whole, whole, whole, whole],
+        in_specs=[smem, smem, whole, whole, whole, whole, whole],
         out_specs=(whole, whole),
         scratch_shapes=[
             vmem((rb_size, 1), jnp.float32),
@@ -133,7 +137,7 @@
         ],
         compiler_params=pltpu.CompilerParams(vmem_limit_bytes=48 * 1024 * 1024),
         cost_estimate=pl.CostEstimate(flops=flops // 4, transcendentals=rows * keys // 2, bytes_accessed=rows * head_width * 6 + keys * head_width * 4 + keys * head_width * 8),
-    )(ends, block_start, flat_query, flat_grad, key_full, value_full)
+    )(ends, block_start, key_doc, flat_query, flat_grad, key_full, value_full)
 
 
 def body(query, key, value, out_grad, lengths, plan):

time: 203 us -> 162 us (0.80)
  Pallas kernels: 57.5 us -> 27.6 us
  starting transfers between devices: 28.7 us -> 18 us
    pallas_call x1, Pallas kernels: 57.5 us -> 27.6 us  [attend_kernel(): pl.pallas_call(functools.partial(_attend_kernel, heads, kb_size), out_sha...]
    all_to_all x1, starting transfers between devices: 14.4 us -> 3.72 us  [body(): lax.all_to_all(terms.reshape(shards, tokens, 2 * head_width), 'cp', split...]
where the time goes in v4:
time: 162 us
  waiting for transfers between devices  101 us (62%)
  Pallas kernels  27.6 us (17%)
  starting transfers between devices  18 us (11%)
  local copies, waits for them, and re-layouts  10.6 us (7%)
  other arithmetic  3.47 us (2%)
    all_to_all x1, waiting for transfers between devices, body(): lax.all_to_all(packed, 'cp', split_axis=0, concat_axis=0, tiled=True)  51.6 us
    all_to_all x1, waiting for transfers between devices, body(): lax.all_to_all(terms.reshape(shards, tokens, 2 * head_width), 'cp', split...  46.9 us
    pallas_call x1, Pallas kernels, attend_kernel(): pl.pallas_call(functools.partial(_attend_kernel, heads, kb_size), out_sha...  27.6 us
    all_to_all x1, starting transfers between devices, body(): lax.all_to_all(packed, 'cp', split_axis=0, concat_axis=0, tiled=True)  13 us
    all_to_all x1, starting transfers between devices, body(): lax.all_to_all(terms.reshape(shards, tokens, 2 * head_width), 'cp', split...  3.72 us
  transfers between devices with their start and end apart: 3, of which 3 were waited for; matrix products, arithmetic and copies ran while one was open for 1% of the time, Pallas kernels for 0%

profile of v4, /device:TPU:56, one launch (start us, length us, event | category | flops | bytes accessed | tf_op | source)
XLA Modules:
  0.0 161.7 jit_solution(816241524973034998)
XLA Ops:
  0.6 0.0 copy-start
  0.6 1.1 select_reduce_fusion
  1.8 0.8 reshape_squeeze.14
  2.6 0.8 reshape_squeeze.15
  3.4 0.0 copy-done
  3.4 0.6 gather_fusion.1
  3.9 1.6 %gather_fusion = bf16[16,8,2048]{2,1,0:T(8,128)(2,1)S(1)} fusion(bf16[16,8,2048]{2,1,0:T(8,128)(2,1)} %bitcast.19, s32[1024]{0:T(1024)S(1)} %pad_clamp_fusion), kind=kCustom, calls=%fused_computation.clone | custom fusion | bytes 1048640 | tf_op jit(solution)/shard_map/jit(_take)/gather | solution.py:159
  5.6 0.2 broadcast_select_fusion.1
  5.8 0.1 broadcast_in_dim.33
  5.9 1.6 pad_maximum_fusion
  7.5 0.0 copy-start.2
  7.5 13.0 %all-to-all-start = ((bf16[16,32,2048]{2,1,0:T(8,128)(2,1)}), bf16[16,32,2048]{2,1,0:T(8,128)(2,1)S(1)}, u32[]{:S(2)}, u32[]{:S(2)}) async-start(bf16[16,32,2048]{2,1,0:T(8,128)(2,1)} %pad_maximum_fusion), calls=%async_computation | async-start | bytes 4194304 | tf_op jit(solution)/shard_map/all_to_all | solution.py:171
  20.5 0.0 copy-done.2
  20.5 0.2 reduce-window.8
  20.7 0.2 multiply_reduce_fusion
  20.9 0.1 convert_reduce_fusion
  21.0 51.6 %all-to-all-done = bf16[16,32,2048]{2,1,0:T(8,128)(2,1)S(1)} async-done(((bf16[16,32,2048]{2,1,0:T(8,128)(2,1)}), bf16[16,32,2048]{2,1,0:T(8,128)(2,1)S(1)}, u32[]{:S(2)}, u32[]{:S(2)}) %all-to-all-start) | async-done | bytes 2097184 | tf_op jit(solution)/shard_map/all_to_all | solution.py:171
  72.6 1.2 fusion
  73.8 0.0 copy-start.1
  73.8 1.3 reshape.61.v_ref
  75.1 1.3 reshape.60.k_ref
  76.4 0.2 reshape.59.g_ref
  76.6 0.0 copy-done.1
  76.6 0.2 reshape.58.q_ref
  76.9 27.6 %shard_map.85 = (bf16[2048,128]{1,0:T(8,128)(2,1)S(1)}, f32[2048,256]{1,0:T(8,128)}) custom-call(s32[6]{0:T(128)S(1)} %bitcast.17, s32[16]{0:T(128)S(1)} %multiply_add_fusion.start_ref, s32[1,2048]{1,0:T(1,128)S(1)} %bitcast.15, bf16[2048,128]{1,0:T(8,128)(2,1)S(1)} %reshape.58.q_ref, bf16[2048,128]{1,0:T(8,128)(2,1)S(1)} %reshape.59.g_ref, ...), custom_call_target="tpu_custom_call" | custom-call | flops 1879048192 | bytes 4718592 | tf_op jit(solution)/shard_map/pallas_call | solution.py:124
  104.5 3.7 %all-to-all-start.1 = ((f32[16,128,256]{2,1,0:T(8,128)}), f32[16,128,256]{2,1,0:T(8,128)S(1)}, u32[]{:S(2)}, u32[]{:S(2)}) async-start(f32[16,128,256]{2,1,0:T(8,128)} %bitcast.7), calls=%async_computation.1 | async-start | bytes 4194304 | tf_op jit(solution)/shard_map/all_to_all | solution.py:191
  108.2 1.0 reshape.62
  109.2 1.3 collective-permute-start
  110.5 2.7 %collective-permute-done = bf16[128,2048]{1,0:T(8,128)(2,1)S(1)} collective-permute-done((bf16[128,2048]{1,0:T(8,128)(2,1)}, bf16[128,2048]{1,0:T(8,128)(2,1)S(1)}, u32[]{:S(2)}, u32[]{:S(2)}) %collective-permute-start) | collective-permute-done | bytes 524320 | tf_op jit(solution)/shard_map/ppermute | solution.py:14
  113.2 46.9 %all-to-all-done.1 = f32[16,128,256]{2,1,0:T(8,128)S(1)} async-done(((f32[16,128,256]{2,1,0:T(8,128)}), f32[16,128,256]{2,1,0:T(8,128)S(1)}, u32[]{:S(2)}, u32[]{:S(2)}) %all-to-all-start.1) | async-done | bytes 2097184 | tf_op jit(solution)/shard_map/all_to_all | solution.py:191
  160.1 0.1 reduce_sum.29
  160.3 0.6 slice_bitcast_fusion
  160.9 0.8 copy.10
  (4 shorter events, 0.0 us)
Async XLA Ops:
  0.6 2.7 %copy-start = (bf16[1,128,2048]{2,1,0:T(8,128)(2,1)S(1)}, bf16[1,128,2048]{2,1,0:T(8,128)(2,1)}, u32[]{:S(2)}) copy-start(bf16[1,128,2048]{2,1,0:T(8,128)(2,1)} %param.11) | copy-start | bytes 1572868
  7.5 13.0 %copy-start.2 = (s32[6]{0:T(128)S(1)}, s32[6]{0:T(128)}, u32[]{:S(2)}) copy-start(s32[6]{0:T(128)} %param.12) | copy-start | bytes 76
  7.5 65.1 %all-to-all-start = ((bf16[16,32,2048]{2,1,0:T(8,128)(2,1)}), bf16[16,32,2048]{2,1,0:T(8,128)(2,1)S(1)}, u32[]{:S(2)}, u32[]{:S(2)}) async-start(bf16[16,32,2048]{2,1,0:T(8,128)(2,1)} %pad_maximum_fusion), calls=%async_computation | async-start | bytes 4194304 | tf_op jit(solution)/shard_map/all_to_all | solution.py:171
  73.8 2.9 %copy-start.1 = (bf16[16,8,2048]{2,1,0:T(8,128)(2,1)S(1)}, bf16[16,8,2048]{2,1,0:T(8,128)(2,1)}, u32[]{:S(2)}) copy-start(bf16[16,8,2048]{2,1,0:T(8,128)(2,1)} %get-tuple-element.13) | copy-start | bytes 1572868
  104.5 55.7 %all-to-all-start.1 = ((f32[16,128,256]{2,1,0:T(8,128)}), f32[16,128,256]{2,1,0:T(8,128)S(1)}, u32[]{:S(2)}, u32[]{:S(2)}) async-start(f32[16,128,256]{2,1,0:T(8,128)} %bitcast.7), calls=%async_computation.1 | async-start | bytes 4194304 | tf_op jit(solution)/shard_map/all_to_all | solution.py:191
  109.2 4.0 %collective-permute-start = (bf16[128,2048]{1,0:T(8,128)(2,1)}, bf16[128,2048]{1,0:T(8,128)(2,1)S(1)}, u32[]{:S(2)}, u32[]{:S(2)}) collective-permute-start(bf16[128,2048]{1,0:T(8,128)(2,1)} %reshape.62), channel_id=1, source_target_pairs={{128,0},{256,128},{384,256},{129,1},{257,129},{385,257},{130,2},{2... | collective-permute-start | bytes 1572872 | tf_op jit(solution)/shard_map/ppermute | solution.py:14

commit v5 on v4

--- a/solution.py
+++ b/solution.py
@@ -189,9 +189,9 @@
     dquery = dquery.reshape(tokens, width)
     handed = passed_along(dquery, "pp", -1)
     partials = lax.all_to_all(
-        terms.reshape(shards, tokens, 2 * head_width), "cp", split_axis=0, concat_axis=0, tiled=True
-    )
-    summed = jnp.sum(partials, axis=0)
+        terms.astype(jnp.bfloat16).reshape(shards, tokens, 2 * head_width), "cp", split_axis=0, concat_axis=0, tiled=True
+    )
+    summed = jnp.sum(partials.astype(jnp.float32), axis=0)
     key_grad = summed[:, :head_width].astype(jnp.bfloat16)
     value_grad = summed[:, head_width:].astype(jnp.bfloat16)
     return (handed[None], key_grad[None], value_grad[None])

time: 162 us -> 140 us (0.86)
  waiting for transfers between devices: 101 us -> 80.1 us
    all_to_all x1, waiting for transfers between devices: 46.9 us -> 26.1 us  [body(): lax.all_to_all(terms.astype(jnp.bfloat16).reshape(shards, tokens, 2 * hea...]
  transfers between devices with their start and end apart: 3 -> 3, of which waited for: 3 -> 3; matrix products, arithmetic and copies ran while one was open for 1% -> 0% of each run, Pallas kernels for 0% -> 0%
where the time goes in v5:
time: 140 us
  waiting for transfers between devices  80.1 us (57%)
  Pallas kernels  26.2 us (19%)
  starting transfers between devices  18 us (13%)
  local copies, waits for them, and re-layouts  9.85 us (7%)
  other arithmetic  4.59 us (3%)
    all_to_all x1, waiting for transfers between devices, body(): lax.all_to_all(packed, 'cp', split_axis=0, concat_axis=0, tiled=True)  51.6 us
    pallas_call x1, Pallas kernels, attend_kernel(): pl.pallas_call(functools.partial(_attend_kernel, heads, kb_size), out_sha...  26.2 us
    all_to_all x1, waiting for transfers between devices, body(): lax.all_to_all(terms.astype(jnp.bfloat16).reshape(shards, tokens, 2 * hea...  26.1 us
    all_to_all x1, starting transfers between devices, body(): lax.all_to_all(packed, 'cp', split_axis=0, concat_axis=0, tiled=True)  13 us
    all_to_all x1, starting transfers between devices, body(): lax.all_to_all(terms.astype(jnp.bfloat16).reshape(shards, tokens, 2 * hea...  3.65 us
  transfers between devices with their start and end apart: 3, of which 3 were waited for; matrix products, arithmetic and copies ran while one was open for 0% of the time, Pallas kernels for 0%

profile of v5, /device:TPU:56, one launch (start us, length us, event | category | flops | bytes accessed | tf_op | source)
XLA Modules:
  0.0 139.6 jit_solution(18157921893737431447)
XLA Ops:
  0.6 0.0 copy-start
  0.6 1.1 select_reduce_fusion
  1.8 0.8 reshape_squeeze.14
  2.6 0.8 reshape_squeeze.15
  3.4 0.0 copy-done
  3.4 0.6 gather_fusion.1
  3.9 1.6 %gather_fusion = bf16[16,8,2048]{2,1,0:T(8,128)(2,1)S(1)} fusion(bf16[16,8,2048]{2,1,0:T(8,128)(2,1)} %bitcast.19, s32[1024]{0:T(1024)S(1)} %pad_clamp_fusion), kind=kCustom, calls=%fused_computation.clone | custom fusion | bytes 1048640 | tf_op jit(solution)/shard_map/jit(_take)/gather | solution.py:159
  5.6 0.2 broadcast_select_fusion.1
  5.8 0.1 broadcast_in_dim.33
  5.9 1.6 %pad_maximum_fusion = bf16[16,32,2048]{2,1,0:T(8,128)(2,1)} fusion(bf16[16,16,2048]{2,1,0:T(8,128)(2,1)S(1)} %broadcast_in_dim.33, bf16[16,8,2048]{2,1,0:T(8,128)(2,1)S(1)} %get-tuple-element.17, bf16[16,8,2048]{2,1,0:T(8,128)(2,1)S(1)} %get-tuple-element.16), kind=kLoop, calls=%fused_computation.2 | loop fusion | flops 6291456 | bytes 4194304 | tf_op jit(solution)/shard_map/concatenate | solution.py:163
  7.5 0.0 copy-start.2
  7.5 13.0 %all-to-all-start = ((bf16[16,32,2048]{2,1,0:T(8,128)(2,1)}), bf16[16,32,2048]{2,1,0:T(8,128)(2,1)S(1)}, u32[]{:S(2)}, u32[]{:S(2)}) async-start(bf16[16,32,2048]{2,1,0:T(8,128)(2,1)} %pad_maximum_fusion), calls=%async_computation | async-start | bytes 4194304 | tf_op jit(solution)/shard_map/all_to_all | solution.py:171
  20.5 0.0 copy-done.2
  20.5 0.2 reduce-window.8
  20.7 0.2 multiply_reduce_fusion
  20.9 0.1 convert_reduce_fusion
  21.0 51.6 %all-to-all-done = bf16[16,32,2048]{2,1,0:T(8,128)(2,1)S(1)} async-done(((bf16[16,32,2048]{2,1,0:T(8,128)(2,1)}), bf16[16,32,2048]{2,1,0:T(8,128)(2,1)S(1)}, u32[]{:S(2)}, u32[]{:S(2)}) %all-to-all-start) | async-done | bytes 2097184 | tf_op jit(solution)/shard_map/all_to_all | solution.py:171
  72.6 1.2 fusion
  73.8 0.0 copy-start.1
  73.8 1.3 reshape.61.v_ref
  75.1 1.3 reshape.60.k_ref
  76.4 0.2 reshape.59.g_ref
  76.7 0.0 copy-done.1
  76.7 0.2 reshape.58.q_ref
  76.9 26.2 %shard_map.85 = (bf16[2048,128]{1,0:T(8,128)(2,1)S(1)}, f32[2048,256]{1,0:T(8,128)S(1)}) custom-call(s32[6]{0:T(128)S(1)} %bitcast.17, s32[16]{0:T(128)S(1)} %multiply_add_fusion.start_ref, s32[1,2048]{1,0:T(1,128)S(1)} %bitcast.15, bf16[2048,128]{1,0:T(8,128)(2,1)S(1)} %reshape.58.q_ref, bf16[2048,128]{1,0:T(8,128)(2,1)S(1)} %reshape.59.g_ref, ...), custom_call_target="tpu_custom_call" | custom-call | flops 1879048192 | bytes 4718592 | tf_op jit(solution)/shard_map/pallas_call | solution.py:124
  103.2 1.1 convert_element_type.13
  104.3 3.7 %all-to-all-start.1 = ((bf16[16,128,256]{2,1,0:T(8,128)(2,1)}), bf16[16,128,256]{2,1,0:T(8,128)(2,1)S(1)}, u32[]{:S(2)}, u32[]{:S(2)}) async-start(bf16[16,128,256]{2,1,0:T(8,128)(2,1)} %bitcast.7), calls=%async_computation.1 | async-start | bytes 2097152 | tf_op jit(solution)/shard_map/all_to_all | solution.py:191
  107.9 0.2 reshape.62
  108.1 1.3 collective-permute-start
  109.4 2.5 %collective-permute-done = bf16[128,2048]{1,0:T(8,128)(2,1)S(1)} collective-permute-done((bf16[128,2048]{1,0:T(8,128)(2,1)S(1)}, bf16[128,2048]{1,0:T(8,128)(2,1)S(1)}, u32[]{:S(2)}, u32[]{:S(2)}) %collective-permute-start) | collective-permute-done | bytes 524320 | tf_op jit(solution)/shard_map/ppermute | solution.py:14
  112.0 26.1 %all-to-all-done.1 = bf16[16,128,256]{2,1,0:T(8,128)(2,1)S(1)} async-done(((bf16[16,128,256]{2,1,0:T(8,128)(2,1)}), bf16[16,128,256]{2,1,0:T(8,128)(2,1)S(1)}, u32[]{:S(2)}, u32[]{:S(2)}) %all-to-all-start.1) | async-done | bytes 1048608 | tf_op jit(solution)/shard_map/all_to_all | solution.py:191
  138.0 0.1 reduce
  138.2 0.6 slice_bitcast_fusion
  138.8 0.8 copy.10
  (4 shorter events, 0.0 us)
Async XLA Ops:
  0.6 2.7 %copy-start = (bf16[1,128,2048]{2,1,0:T(8,128)(2,1)S(1)}, bf16[1,128,2048]{2,1,0:T(8,128)(2,1)}, u32[]{:S(2)}) copy-start(bf16[1,128,2048]{2,1,0:T(8,128)(2,1)} %param.11) | copy-start | bytes 1572868
  7.5 13.0 %copy-start.2 = (s32[6]{0:T(128)S(1)}, s32[6]{0:T(128)}, u32[]{:S(2)}) copy-start(s32[6]{0:T(128)} %param.12) | copy-start | bytes 76
  7.5 65.1 %all-to-all-start = ((bf16[16,32,2048]{2,1,0:T(8,128)(2,1)}), bf16[16,32,2048]{2,1,0:T(8,128)(2,1)S(1)}, u32[]{:S(2)}, u32[]{:S(2)}) async-start(bf16[16,32,2048]{2,1,0:T(8,128)(2,1)} %pad_maximum_fusion), calls=%async_computation | async-start | bytes 4194304 | tf_op jit(solution)/shard_map/all_to_all | solution.py:171
  73.8 2.9 %copy-start.1 = (bf16[16,8,2048]{2,1,0:T(8,128)(2,1)S(1)}, bf16[16,8,2048]{2,1,0:T(8,128)(2,1)}, u32[]{:S(2)}) copy-start(bf16[16,8,2048]{2,1,0:T(8,128)(2,1)} %get-tuple-element.13) | copy-start | bytes 1572868
  104.3 33.8 %all-to-all-start.1 = ((bf16[16,128,256]{2,1,0:T(8,128)(2,1)}), bf16[16,128,256]{2,1,0:T(8,128)(2,1)S(1)}, u32[]{:S(2)}, u32[]{:S(2)}) async-start(bf16[16,128,256]{2,1,0:T(8,128)(2,1)} %bitcast.7), calls=%async_computation.1 | async-start | bytes 2097152 | tf_op jit(solution)/shard_map/all_to_all | solution.py:191
  108.1 3.8 %collective-permute-start = (bf16[128,2048]{1,0:T(8,128)(2,1)S(1)}, bf16[128,2048]{1,0:T(8,128)(2,1)S(1)}, u32[]{:S(2)}, u32[]{:S(2)}) collective-permute-start(bf16[128,2048]{1,0:T(8,128)(2,1)S(1)} %reshape.62), channel_id=1, source_target_pairs={{128,0},{256,128},{384,256},{129,1},{257,129},{385,257},{130,2},{2... | collective-permute-start | bytes 1572872 | tf_op jit(solution)/shard_map/ppermute | solution.py:14

commit v6 on v5

--- a/solution.py
+++ b/solution.py
@@ -21,9 +21,9 @@
     return doc
 
 
-def _attend_kernel(heads, kb_size, ends_ref, start_ref, kdoc_ref, q_ref, g_ref, k_ref, v_ref, dq_ref, dkv_ref, top_ref, total_ref, weighted_ref, dq_acc):
+def _attend_kernel(heads, kb_size, ends_ref, start_ref, kdoc_ref, q_ref, g_ref, kv_ref, dq_ref, dkv_ref, top_ref, total_ref, weighted_ref, dq_acc):
     rows, head_width = q_ref.shape
-    keys = k_ref.shape[0]
+    keys = kv_ref.shape[0]
     rb_size = rows // start_ref.shape[0]
     row_blocks = rows // rb_size
     key_blocks = keys // kb_size
@@ -61,8 +61,8 @@
 
         def scores_of(kb):
             k0 = pl.multiple_of(kb * kb_size, kb_size)
-            k = k_ref[pl.ds(k0, kb_size), :]
-            v = v_ref[pl.ds(k0, kb_size), :]
+            k = kv_ref[pl.ds(k0, kb_size), pl.ds(0, head_width)]
+            v = kv_ref[pl.ds(k0, kb_size), pl.ds(head_width, head_width)]
             s = lax.dot_general(q, k, (((1,), (1,)), ((), ())), preferred_element_type=jnp.float32) * scale
             key_pos = k0 + col_iota
             key_doc = kdoc_ref[:, pl.ds(k0, kb_size)]
@@ -111,9 +111,9 @@
     lax.fori_loop(0, row_blocks, row_block, 0)
 
 
-def attend_kernel(flat_query, flat_grad, key_full, value_full, ends, block_start, heads, kb_size=512):
+def attend_kernel(flat_query, flat_grad, keys_all, ends, block_start, heads, kb_size=512):
     rows, head_width = flat_query.shape
-    keys = key_full.shape[0]
+    keys = keys_all.shape[0]
     rb_size = rows // block_start.shape[0]
     vmem = pltpu.VMEM
     smem = pl.BlockSpec(memory_space=pltpu.SMEM)
@@ -127,7 +127,7 @@
             jax.ShapeDtypeStruct((rows, head_width), jnp.bfloat16),
             jax.ShapeDtypeStruct((keys, 2 * head_width), jnp.float32),
         ),
-        in_specs=[smem, smem, whole, whole, whole, whole, whole],
+        in_specs=[smem, smem, whole, whole, whole, whole],
         out_specs=(whole, whole),
         scratch_shapes=[
             vmem((rb_size, 1), jnp.float32),
@@ -137,7 +137,7 @@
         ],
         compiler_params=pltpu.CompilerParams(vmem_limit_bytes=48 * 1024 * 1024),
         cost_estimate=pl.CostEstimate(flops=flops // 4, transcendentals=rows * keys // 2, bytes_accessed=rows * head_width * 6 + keys * head_width * 4 + keys * head_width * 8),
-    )(ends, block_start, key_doc, flat_query, flat_grad, key_full, value_full)
+    )(ends, block_start, key_doc, flat_query, flat_grad, keys_all)
 
 
 def body(query, key, value, out_grad, lengths, plan):
@@ -158,30 +158,26 @@
         grouped = rows.reshape(shards, block_rows, rows.shape[1])
         return jnp.take(grouped, send_order, axis=0)
 
-    key_rows = tokens * head_width // width
-    own_keys = jnp.concatenate([key[0].reshape(key_rows, width), value[0].reshape(key_rows, width)], axis=0)
-    packed = jnp.concatenate(
-        [
-            reorder(query[0]),
-            reorder(out_grad[0]),
-            jnp.broadcast_to(own_keys[None], (shards,) + own_keys.shape),
-        ],
-        axis=1,
-    )
-    received = lax.all_to_all(packed, "cp", split_axis=0, concat_axis=0, tiled=True)
+    rows_sent = jnp.concatenate([reorder(query[0]), reorder(out_grad[0])], axis=1)
+    received = lax.all_to_all(rows_sent, "cp", split_axis=0, concat_axis=0, tiled=True)
     query_sent = received[:, :block_rows]
-    grad_sent = received[:, block_rows : 2 * block_rows]
-    key_at = 2 * block_rows
-    key_full = received[:, key_at : key_at + key_rows].reshape(key_count, head_width)
-    value_full = received[:, key_at + key_rows :].reshape(key_count, head_width)
+    grad_sent = received[:, block_rows:]
+    held = jnp.concatenate([key[0], value[0]], axis=1)[None]
+    step = 1
+    while step < shards:
+        pairs = [(i, i ^ step) for i in range(shards)]
+        other = lax.ppermute(held, "cp", pairs)
+        upper = (own_index & step) != 0
+        held = jnp.where(upper, jnp.concatenate([other, held], 0), jnp.concatenate([held, other], 0))
+        step *= 2
+    keys_all = held.reshape(key_count, 2 * head_width)
     ends = jnp.cumsum(lengths).astype(jnp.int32)
     taken = lax.dynamic_index_in_dim(inverse, own_index, 1, keepdims=False)
     head_count = width // head_width
     dquery, terms = attend_kernel(
         query_sent.reshape(tokens * head_count, head_width),
         grad_sent.reshape(tokens * head_count, head_width),
-        key_full,
-        value_full,
+        keys_all,
         ends,
         iota * tokens + taken * block_rows,
         head_count,

time: 140 us -> 166 us (1.19)
  starting transfers between devices: 18 us -> 40.7 us
  Pallas kernels: 26.2 us -> 30.2 us
  local copies, waits for them, and re-layouts: 9.85 us -> 6.27 us
  waiting for transfers between devices: 80.1 us -> 82.3 us
    ppermute x0 -> x4, waiting for transfers between devices: none -> 53.5 us  [body(): other = lax.ppermute(held, 'cp', pairs)]
    all_to_all x1, waiting for transfers between devices: 51.6 us -> 0.01 us  [body(): lax.all_to_all(rows_sent, 'cp', split_axis=0, concat_axis=0, tiled=True)]
    ppermute x0 -> x4, starting transfers between devices: none -> 20.1 us  [body(): other = lax.ppermute(held, 'cp', pairs)]
    pallas_call x1, Pallas kernels: 26.2 us -> 30.2 us  [attend_kernel(): pl.pallas_call(functools.partial(_attend_kernel, heads, kb_size), out_sha...]
    reshape x2 -> x0, local copies, waits for them, and re-layouts: 2.62 us -> none  [the longest x1 1.34 us: body(): value_full = received[:, key_at + key_rows:].reshape(key_count, head_width)]
    all_to_all x1, starting transfers between devices: 3.65 us -> 6.26 us  [body(): lax.all_to_all(terms.astype(jnp.bfloat16).reshape(shards, tokens, 2 * hea...]
  transfers between devices with their start and end apart: 3 -> 7, of which waited for: 3 -> 6; matrix products, arithmetic and copies ran while one was open for 0% -> 1% of each run, Pallas kernels for 0% -> 0%
where the time goes in v6:
time: 166 us
  waiting for transfers between devices  82.3 us (50%)
  starting transfers between devices  40.7 us (25%)
  Pallas kernels  30.2 us (18%)
  local copies, waits for them, and re-layouts  6.27 us (4%)
  other arithmetic  5.49 us (3%)
    ppermute x4, waiting for transfers between devices, body(): other = lax.ppermute(held, 'cp', pairs)  53.5 us
    pallas_call x1, Pallas kernels, attend_kernel(): pl.pallas_call(functools.partial(_attend_kernel, heads, kb_size), out_sha...  30.2 us
    all_to_all x1, waiting for transfers between devices, body(): lax.all_to_all(terms.astype(jnp.bfloat16).reshape(shards, tokens, 2 * hea...  26.4 us
    ppermute x4, starting transfers between devices, body(): other = lax.ppermute(held, 'cp', pairs)  20.1 us
    all_to_all x1, starting transfers between devices, body(): lax.all_to_all(rows_sent, 'cp', split_axis=0, concat_axis=0, tiled=True)  13 us
    all_to_all x1, starting transfers between devices, body(): lax.all_to_all(terms.astype(jnp.bfloat16).reshape(shards, tokens, 2 * hea...  6.26 us
  transfers between devices with their start and end apart: 7, of which 6 were waited for; matrix products, arithmetic and copies ran while one was open for 1% of the time, Pallas kernels for 0%

profile of v6, /device:TPU:56, one launch (start us, length us, event | category | flops | bytes accessed | tf_op | source)
XLA Modules:
  0.0 165.8 jit_solution(2641179201834346164)
XLA Ops:
  0.6 0.0 copy-start
  0.7 1.1 select_reduce_fusion
  1.8 0.0 copy-done
  1.8 0.6 gather_fusion.1
  2.4 1.6 gather_fusion
  4.0 0.2 broadcast_select_fusion.1
  4.2 0.0 copy-start.1
  4.2 0.0 copy-start.2
  4.2 1.0 pad_maximum_fusion
  5.2 0.0 copy-start.3
  5.2 13.0 %all-to-all-start = ((bf16[16,16,2048]{2,1,0:T(8,128)(2,1)}), bf16[16,16,2048]{2,1,0:T(8,128)(2,1)S(1)}, u32[]{:S(2)}, u32[]{:S(2)}) async-start(bf16[16,16,2048]{2,1,0:T(8,128)(2,1)} %pad_maximum_fusion), calls=%async_computation | async-start | bytes 2097152 | tf_op jit(solution)/shard_map/all_to_all | solution.py:162
  18.3 0.0 copy-done.1
  18.3 0.0 copy-done.2
  18.3 5.3 %collective-permute-start = (bf16[1,128,256]{2,1,0:T(8,128)(2,1)S(1)}, bf16[1,128,256]{2,1,0:T(8,128)(2,1)S(1)}, u32[]{:S(2)}, u32[]{:S(2)}) collective-permute-start(bf16[1,128,256]{2,1,0:T(8,128)(2,1)S(1)} %maximum_bitcast_fusion), channel_id=1, source_target_pairs={{0,8},{8,0},{16,24},{24,16},{32,40},{40,32},{48,56},{56,48},{64,72... | collective-permute-start | bytes 196616 | tf_op jit(solution)/shard_map/ppermute | solution.py:169
  23.6 2.3 %collective-permute-done = bf16[1,128,256]{2,1,0:T(8,128)(2,1)S(1)} collective-permute-done((bf16[1,128,256]{2,1,0:T(8,128)(2,1)S(1)}, bf16[1,128,256]{2,1,0:T(8,128)(2,1)S(1)}, u32[]{:S(2)}, u32[]{:S(2)}) %collective-permute-start) | collective-permute-done | bytes 65568 | tf_op jit(solution)/shard_map/ppermute | solution.py:169
  26.0 3.9 %collective-permute-start.1 = (bf16[2,128,256]{2,1,0:T(8,128)(2,1)S(1)}, bf16[2,128,256]{2,1,0:T(8,128)(2,1)S(1)}, u32[]{:S(2)}, u32[]{:S(2)}) collective-permute-start(bf16[2,128,256]{2,1,0:T(8,128)(2,1)S(1)} %maximum_select_fusion.3), channel_id=1, source_target_pairs={{0,16},{8,24},{16,0},{24,8},{32,48},{40,56},{48,32},{56,40},{64,80... | collective-permute-start | bytes 393224 | tf_op jit(solution)/shard_map/ppermute | solution.py:169
  29.9 15.9 %collective-permute-done.1 = bf16[2,128,256]{2,1,0:T(8,128)(2,1)S(1)} collective-permute-done((bf16[2,128,256]{2,1,0:T(8,128)(2,1)S(1)}, bf16[2,128,256]{2,1,0:T(8,128)(2,1)S(1)}, u32[]{:S(2)}, u32[]{:S(2)}) %collective-permute-start.1) | collective-permute-done | bytes 131104 | tf_op jit(solution)/shard_map/ppermute | solution.py:169
  45.9 4.4 %collective-permute-start.2 = (bf16[4,128,256]{2,1,0:T(8,128)(2,1)S(1)}, bf16[4,128,256]{2,1,0:T(8,128)(2,1)S(1)}, u32[]{:S(2)}, u32[]{:S(2)}) collective-permute-start(bf16[4,128,256]{2,1,0:T(8,128)(2,1)S(1)} %maximum_select_fusion.2), channel_id=1, source_target_pairs={{0,32},{8,40},{16,48},{24,56},{32,0},{40,8},{48,16},{56,24},{64,96... | collective-permute-start | bytes 786440 | tf_op jit(solution)/shard_map/ppermute | solution.py:169
  50.3 11.3 %collective-permute-done.2 = bf16[4,128,256]{2,1,0:T(8,128)(2,1)S(1)} collective-permute-done((bf16[4,128,256]{2,1,0:T(8,128)(2,1)S(1)}, bf16[4,128,256]{2,1,0:T(8,128)(2,1)S(1)}, u32[]{:S(2)}, u32[]{:S(2)}) %collective-permute-start.2) | collective-permute-done | bytes 262176 | tf_op jit(solution)/shard_map/ppermute | solution.py:169
  61.6 0.1 maximum_select_fusion.1
  61.6 6.5 %collective-permute-start.3 = (bf16[8,128,256]{2,1,0:T(8,128)(2,1)S(1)}, bf16[8,128,256]{2,1,0:T(8,128)(2,1)}, u32[]{:S(2)}, u32[]{:S(2)}) collective-permute-start(bf16[8,128,256]{2,1,0:T(8,128)(2,1)S(1)} %maximum_select_fusion.1), channel_id=1, source_target_pairs={{0,64},{8,72},{16,80},{24,88},{32,96},{40,104},{48,112},{56,120},{... | collective-permute-start | bytes 1572872 | tf_op jit(solution)/shard_map/ppermute | solution.py:169
  68.2 0.0 copy-done.3
  68.2 0.2 reduce-window.8
  68.4 0.2 multiply_reduce_fusion
  68.6 0.1 convert_reduce_fusion
  68.7 23.9 %collective-permute-done.3 = bf16[8,128,256]{2,1,0:T(8,128)(2,1)} collective-permute-done((bf16[8,128,256]{2,1,0:T(8,128)(2,1)S(1)}, bf16[8,128,256]{2,1,0:T(8,128)(2,1)}, u32[]{:S(2)}, u32[]{:S(2)}) %collective-permute-start.3) | collective-permute-done | bytes 524320 | tf_op jit(solution)/shard_map/ppermute | solution.py:169
  92.6 1.4 maximum_select_fusion
  94.0 0.0 all-to-all-done
  94.0 0.9 fusion
  94.8 1.3 reshape.57.g_ref
  96.1 0.2 reshape.56.q_ref
  96.4 30.2 %shard_map.85 = (bf16[2048,128]{1,0:T(8,128)(2,1)S(1)}, f32[2048,256]{1,0:T(8,128)S(1)}) custom-call(s32[6]{0:T(128)S(1)} %bitcast.23, s32[16]{0:T(128)S(1)} %multiply_add_fusion.start_ref, s32[1,2048]{1,0:T(1,128)S(1)} %bitcast.21, bf16[2048,128]{1,0:T(8,128)(2,1)S(1)} %reshape.56.q_ref, bf16[2048,128]{1,0:T(8,128)(2,1)S(1)} %reshape.57.g_ref, ...), custom_call_target="tpu_custom_call" | custom-call | flops 1879048192 | bytes 4718592 | tf_op jit(solution)/shard_map/pallas_call | solution.py:124
  126.5 1.1 convert_element_type.13
  127.6 6.3 %all-to-all-start.1 = ((bf16[16,128,256]{2,1,0:T(8,128)(2,1)}), bf16[16,128,256]{2,1,0:T(8,128)(2,1)S(1)}, u32[]{:S(2)}, u32[]{:S(2)}) async-start(bf16[16,128,256]{2,1,0:T(8,128)(2,1)} %bitcast.11), calls=%async_computation.1 | async-start | bytes 2097152 | tf_op jit(solution)/shard_map/all_to_all | solution.py:187
  133.9 0.2 reshape.58
  134.1 1.3 collective-permute-start.4
  135.4 2.5 %collective-permute-done.4 = bf16[128,2048]{1,0:T(8,128)(2,1)S(1)} collective-permute-done((bf16[128,2048]{1,0:T(8,128)(2,1)S(1)}, bf16[128,2048]{1,0:T(8,128)(2,1)S(1)}, u32[]{:S(2)}, u32[]{:S(2)}) %collective-permute-start.4) | collective-permute-done | bytes 524320 | tf_op jit(solution)/shard_map/ppermute | solution.py:14
  137.9 26.4 %all-to-all-done.1 = bf16[16,128,256]{2,1,0:T(8,128)(2,1)S(1)} async-done(((bf16[16,128,256]{2,1,0:T(8,128)(2,1)}), bf16[16,128,256]{2,1,0:T(8,128)(2,1)S(1)}, u32[]{:S(2)}, u32[]{:S(2)}) %all-to-all-start.1) | async-done | bytes 1048608 | tf_op jit(solution)/shard_map/all_to_all | solution.py:187
  164.3 0.1 reduce
  164.4 0.6 slice_bitcast_fusion
  165.1 0.8 copy.10
  (6 shorter events, 0.1 us)
Async XLA Ops:
  0.6 1.2 copy-start
  4.2 14.1 %copy-start.1 = (bf16[1,128,128]{2,1,0:T(8,128)(2,1)S(1)}, bf16[1,128,128]{2,1,0:T(8,128)(2,1)}, u32[]{:S(2)}) copy-start(bf16[1,128,128]{2,1,0:T(8,128)(2,1)} %param.10) | copy-start | bytes 98308
  4.2 14.1 %copy-start.2 = (bf16[1,128,128]{2,1,0:T(8,128)(2,1)S(1)}, bf16[1,128,128]{2,1,0:T(8,128)(2,1)}, u32[]{:S(2)}) copy-start(bf16[1,128,128]{2,1,0:T(8,128)(2,1)} %param.9) | copy-start | bytes 98308
  5.2 62.9 %copy-start.3 = (s32[6]{0:T(128)S(1)}, s32[6]{0:T(128)}, u32[]{:S(2)}) copy-start(s32[6]{0:T(128)} %param.12) | copy-start | bytes 76
  5.2 88.7 %all-to-all-start = ((bf16[16,16,2048]{2,1,0:T(8,128)(2,1)}), bf16[16,16,2048]{2,1,0:T(8,128)(2,1)S(1)}, u32[]{:S(2)}, u32[]{:S(2)}) async-start(bf16[16,16,2048]{2,1,0:T(8,128)(2,1)} %pad_maximum_fusion), calls=%async_computation | async-start | bytes 2097152 | tf_op jit(solution)/shard_map/all_to_all | solution.py:162
  18.3 7.7 %collective-permute-start = (bf16[1,128,256]{2,1,0:T(8,128)(2,1)S(1)}, bf16[1,128,256]{2,1,0:T(8,128)(2,1)S(1)}, u32[]{:S(2)}, u32[]{:S(2)}) collective-permute-start(bf16[1,128,256]{2,1,0:T(8,128)(2,1)S(1)} %maximum_bitcast_fusion), channel_id=1, source_target_pairs={{0,8},{8,0},{16,24},{24,16},{32,40},{40,32},{48,56},{56,48},{64,72... | collective-permute-start | bytes 196616 | tf_op jit(solution)/shard_map/ppermute | solution.py:169
  26.0 19.9 %collective-permute-start.1 = (bf16[2,128,256]{2,1,0:T(8,128)(2,1)S(1)}, bf16[2,128,256]{2,1,0:T(8,128)(2,1)S(1)}, u32[]{:S(2)}, u32[]{:S(2)}) collective-permute-start(bf16[2,128,256]{2,1,0:T(8,128)(2,1)S(1)} %maximum_select_fusion.3), channel_id=1, source_target_pairs={{0,16},{8,24},{16,0},{24,8},{32,48},{40,56},{48,32},{56,40},{64,80... | collective-permute-start | bytes 393224 | tf_op jit(solution)/shard_map/ppermute | solution.py:169
  45.9 15.7 %collective-permute-start.2 = (bf16[4,128,256]{2,1,0:T(8,128)(2,1)S(1)}, bf16[4,128,256]{2,1,0:T(8,128)(2,1)S(1)}, u32[]{:S(2)}, u32[]{:S(2)}) collective-permute-start(bf16[4,128,256]{2,1,0:T(8,128)(2,1)S(1)} %maximum_select_fusion.2), channel_id=1, source_target_pairs={{0,32},{8,40},{16,48},{24,56},{32,0},{40,8},{48,16},{56,24},{64,96... | collective-permute-start | bytes 786440 | tf_op jit(solution)/shard_map/ppermute | solution.py:169
  61.6 30.9 %collective-permute-start.3 = (bf16[8,128,256]{2,1,0:T(8,128)(2,1)S(1)}, bf16[8,128,256]{2,1,0:T(8,128)(2,1)}, u32[]{:S(2)}, u32[]{:S(2)}) collective-permute-start(bf16[8,128,256]{2,1,0:T(8,128)(2,1)S(1)} %maximum_select_fusion.1), channel_id=1, source_target_pairs={{0,64},{8,72},{16,80},{24,88},{32,96},{40,104},{48,112},{56,120},{... | collective-permute-start | bytes 1572872 | tf_op jit(solution)/shard_map/ppermute | solution.py:169
  127.6 36.7 %all-to-all-start.1 = ((bf16[16,128,256]{2,1,0:T(8,128)(2,1)}), bf16[16,128,256]{2,1,0:T(8,128)(2,1)S(1)}, u32[]{:S(2)}, u32[]{:S(2)}) async-start(bf16[16,128,256]{2,1,0:T(8,128)(2,1)} %bitcast.11), calls=%async_computation.1 | async-start | bytes 2097152 | tf_op jit(solution)/shard_map/all_to_all | solution.py:187
  134.1 3.8 %collective-permute-start.4 = (bf16[128,2048]{1,0:T(8,128)(2,1)S(1)}, bf16[128,2048]{1,0:T(8,128)(2,1)S(1)}, u32[]{:S(2)}, u32[]{:S(2)}) collective-permute-start(bf16[128,2048]{1,0:T(8,128)(2,1)S(1)} %reshape.58), channel_id=1, source_target_pairs={{128,0},{256,128},{384,256},{129,1},{257,129},{385,257},{130,2},{2... | collective-permute-start | bytes 1572872 | tf_op jit(solution)/shard_map/ppermute | solution.py:14

commit v7 on v5

--- a/solution.py
+++ b/solution.py
@@ -111,7 +111,7 @@
     lax.fori_loop(0, row_blocks, row_block, 0)
 
 
-def attend_kernel(flat_query, flat_grad, key_full, value_full, ends, block_start, heads, kb_size=512):
+def attend_kernel(flat_query, flat_grad, key_full, value_full, ends, block_start, heads, kb_size=1024):
     rows, head_width = flat_query.shape
     keys = key_full.shape[0]
     rb_size = rows // block_start.shape[0]

time: 140 us -> 141 us (level)
  no operation moved by 1% of the time
where the time goes in v7:
time: 141 us; the launch traced here: 140 us
  waiting for transfers between devices  80.4 us (57%)
  Pallas kernels  25.6 us (18%)
  starting transfers between devices  19 us (13%)
  local copies, waits for them, and re-layouts  9.85 us (7%)
  other arithmetic  4.59 us (3%)
    all_to_all x1, waiting for transfers between devices, body(): lax.all_to_all(packed, 'cp', split_axis=0, concat_axis=0, tiled=True)  51.6 us
    all_to_all x1, waiting for transfers between devices, body(): lax.all_to_all(terms.astype(jnp.bfloat16).reshape(shards, tokens, 2 * hea...  26.3 us
    pallas_call x1, Pallas kernels, attend_kernel(): pl.pallas_call(functools.partial(_attend_kernel, heads, kb_size), out_sha...  25.6 us
    all_to_all x1, starting transfers between devices, body(): lax.all_to_all(packed, 'cp', split_axis=0, concat_axis=0, tiled=True)  13 us
    all_to_all x1, starting transfers between devices, body(): lax.all_to_all(terms.astype(jnp.bfloat16).reshape(shards, tokens, 2 * hea...  4.68 us
  transfers between devices with their start and end apart: 3, of which 3 were waited for; matrix products, arithmetic and copies ran while one was open for 0% of the time, Pallas kernels for 0%

profile of v7, /device:TPU:56, one launch (start us, length us, event | category | flops | bytes accessed | tf_op | source)
XLA Modules:
  0.0 140.3 jit_solution(2802111795382603634)
XLA Ops:
  0.6 0.0 copy-start
  0.6 1.1 select_reduce_fusion
  1.8 0.8 reshape_squeeze.14
  2.6 0.8 reshape_squeeze.15
  3.4 0.0 copy-done
  3.4 0.6 gather_fusion.1
  3.9 1.6 %gather_fusion = bf16[16,8,2048]{2,1,0:T(8,128)(2,1)S(1)} fusion(bf16[16,8,2048]{2,1,0:T(8,128)(2,1)} %bitcast.19, s32[1024]{0:T(1024)S(1)} %pad_clamp_fusion), kind=kCustom, calls=%fused_computation.clone | custom fusion | bytes 1048640 | tf_op jit(solution)/shard_map/jit(_take)/gather | solution.py:159
  5.6 0.2 broadcast_select_fusion.1
  5.8 0.1 broadcast_in_dim.33
  5.9 1.6 %pad_maximum_fusion = bf16[16,32,2048]{2,1,0:T(8,128)(2,1)} fusion(bf16[16,16,2048]{2,1,0:T(8,128)(2,1)S(1)} %broadcast_in_dim.33, bf16[16,8,2048]{2,1,0:T(8,128)(2,1)S(1)} %get-tuple-element.17, bf16[16,8,2048]{2,1,0:T(8,128)(2,1)S(1)} %get-tuple-element.16), kind=kLoop, calls=%fused_computation.2 | loop fusion | flops 6291456 | bytes 4194304 | tf_op jit(solution)/shard_map/concatenate | solution.py:163
  7.5 0.0 copy-start.2
  7.5 13.0 %all-to-all-start = ((bf16[16,32,2048]{2,1,0:T(8,128)(2,1)}), bf16[16,32,2048]{2,1,0:T(8,128)(2,1)S(1)}, u32[]{:S(2)}, u32[]{:S(2)}) async-start(bf16[16,32,2048]{2,1,0:T(8,128)(2,1)} %pad_maximum_fusion), calls=%async_computation | async-start | bytes 4194304 | tf_op jit(solution)/shard_map/all_to_all | solution.py:171
  20.5 0.0 copy-done.2
  20.5 0.2 reduce-window.8
  20.7 0.2 multiply_reduce_fusion
  20.9 0.1 convert_reduce_fusion
  21.0 51.6 %all-to-all-done = bf16[16,32,2048]{2,1,0:T(8,128)(2,1)S(1)} async-done(((bf16[16,32,2048]{2,1,0:T(8,128)(2,1)}), bf16[16,32,2048]{2,1,0:T(8,128)(2,1)S(1)}, u32[]{:S(2)}, u32[]{:S(2)}) %all-to-all-start) | async-done | bytes 2097184 | tf_op jit(solution)/shard_map/all_to_all | solution.py:171
  72.6 1.2 fusion
  73.8 0.0 copy-start.1
  73.8 1.3 reshape.61.v_ref
  75.1 1.3 reshape.60.k_ref
  76.4 0.2 reshape.59.g_ref
  76.7 0.0 copy-done.1
  76.7 0.2 reshape.58.q_ref
  76.9 25.6 %shard_map.85 = (bf16[2048,128]{1,0:T(8,128)(2,1)S(1)}, f32[2048,256]{1,0:T(8,128)S(1)}) custom-call(s32[6]{0:T(128)S(1)} %bitcast.17, s32[16]{0:T(128)S(1)} %multiply_add_fusion.start_ref, s32[1,2048]{1,0:T(1,128)S(1)} %bitcast.15, bf16[2048,128]{1,0:T(8,128)(2,1)S(1)} %reshape.58.q_ref, bf16[2048,128]{1,0:T(8,128)(2,1)S(1)} %reshape.59.g_ref, ...), custom_call_target="tpu_custom_call" | custom-call | flops 1879048192 | bytes 4718592 | tf_op jit(solution)/shard_map/pallas_call | solution.py:124
  102.5 1.1 convert_element_type.13
  103.6 4.7 %all-to-all-start.1 = ((bf16[16,128,256]{2,1,0:T(8,128)(2,1)}), bf16[16,128,256]{2,1,0:T(8,128)(2,1)S(1)}, u32[]{:S(2)}, u32[]{:S(2)}) async-start(bf16[16,128,256]{2,1,0:T(8,128)(2,1)} %bitcast.7), calls=%async_computation.1 | async-start | bytes 2097152 | tf_op jit(solution)/shard_map/all_to_all | solution.py:191
  108.3 0.2 reshape.62
  108.6 1.3 collective-permute-start
  109.9 2.5 %collective-permute-done = bf16[128,2048]{1,0:T(8,128)(2,1)S(1)} collective-permute-done((bf16[128,2048]{1,0:T(8,128)(2,1)S(1)}, bf16[128,2048]{1,0:T(8,128)(2,1)S(1)}, u32[]{:S(2)}, u32[]{:S(2)}) %collective-permute-start) | collective-permute-done | bytes 524320 | tf_op jit(solution)/shard_map/ppermute | solution.py:14
  112.4 26.3 %all-to-all-done.1 = bf16[16,128,256]{2,1,0:T(8,128)(2,1)S(1)} async-done(((bf16[16,128,256]{2,1,0:T(8,128)(2,1)}), bf16[16,128,256]{2,1,0:T(8,128)(2,1)S(1)}, u32[]{:S(2)}, u32[]{:S(2)}) %all-to-all-start.1) | async-done | bytes 1048608 | tf_op jit(solution)/shard_map/all_to_all | solution.py:191
  138.7 0.1 reduce
  138.9 0.6 slice_bitcast_fusion
  139.5 0.8 copy.10
  (4 shorter events, 0.0 us)
Async XLA Ops:
  0.6 2.7 %copy-start = (bf16[1,128,2048]{2,1,0:T(8,128)(2,1)S(1)}, bf16[1,128,2048]{2,1,0:T(8,128)(2,1)}, u32[]{:S(2)}) copy-start(bf16[1,128,2048]{2,1,0:T(8,128)(2,1)} %param.11) | copy-start | bytes 1572868
  7.5 13.0 %copy-start.2 = (s32[6]{0:T(128)S(1)}, s32[6]{0:T(128)}, u32[]{:S(2)}) copy-start(s32[6]{0:T(128)} %param.12) | copy-start | bytes 76
  7.5 65.1 %all-to-all-start = ((bf16[16,32,2048]{2,1,0:T(8,128)(2,1)}), bf16[16,32,2048]{2,1,0:T(8,128)(2,1)S(1)}, u32[]{:S(2)}, u32[]{:S(2)}) async-start(bf16[16,32,2048]{2,1,0:T(8,128)(2,1)} %pad_maximum_fusion), calls=%async_computation | async-start | bytes 4194304 | tf_op jit(solution)/shard_map/all_to_all | solution.py:171
  73.8 2.9 %copy-start.1 = (bf16[16,8,2048]{2,1,0:T(8,128)(2,1)S(1)}, bf16[16,8,2048]{2,1,0:T(8,128)(2,1)}, u32[]{:S(2)}) copy-start(bf16[16,8,2048]{2,1,0:T(8,128)(2,1)} %get-tuple-element.13) | copy-start | bytes 1572868
  103.6 35.1 %all-to-all-start.1 = ((bf16[16,128,256]{2,1,0:T(8,128)(2,1)}), bf16[16,128,256]{2,1,0:T(8,128)(2,1)S(1)}, u32[]{:S(2)}, u32[]{:S(2)}) async-start(bf16[16,128,256]{2,1,0:T(8,128)(2,1)} %bitcast.7), calls=%async_computation.1 | async-start | bytes 2097152 | tf_op jit(solution)/shard_map/all_to_all | solution.py:191
  108.6 3.8 %collective-permute-start = (bf16[128,2048]{1,0:T(8,128)(2,1)S(1)}, bf16[128,2048]{1,0:T(8,128)(2,1)S(1)}, u32[]{:S(2)}, u32[]{:S(2)}) collective-permute-start(bf16[128,2048]{1,0:T(8,128)(2,1)S(1)} %reshape.62), channel_id=1, source_target_pairs={{128,0},{256,128},{384,256},{129,1},{257,129},{385,257},{130,2},{2... | collective-permute-start | bytes 1572872 | tf_op jit(solution)/shard_map/ppermute | solution.py:14

commit v8 on v7

--- a/solution.py
+++ b/solution.py
@@ -144,6 +144,7 @@
     tokens = query.shape[1]
     width = query.shape[2]
     head_width = key.shape[2]
+    head_count = width // head_width
     shards = lax.axis_size("cp")
     own_index = lax.axis_index("cp")
     block_rows = tokens // shards
@@ -160,37 +161,30 @@
 
     key_rows = tokens * head_width // width
     own_keys = jnp.concatenate([key[0].reshape(key_rows, width), value[0].reshape(key_rows, width)], axis=0)
-    packed = jnp.concatenate(
-        [
-            reorder(query[0]),
-            reorder(out_grad[0]),
-            jnp.broadcast_to(own_keys[None], (shards,) + own_keys.shape),
-        ],
-        axis=1,
-    )
-    received = lax.all_to_all(packed, "cp", split_axis=0, concat_axis=0, tiled=True)
-    query_sent = received[:, :block_rows]
-    grad_sent = received[:, block_rows : 2 * block_rows]
-    key_at = 2 * block_rows
-    key_full = received[:, key_at : key_at + key_rows].reshape(key_count, head_width)
-    value_full = received[:, key_at + key_rows :].reshape(key_count, head_width)
+    keys_taken = lax.all_to_all(
+        jnp.broadcast_to(own_keys[None], (shards,) + own_keys.shape), "cp", split_axis=0, concat_axis=0, tiled=True
+    )
+    key_full = keys_taken[:, :key_rows].reshape(key_count, head_width)
+    value_full = keys_taken[:, key_rows:].reshape(key_count, head_width)
     ends = jnp.cumsum(lengths).astype(jnp.int32)
-    taken = lax.dynamic_index_in_dim(inverse, own_index, 1, keepdims=False)
-    head_count = width // head_width
     dquery, terms = attend_kernel(
-        query_sent.reshape(tokens * head_count, head_width),
-        grad_sent.reshape(tokens * head_count, head_width),
+        query[0].reshape(tokens * head_count, head_width),
+        out_grad[0].reshape(tokens * head_count, head_width),
         key_full,
         value_full,
         ends,
-        iota * tokens + taken * block_rows,
+        own_index * tokens + iota * block_rows,
         head_count,
     )
     dquery = dquery.reshape(tokens, width)
-    handed = passed_along(dquery, "pp", -1)
-    partials = lax.all_to_all(
-        terms.astype(jnp.bfloat16).reshape(shards, tokens, 2 * head_width), "cp", split_axis=0, concat_axis=0, tiled=True
-    )
+    term_rows = tokens * 2 * head_width // width
+    packed = jnp.concatenate(
+        [reorder(dquery), terms.astype(jnp.bfloat16).reshape(shards, term_rows, width)], axis=1
+    )
+    received = lax.all_to_all(packed, "cp", split_axis=0, concat_axis=0, tiled=True)
+    planned = received[:, :block_rows].reshape(tokens, width)
+    handed = passed_along(planned, "pp", -1)
+    partials = received[:, block_rows:].reshape(shards, tokens, 2 * head_width)
     summed = jnp.sum(partials.astype(jnp.float32), axis=0)
     key_grad = summed[:, :head_width].astype(jnp.bfloat16)
     value_grad = summed[:, head_width:].astype(jnp.bfloat16)

time: 141 us -> 147 us (1.043)
  the two profiles are of different devices: /device:TPU:56 before, /device:TPU:1 now
where the time goes in v8:
time: 147 us
  blocking collectives  63.5 us (43%)
  waiting for transfers between devices  31.8 us (22%)
  Pallas kernels  24.3 us (17%)
  starting transfers between devices  18.6 us (13%)
  local copies, waits for them, and re-layouts  6.57 us (4%)
    all_to_all x1, blocking collectives, body(): lax.all_to_all(packed, 'cp', split_axis=0, concat_axis=0, tiled=True)  63.5 us
    all_to_all x1, waiting for transfers between devices, body(): lax.all_to_all(jnp.broadcast_to(own_keys[None], (shards,) + own_keys.shap...  25.6 us
    pallas_call x1, Pallas kernels, attend_kernel(): pl.pallas_call(functools.partial(_attend_kernel, heads, kb_size), out_sha...  24.3 us
    all_to_all x1, starting transfers between devices, body(): lax.all_to_all(jnp.broadcast_to(own_keys[None], (shards,) + own_keys.shap...  13.6 us
    ppermute x1, waiting for transfers between devices, passed_along(): return lax.ppermute(array, axis, pairs)  6.22 us
    ppermute x1, starting transfers between devices, passed_along(): return lax.ppermute(array, axis, pairs)  5.08 us
  transfers between devices with their start and end apart: 2, of which 2 were waited for; matrix products, arithmetic and copies ran while one was open for 1% of the time, Pallas kernels for 0%

profile of v8, /device:TPU:1, one launch (start us, length us, event | category | flops | bytes accessed | tf_op | source)
XLA Modules:
  0.0 146.8 jit_solution(15646646860913043028)
XLA Ops:
  0.6 0.8 reshape_squeeze.15
  1.4 0.8 reshape_squeeze.14
  2.2 0.0 copy-start.3
  2.2 0.0 copy-start
  2.2 1.1 broadcast_in_dim.35
  3.3 0.0 copy-start.1
  3.3 13.6 %all-to-all-start = ((bf16[16,16,2048]{2,1,0:T(8,128)(2,1)}), bf16[16,16,2048]{2,1,0:T(8,128)(2,1)S(1)}, u32[]{:S(2)}, u32[]{:S(2)}) async-start(bf16[16,16,2048]{2,1,0:T(8,128)(2,1)} %broadcast_in_dim.35), calls=%async_computation | async-start | bytes 2097152 | tf_op jit(solution)/shard_map/all_to_all | solution.py:164
  16.9 0.0 copy-start.2
  16.9 0.0 copy-done.3
  16.9 0.2 reduce-window.8
  17.1 0.0 copy-done
  17.1 0.2 reshape_squeeze.12.q_ref
  17.4 0.0 copy-done.1
  17.4 0.2 reshape_squeeze.13.g_ref
  17.6 0.0 copy-done.2
  17.6 0.3 select_reduce_fusion
  18.1 0.1 convert_reduce_fusion
  18.2 25.6 %all-to-all-done = bf16[16,16,2048]{2,1,0:T(8,128)(2,1)S(1)} async-done(((bf16[16,16,2048]{2,1,0:T(8,128)(2,1)}), bf16[16,16,2048]{2,1,0:T(8,128)(2,1)S(1)}, u32[]{:S(2)}, u32[]{:S(2)}) %all-to-all-start) | async-done | bytes 1048608 | tf_op jit(solution)/shard_map/all_to_all | solution.py:164
  43.7 0.1 fusion.1
  43.8 0.2 reshape.81.k_ref
  44.1 0.2 reshape.82.v_ref
  44.3 24.3 %shard_map.85 = (bf16[2048,128]{1,0:T(8,128)(2,1)S(1)}, f32[2048,256]{1,0:T(8,128)S(1)}) custom-call(s32[6]{0:T(128)S(1)} %bitcast.18, s32[16]{0:T(128)S(1)} %multiply_add_fusion.start_ref, s32[1,2048]{1,0:T(1,128)S(1)} %bitcast.16, bf16[2048,128]{1,0:T(8,128)(2,1)S(1)} %reshape_squeeze.12.q_ref, bf16[2048,128]{1,0:T(8,128)(2,1)S(1)} %reshape_squeeze.13.g_ref, ...), custom_call_target="tpu_custom_call" | custom-call | flops 1879048192 | bytes 4718592 | tf_op jit(solution)/shard_map/pallas_call | solution.py:124
  68.6 0.1 convert_element_type.14
  68.7 0.5 reshape.83
  69.2 0.2 reshape_reshape.3
  69.5 0.6 gather_fusion
  70.0 0.1 broadcast_select_fusion
  70.2 0.1 pad_maximum_fusion
  70.3 63.5 %all_to_all.10 = bf16[16,24,2048]{2,1,0:T(8,128)(2,1)S(1)} all-to-all(bf16[16,24,2048]{2,1,0:T(8,128)(2,1)S(1)} %pad_maximum_fusion), channel_id=1, replica_groups=mesh['pp'=4,'cp'=16,'tp'=8] {'cp'}, dimensions={0} | all-to-all | bytes 3145728 | tf_op jit(solution)/shard_map/all_to_all | solution.py:184
  133.8 5.1 %collective-permute-start = (bf16[128,2048]{1,0:T(8,128)(2,1)S(1)}, bf16[128,2048]{1,0:T(8,128)(2,1)S(1)}, u32[]{:S(2)}, u32[]{:S(2)}) collective-permute-start(bf16[128,2048]{1,0:T(8,128)(2,1)S(1)} %slice_bitcast_fusion), channel_id=1, source_target_pairs={{128,0},{256,128},{384,256},{129,1},{257,129},{385,257},{130,2},{2... | collective-permute-start | bytes 1572872 | tf_op jit(solution)/shard_map/ppermute | solution.py:14
  138.9 0.1 slice_reduce_fusion
  139.1 0.6 slice_bitcast_fusion.1
  139.8 6.2 %collective-permute-done = bf16[128,2048]{1,0:T(8,128)(2,1)S(1)} collective-permute-done((bf16[128,2048]{1,0:T(8,128)(2,1)S(1)}, bf16[128,2048]{1,0:T(8,128)(2,1)S(1)}, u32[]{:S(2)}, u32[]{:S(2)}) %collective-permute-start) | collective-permute-done | bytes 524320 | tf_op jit(solution)/shard_map/ppermute | solution.py:14
  146.0 0.8 copy.10
  (7 shorter events, 0.1 us)
Async XLA Ops:
  2.2 14.7 %copy-start.3 = (s32[6]{0:T(128)S(1)}, s32[6]{0:T(128)}, u32[]{:S(2)}) copy-start(s32[6]{0:T(128)} %param.10) | copy-start | bytes 76
  2.2 14.9 %copy-start = (bf16[1,128,2048]{2,1,0:T(8,128)(2,1)S(1)}, bf16[1,128,2048]{2,1,0:T(8,128)(2,1)}, u32[]{:S(2)}) copy-start(bf16[1,128,2048]{2,1,0:T(8,128)(2,1)} %param.6) | copy-start | bytes 1572868
  3.3 14.0 %copy-start.1 = (bf16[1,128,2048]{2,1,0:T(8,128)(2,1)S(1)}, bf16[1,128,2048]{2,1,0:T(8,128)(2,1)}, u32[]{:S(2)}) copy-start(bf16[1,128,2048]{2,1,0:T(8,128)(2,1)} %param.9) | copy-start | bytes 1572868
  3.3 40.4 %all-to-all-start = ((bf16[16,16,2048]{2,1,0:T(8,128)(2,1)}), bf16[16,16,2048]{2,1,0:T(8,128)(2,1)S(1)}, u32[]{:S(2)}, u32[]{:S(2)}) async-start(bf16[16,16,2048]{2,1,0:T(8,128)(2,1)} %broadcast_in_dim.35), calls=%async_computation | async-start | bytes 2097152 | tf_op jit(solution)/shard_map/all_to_all | solution.py:164
  16.9 0.7 copy-start.2
  133.8 12.1 %collective-permute-start = (bf16[128,2048]{1,0:T(8,128)(2,1)S(1)}, bf16[128,2048]{1,0:T(8,128)(2,1)S(1)}, u32[]{:S(2)}, u32[]{:S(2)}) collective-permute-start(bf16[128,2048]{1,0:T(8,128)(2,1)S(1)} %slice_bitcast_fusion), channel_id=1, source_target_pairs={{128,0},{256,128},{384,256},{129,1},{257,129},{385,257},{130,2},{2... | collective-permute-start | bytes 1572872 | tf_op jit(solution)/shard_map/ppermute | solution.py:14

commit v9 on v8

--- a/solution.py
+++ b/solution.py
@@ -177,14 +177,11 @@
         head_count,
     )
     dquery = dquery.reshape(tokens, width)
-    term_rows = tokens * 2 * head_width // width
-    packed = jnp.concatenate(
-        [reorder(dquery), terms.astype(jnp.bfloat16).reshape(shards, term_rows, width)], axis=1
-    )
-    received = lax.all_to_all(packed, "cp", split_axis=0, concat_axis=0, tiled=True)
-    planned = received[:, :block_rows].reshape(tokens, width)
-    handed = passed_along(planned, "pp", -1)
-    partials = received[:, block_rows:].reshape(shards, tokens, 2 * head_width)
+    planned = lax.all_to_all(reorder(dquery), "cp", split_axis=0, concat_axis=0, tiled=True)
+    handed = passed_along(planned.reshape(tokens, width), "pp", -1)
+    partials = lax.all_to_all(
+        terms.astype(jnp.bfloat16).reshape(shards, tokens, 2 * head_width), "cp", split_axis=0, concat_axis=0, tiled=True
+    )
     summed = jnp.sum(partials.astype(jnp.float32), axis=0)
     key_grad = summed[:, :head_width].astype(jnp.bfloat16)
     value_grad = summed[:, head_width:].astype(jnp.bfloat16)

time: 147 us -> 134 us (0.912)
  the two profiles are of different devices: /device:TPU:1 before, /device:TPU:56 now
where the time goes in v9:
time: 134 us; the launch traced here: 133 us
  waiting for transfers between devices  71.9 us (54%)
  Pallas kernels  24.3 us (18%)
  starting transfers between devices  22.2 us (17%)
  local copies, waits for them, and re-layouts  11.5 us (9%)
  other arithmetic  2.8 us (2%)
    all_to_all x1, waiting for transfers between devices, body(): lax.all_to_all(jnp.broadcast_to(own_keys[None], (shards,) + own_keys.shap...  29 us
    pallas_call x1, Pallas kernels, attend_kernel(): pl.pallas_call(functools.partial(_attend_kernel, heads, kb_size), out_sha...  24.3 us
    all_to_all x1, waiting for transfers between devices, body(): lax.all_to_all(terms.astype(jnp.bfloat16).reshape(shards, tokens, 2 * hea...  23.3 us
    all_to_all x1, waiting for transfers between devices, body(): lax.all_to_all(reorder(dquery), 'cp', split_axis=0, concat_axis=0, tiled=...  16.9 us
    all_to_all x1, starting transfers between devices, body(): lax.all_to_all(jnp.broadcast_to(own_keys[None], (shards,) + own_keys.shap...  13 us
    all_to_all x1, starting transfers between devices, body(): lax.all_to_all(reorder(dquery), 'cp', split_axis=0, concat_axis=0, tiled=...  4.24 us
    unnamed x15, local copies, waits for them, and re-layouts  3.68 us
    all_to_all x1, starting transfers between devices, body(): lax.all_to_all(terms.astype(jnp.bfloat16).reshape(shards, tokens, 2 * hea...  3.65 us
  transfers between devices with their start and end apart: 4, of which 4 were waited for; matrix products, arithmetic and copies ran while one was open for 2% of the time, Pallas kernels for 0%

profile of v9, /device:TPU:56, one launch (start us, length us, event | category | flops | bytes accessed | tf_op | source)
XLA Modules:
  0.0 133.5 jit_solution(9740505605694635441)
XLA Ops:
  0.6 0.0 copy-start.6
  0.6 0.0 copy-start.3
  0.7 0.8 reshape_squeeze.15
  1.5 0.8 reshape_squeeze.14
  2.3 0.0 copy-start.4
  2.3 1.1 broadcast_in_dim.35
  3.4 0.0 copy-start.5
  3.4 13.0 %all-to-all-start = ((bf16[16,16,2048]{2,1,0:T(8,128)(2,1)}), bf16[16,16,2048]{2,1,0:T(8,128)(2,1)S(1)}, u32[]{:S(2)}, u32[]{:S(2)}) async-start(bf16[16,16,2048]{2,1,0:T(8,128)(2,1)} %broadcast_in_dim.35), calls=%async_computation | async-start | bytes 2097152 | tf_op jit(solution)/shard_map/all_to_all | solution.py:164
  16.4 0.0 copy-done.6
  16.4 0.2 reduce-window.8
  16.6 0.0 copy-done.3
  16.6 0.2 reshape_squeeze.12.q_ref
  16.9 0.0 copy-done.4
  16.9 0.2 reshape_squeeze.13.g_ref
  17.1 0.0 copy-done.5
  17.1 0.3 select_reduce_fusion
  17.5 0.1 convert_reduce_fusion
  17.6 29.0 %all-to-all-done = bf16[16,16,2048]{2,1,0:T(8,128)(2,1)S(1)} async-done(((bf16[16,16,2048]{2,1,0:T(8,128)(2,1)}), bf16[16,16,2048]{2,1,0:T(8,128)(2,1)S(1)}, u32[]{:S(2)}, u32[]{:S(2)}) %all-to-all-start) | async-done | bytes 1048608 | tf_op jit(solution)/shard_map/all_to_all | solution.py:164
  46.6 0.1 fusion.1
  46.7 1.0 reshape.79.k_ref
  47.7 1.0 reshape.80.v_ref
  48.8 0.0 copy-start
  48.8 1.0 copy-done
  49.8 0.0 copy-start.1
  49.8 1.0 copy-done.1
  50.8 24.3 %shard_map.85 = (bf16[2048,128]{1,0:T(8,128)(2,1)S(1)}, f32[2048,256]{1,0:T(8,128)S(1)}) custom-call(s32[6]{0:T(128)S(1)} %bitcast.18, s32[16]{0:T(128)S(1)} %multiply_add_fusion.start_ref, s32[1,2048]{1,0:T(1,128)S(1)} %bitcast.16, bf16[2048,128]{1,0:T(8,128)(2,1)S(1)} %reshape_squeeze.12.q_ref, bf16[2048,128]{1,0:T(8,128)(2,1)S(1)} %reshape_squeeze.13.g_ref, ...), custom_call_target="tpu_custom_call" | custom-call | flops 1879048192 | bytes 4718592 | tf_op jit(solution)/shard_map/pallas_call | solution.py:124
  75.1 0.0 copy-start.2
  75.1 0.8 copy-done.2
  75.9 1.3 reshape_reshape.3
  77.2 0.6 gather_fusion
  77.8 0.9 broadcast_select_fusion
  78.7 4.2 %all-to-all-start.1 = ((bf16[16,8,2048]{2,1,0:T(8,128)(2,1)}), bf16[16,8,2048]{2,1,0:T(8,128)(2,1)}, u32[]{:S(2)}, u32[]{:S(2)}) async-start(bf16[16,8,2048]{2,1,0:T(8,128)(2,1)} %broadcast_select_fusion), calls=%async_computation.1 | async-start | bytes 1048576 | tf_op jit(solution)/shard_map/all_to_all | solution.py:180
  82.9 1.1 convert_element_type.13
  84.0 16.9 %all-to-all-done.1 = bf16[16,8,2048]{2,1,0:T(8,128)(2,1)} async-done(((bf16[16,8,2048]{2,1,0:T(8,128)(2,1)}), bf16[16,8,2048]{2,1,0:T(8,128)(2,1)}, u32[]{:S(2)}, u32[]{:S(2)}) %all-to-all-start.1) | async-done | bytes 524320 | tf_op jit(solution)/shard_map/all_to_all | solution.py:180
  100.9 3.7 %all-to-all-start.2 = ((bf16[16,128,256]{2,1,0:T(8,128)(2,1)}), bf16[16,128,256]{2,1,0:T(8,128)(2,1)S(1)}, u32[]{:S(2)}, u32[]{:S(2)}) async-start(bf16[16,128,256]{2,1,0:T(8,128)(2,1)} %bitcast.8), calls=%async_computation.2 | async-start | bytes 2097152 | tf_op jit(solution)/shard_map/all_to_all | solution.py:182
  104.6 1.3 collective-permute-start
  105.9 2.7 %collective-permute-done = bf16[128,2048]{1,0:T(8,128)(2,1)S(1)} collective-permute-done((bf16[128,2048]{1,0:T(8,128)(2,1)}, bf16[128,2048]{1,0:T(8,128)(2,1)S(1)}, u32[]{:S(2)}, u32[]{:S(2)}) %collective-permute-start) | collective-permute-done | bytes 524320 | tf_op jit(solution)/shard_map/ppermute | solution.py:14
  108.6 23.3 %all-to-all-done.2 = bf16[16,128,256]{2,1,0:T(8,128)(2,1)S(1)} async-done(((bf16[16,128,256]{2,1,0:T(8,128)(2,1)}), bf16[16,128,256]{2,1,0:T(8,128)(2,1)S(1)}, u32[]{:S(2)}, u32[]{:S(2)}) %all-to-all-start.2) | async-done | bytes 1048608 | tf_op jit(solution)/shard_map/all_to_all | solution.py:182
  131.9 0.1 reduce
  132.1 0.6 slice_bitcast_fusion
  132.7 0.8 copy.10
  (5 shorter events, 0.1 us)
Async XLA Ops:
  0.6 15.8 %copy-start.6 = (s32[6]{0:T(128)S(1)}, s32[6]{0:T(128)}, u32[]{:S(2)}) copy-start(s32[6]{0:T(128)} %param.10) | copy-start | bytes 76
  0.6 16.0 %copy-start.3 = (bf16[1,128,2048]{2,1,0:T(8,128)(2,1)S(1)}, bf16[1,128,2048]{2,1,0:T(8,128)(2,1)}, u32[]{:S(2)}) copy-start(bf16[1,128,2048]{2,1,0:T(8,128)(2,1)} %param.6) | copy-start | bytes 1572868
  2.3 14.6 %copy-start.4 = (bf16[1,128,2048]{2,1,0:T(8,128)(2,1)S(1)}, bf16[1,128,2048]{2,1,0:T(8,128)(2,1)}, u32[]{:S(2)}) copy-start(bf16[1,128,2048]{2,1,0:T(8,128)(2,1)} %param.9) | copy-start | bytes 1572868
  3.4 13.7 %copy-start.5 = (s32[16,16]{1,0:T(8,128)S(1)}, s32[16,16]{1,0:T(8,128)}, u32[]{:S(2)}) copy-start(s32[16,16]{1,0:T(8,128)} %param.11) | copy-start | bytes 3076
  3.4 43.2 %all-to-all-start = ((bf16[16,16,2048]{2,1,0:T(8,128)(2,1)}), bf16[16,16,2048]{2,1,0:T(8,128)(2,1)S(1)}, u32[]{:S(2)}, u32[]{:S(2)}) async-start(bf16[16,16,2048]{2,1,0:T(8,128)(2,1)} %broadcast_in_dim.35), calls=%async_computation | async-start | bytes 2097152 | tf_op jit(solution)/shard_map/all_to_all | solution.py:164
  48.8 1.0 copy-start
  49.8 1.0 copy-start.1
  75.1 0.8 copy-start.2
  78.7 22.2 %all-to-all-start.1 = ((bf16[16,8,2048]{2,1,0:T(8,128)(2,1)}), bf16[16,8,2048]{2,1,0:T(8,128)(2,1)}, u32[]{:S(2)}, u32[]{:S(2)}) async-start(bf16[16,8,2048]{2,1,0:T(8,128)(2,1)} %broadcast_select_fusion), calls=%async_computation.1 | async-start | bytes 1048576 | tf_op jit(solution)/shard_map/all_to_all | solution.py:180
  100.9 31.0 %all-to-all-start.2 = ((bf16[16,128,256]{2,1,0:T(8,128)(2,1)}), bf16[16,128,256]{2,1,0:T(8,128)(2,1)S(1)}, u32[]{:S(2)}, u32[]{:S(2)}) async-start(bf16[16,128,256]{2,1,0:T(8,128)(2,1)} %bitcast.8), calls=%async_computation.2 | async-start | bytes 2097152 | tf_op jit(solution)/shard_map/all_to_all | solution.py:182
  104.6 4.0 %collective-permute-start = (bf16[128,2048]{1,0:T(8,128)(2,1)}, bf16[128,2048]{1,0:T(8,128)(2,1)S(1)}, u32[]{:S(2)}, u32[]{:S(2)}) collective-permute-start(bf16[128,2048]{1,0:T(8,128)(2,1)} %bitcast.6), channel_id=1, source_target_pairs={{128,0},{256,128},{384,256},{129,1},{257,129},{385,257},{130,2},{2... | collective-permute-start | bytes 1572872 | tf_op jit(solution)/shard_map/ppermute | solution.py:14

commit v10 on v7

--- a/solution.py
+++ b/solution.py
@@ -21,18 +21,20 @@
     return doc
 
 
-def _attend_kernel(heads, kb_size, ends_ref, start_ref, kdoc_ref, q_ref, g_ref, k_ref, v_ref, dq_ref, dkv_ref, top_ref, total_ref, weighted_ref, dq_acc):
+def _attend_kernel(heads, kb_size, sub, ends_ref, start_ref, kdoc_ref, q_ref, g_ref, k_ref, v_ref, dq_ref, dkv_ref, top_ref, total_ref, weighted_ref, dq_acc):
     rows, head_width = q_ref.shape
     keys = k_ref.shape[0]
-    rb_size = rows // start_ref.shape[0]
+    piece = rows // start_ref.shape[0]
+    rb_size = piece * sub
     row_blocks = rows // rb_size
     key_blocks = keys // kb_size
-    tokens_per_block = rb_size // heads
+    tokens_per_block = piece // heads
     scale = head_width ** (-0.5)
     dkv_ref[...] = jnp.zeros_like(dkv_ref)
-    row_iota = lax.broadcasted_iota(jnp.int32, (rb_size, kb_size), 0) // heads
+    row_raw = lax.broadcasted_iota(jnp.int32, (rb_size, kb_size), 0)
+    row_iota = (row_raw % piece) // heads
+    row_part = row_raw // piece
     col_iota = lax.broadcasted_iota(jnp.int32, (rb_size, kb_size), 1)
-    row_iota1 = lax.broadcasted_iota(jnp.int32, (rb_size, 1), 0) // heads
 
     def vector_doc(position):
         doc = jnp.zeros(position.shape, jnp.int32)
@@ -41,15 +43,17 @@
         return doc
 
     def row_block(rb, carry):
-        first = start_ref[rb]
-        last = first + tokens_per_block - 1
-        first_doc = _doc_of(ends_ref, first)
-        last_doc = _doc_of(ends_ref, last)
+        firsts = [start_ref[rb * sub + i] for i in range(sub)]
+        first_docs = [_doc_of(ends_ref, f) for f in firsts]
+        last_docs = [_doc_of(ends_ref, f + tokens_per_block - 1) for f in firsts]
         r0 = pl.multiple_of(rb * rb_size, rb_size)
         q = q_ref[pl.ds(r0, rb_size), :]
         g = g_ref[pl.ds(r0, rb_size), :]
-        row_pos = first + row_iota
-        row_doc = vector_doc(first + row_iota1)
+        row_first = firsts[0]
+        for i in range(1, sub):
+            row_first = jnp.where(row_part == i, firsts[i], row_first)
+        row_pos = row_first + row_iota
+        row_doc = vector_doc(row_pos)
         top_ref[...] = jnp.full(top_ref.shape, -1e30, jnp.float32)
         total_ref[...] = jnp.zeros(total_ref.shape, jnp.float32)
         weighted_ref[...] = jnp.zeros(weighted_ref.shape, jnp.float32)
@@ -57,7 +61,13 @@
 
         def seen(kb):
             k0 = kb * kb_size
-            return (k0 <= last) & (_doc_of(ends_ref, k0) <= last_doc) & (_doc_of(ends_ref, k0 + kb_size - 1) >= first_doc)
+            k0_doc = _doc_of(ends_ref, k0)
+            k1_doc = _doc_of(ends_ref, k0 + kb_size - 1)
+            result = None
+            for f, fd, ld in zip(firsts, first_docs, last_docs):
+                one = (k0 <= f + tokens_per_block - 1) & (k0_doc <= ld) & (k1_doc >= fd)
+                result = one if result is None else (result | one)
+            return result
 
         def scores_of(kb):
             k0 = pl.multiple_of(kb * kb_size, kb_size)
@@ -111,10 +121,10 @@
     lax.fori_loop(0, row_blocks, row_block, 0)
 
 
-def attend_kernel(flat_query, flat_grad, key_full, value_full, ends, block_start, heads, kb_size=1024):
+def attend_kernel(flat_query, flat_grad, key_full, value_full, ends, block_start, heads, kb_size=1024, sub=4):
     rows, head_width = flat_query.shape
     keys = key_full.shape[0]
-    rb_size = rows // block_start.shape[0]
+    rb_size = rows // block_start.shape[0] * sub
     vmem = pltpu.VMEM
     smem = pl.BlockSpec(memory_space=pltpu.SMEM)
     whole = pl.BlockSpec(memory_space=pltpu.VMEM)
@@ -122,7 +132,7 @@
     positions = jnp.arange(keys, dtype=jnp.int32)
     key_doc = jnp.sum((positions[:, None] >= ends[None, :]).astype(jnp.int32), axis=1)[None, :]
     return pl.pallas_call(
-        functools.partial(_attend_kernel, heads, kb_size),
+        functools.partial(_attend_kernel, heads, kb_size, sub),
         out_shape=(
             jax.ShapeDtypeStruct((rows, head_width), jnp.bfloat16),
             jax.ShapeDtypeStruct((keys, 2 * head_width), jnp.float32),

time: 141 us -> 131 us (0.929)
  Pallas kernels: 25.6 us -> 16.9 us
    pallas_call x1, Pallas kernels: 25.6 us -> 16.9 us  [attend_kernel(): pl.pallas_call(functools.partial(_attend_kernel, heads, kb_size, sub), ou...]
  transfers between devices with their start and end apart: 3 -> 3, of which waited for: 3 -> 3; matrix products, arithmetic and copies ran while one was open for 0% -> 1% of each run, Pallas kernels for 0% -> 0%
where the time goes in v10:
time: 131 us; the launch traced here: 130 us
  waiting for transfers between devices  80.2 us (61%)
  starting transfers between devices  18 us (14%)
  Pallas kernels  16.9 us (13%)
  local copies, waits for them, and re-layouts  9.85 us (8%)
  other arithmetic  4.59 us (4%)
    all_to_all x1, waiting for transfers between devices, body(): lax.all_to_all(packed, 'cp', split_axis=0, concat_axis=0, tiled=True)  51.6 us
    all_to_all x1, waiting for transfers between devices, body(): lax.all_to_all(terms.astype(jnp.bfloat16).reshape(shards, tokens, 2 * hea...  26.1 us
    pallas_call x1, Pallas kernels, attend_kernel(): pl.pallas_call(functools.partial(_attend_kernel, heads, kb_size, sub), ou...  16.9 us
    all_to_all x1, starting transfers between devices, body(): lax.all_to_all(packed, 'cp', split_axis=0, concat_axis=0, tiled=True)  13 us
    all_to_all x1, starting transfers between devices, body(): lax.all_to_all(terms.astype(jnp.bfloat16).reshape(shards, tokens, 2 * hea...  3.65 us
  transfers between devices with their start and end apart: 3, of which 3 were waited for; matrix products, arithmetic and copies ran while one was open for 1% of the time, Pallas kernels for 0%

profile of v10, /device:TPU:56, one launch (start us, length us, event | category | flops | bytes accessed | tf_op | source)
XLA Modules:
  0.0 130.3 jit_solution(14937132656295553651)
XLA Ops:
  0.6 0.0 copy-start
  0.6 1.1 select_reduce_fusion
  1.8 0.8 reshape_squeeze.14
  2.6 0.8 reshape_squeeze.15
  3.4 0.0 copy-done
  3.4 0.6 gather_fusion.1
  3.9 1.6 %gather_fusion = bf16[16,8,2048]{2,1,0:T(8,128)(2,1)S(1)} fusion(bf16[16,8,2048]{2,1,0:T(8,128)(2,1)} %bitcast.19, s32[1024]{0:T(1024)S(1)} %pad_clamp_fusion), kind=kCustom, calls=%fused_computation.clone | custom fusion | bytes 1048640 | tf_op jit(solution)/shard_map/jit(_take)/gather | solution.py:169
  5.6 0.2 broadcast_select_fusion.1
  5.8 0.1 broadcast_in_dim.33
  5.9 1.6 %pad_maximum_fusion = bf16[16,32,2048]{2,1,0:T(8,128)(2,1)} fusion(bf16[16,16,2048]{2,1,0:T(8,128)(2,1)S(1)} %broadcast_in_dim.33, bf16[16,8,2048]{2,1,0:T(8,128)(2,1)S(1)} %get-tuple-element.17, bf16[16,8,2048]{2,1,0:T(8,128)(2,1)S(1)} %get-tuple-element.16), kind=kLoop, calls=%fused_computation.2 | loop fusion | flops 6291456 | bytes 4194304 | tf_op jit(solution)/shard_map/concatenate | solution.py:173
  7.5 0.0 copy-start.2
  7.5 13.0 %all-to-all-start = ((bf16[16,32,2048]{2,1,0:T(8,128)(2,1)}), bf16[16,32,2048]{2,1,0:T(8,128)(2,1)S(1)}, u32[]{:S(2)}, u32[]{:S(2)}) async-start(bf16[16,32,2048]{2,1,0:T(8,128)(2,1)} %pad_maximum_fusion), calls=%async_computation | async-start | bytes 4194304 | tf_op jit(solution)/shard_map/all_to_all | solution.py:181
  20.5 0.0 copy-done.2
  20.5 0.2 reduce-window.8
  20.7 0.2 multiply_reduce_fusion
  20.9 0.1 convert_reduce_fusion
  21.0 51.6 %all-to-all-done = bf16[16,32,2048]{2,1,0:T(8,128)(2,1)S(1)} async-done(((bf16[16,32,2048]{2,1,0:T(8,128)(2,1)}), bf16[16,32,2048]{2,1,0:T(8,128)(2,1)S(1)}, u32[]{:S(2)}, u32[]{:S(2)}) %all-to-all-start) | async-done | bytes 2097184 | tf_op jit(solution)/shard_map/all_to_all | solution.py:181
  72.6 1.2 fusion
  73.8 0.0 copy-start.1
  73.8 1.3 %reshape.61.v_ref = bf16[2048,128]{1,0:T(8,128)(2,1)S(1)} reshape(bf16[16,8,2048]{2,1,0:T(8,128)(2,1)} %get-tuple-element.10) | data formatting | bytes 1048576 | tf_op jit(solution)/shard_map/reshape | solution.py:186
  75.1 1.3 reshape.60.k_ref
  76.4 0.2 reshape.59.g_ref
  76.7 0.0 copy-done.1
  76.7 0.2 reshape.58.q_ref
  76.9 16.9 %shard_map.85 = (bf16[2048,128]{1,0:T(8,128)(2,1)S(1)}, f32[2048,256]{1,0:T(8,128)S(1)}) custom-call(s32[6]{0:T(128)S(1)} %bitcast.17, s32[16]{0:T(128)S(1)} %multiply_add_fusion.start_ref, s32[1,2048]{1,0:T(1,128)S(1)} %bitcast.15, bf16[2048,128]{1,0:T(8,128)(2,1)S(1)} %reshape.58.q_ref, bf16[2048,128]{1,0:T(8,128)(2,1)S(1)} %reshape.59.g_ref, ...), custom_call_target="tpu_custom_call" | custom-call | flops 1879048192 | bytes 4718592 | tf_op jit(solution)/shard_map/pallas_call | solution.py:134
  93.9 1.1 convert_element_type.13
  95.0 3.7 %all-to-all-start.1 = ((bf16[16,128,256]{2,1,0:T(8,128)(2,1)}), bf16[16,128,256]{2,1,0:T(8,128)(2,1)S(1)}, u32[]{:S(2)}, u32[]{:S(2)}) async-start(bf16[16,128,256]{2,1,0:T(8,128)(2,1)} %bitcast.7), calls=%async_computation.1 | async-start | bytes 2097152 | tf_op jit(solution)/shard_map/all_to_all | solution.py:201
  98.6 0.2 reshape.62
  98.8 1.3 collective-permute-start
  100.1 2.5 %collective-permute-done = bf16[128,2048]{1,0:T(8,128)(2,1)S(1)} collective-permute-done((bf16[128,2048]{1,0:T(8,128)(2,1)S(1)}, bf16[128,2048]{1,0:T(8,128)(2,1)S(1)}, u32[]{:S(2)}, u32[]{:S(2)}) %collective-permute-start) | collective-permute-done | bytes 524320 | tf_op jit(solution)/shard_map/ppermute | solution.py:14
  102.7 26.1 %all-to-all-done.1 = bf16[16,128,256]{2,1,0:T(8,128)(2,1)S(1)} async-done(((bf16[16,128,256]{2,1,0:T(8,128)(2,1)}), bf16[16,128,256]{2,1,0:T(8,128)(2,1)S(1)}, u32[]{:S(2)}, u32[]{:S(2)}) %all-to-all-start.1) | async-done | bytes 1048608 | tf_op jit(solution)/shard_map/all_to_all | solution.py:201
  128.7 0.1 reduce
  128.9 0.6 slice_bitcast_fusion
  129.5 0.8 copy.10
  (4 shorter events, 0.0 us)
Async XLA Ops:
  0.6 2.7 %copy-start = (bf16[1,128,2048]{2,1,0:T(8,128)(2,1)S(1)}, bf16[1,128,2048]{2,1,0:T(8,128)(2,1)}, u32[]{:S(2)}) copy-start(bf16[1,128,2048]{2,1,0:T(8,128)(2,1)} %param.11) | copy-start | bytes 1572868
  7.5 13.0 %copy-start.2 = (s32[6]{0:T(128)S(1)}, s32[6]{0:T(128)}, u32[]{:S(2)}) copy-start(s32[6]{0:T(128)} %param.12) | copy-start | bytes 76
  7.5 65.1 %all-to-all-start = ((bf16[16,32,2048]{2,1,0:T(8,128)(2,1)}), bf16[16,32,2048]{2,1,0:T(8,128)(2,1)S(1)}, u32[]{:S(2)}, u32[]{:S(2)}) async-start(bf16[16,32,2048]{2,1,0:T(8,128)(2,1)} %pad_maximum_fusion), calls=%async_computation | async-start | bytes 4194304 | tf_op jit(solution)/shard_map/all_to_all | solution.py:181
  73.8 2.9 %copy-start.1 = (bf16[16,8,2048]{2,1,0:T(8,128)(2,1)S(1)}, bf16[16,8,2048]{2,1,0:T(8,128)(2,1)}, u32[]{:S(2)}) copy-start(bf16[16,8,2048]{2,1,0:T(8,128)(2,1)} %get-tuple-element.13) | copy-start | bytes 1572868
  95.0 33.8 %all-to-all-start.1 = ((bf16[16,128,256]{2,1,0:T(8,128)(2,1)}), bf16[16,128,256]{2,1,0:T(8,128)(2,1)S(1)}, u32[]{:S(2)}, u32[]{:S(2)}) async-start(bf16[16,128,256]{2,1,0:T(8,128)(2,1)} %bitcast.7), calls=%async_computation.1 | async-start | bytes 2097152 | tf_op jit(solution)/shard_map/all_to_all | solution.py:201
  98.8 3.8 %collective-permute-start = (bf16[128,2048]{1,0:T(8,128)(2,1)S(1)}, bf16[128,2048]{1,0:T(8,128)(2,1)S(1)}, u32[]{:S(2)}, u32[]{:S(2)}) collective-permute-start(bf16[128,2048]{1,0:T(8,128)(2,1)S(1)} %reshape.62), channel_id=1, source_target_pairs={{128,0},{256,128},{384,256},{129,1},{257,129},{385,257},{130,2},{2... | collective-permute-start | bytes 1572872 | tf_op jit(solution)/shard_map/ppermute | solution.py:14

commit v11 on v10

--- a/solution.py
+++ b/solution.py
@@ -168,28 +168,32 @@
         grouped = rows.reshape(shards, block_rows, rows.shape[1])
         return jnp.take(grouped, send_order, axis=0)
 
-    key_rows = tokens * head_width // width
-    own_keys = jnp.concatenate([key[0].reshape(key_rows, width), value[0].reshape(key_rows, width)], axis=0)
+    head_count = width // head_width
+    piece = block_rows * head_count
+
+    def as_heads(rows):
+        return reorder(rows).reshape(shards, piece, head_width)
+
+    own_keys = jnp.concatenate([key[0], value[0]], axis=0)
     packed = jnp.concatenate(
         [
-            reorder(query[0]),
-            reorder(out_grad[0]),
+            as_heads(query[0]),
+            as_heads(out_grad[0]),
             jnp.broadcast_to(own_keys[None], (shards,) + own_keys.shape),
         ],
         axis=1,
     )
     received = lax.all_to_all(packed, "cp", split_axis=0, concat_axis=0, tiled=True)
-    query_sent = received[:, :block_rows]
-    grad_sent = received[:, block_rows : 2 * block_rows]
-    key_at = 2 * block_rows
-    key_full = received[:, key_at : key_at + key_rows].reshape(key_count, head_width)
-    value_full = received[:, key_at + key_rows :].reshape(key_count, head_width)
+    flat_query = received[:, :piece].reshape(shards * piece, head_width)
+    flat_grad = received[:, piece : 2 * piece].reshape(shards * piece, head_width)
+    key_at = 2 * piece
+    key_full = received[:, key_at : key_at + tokens].reshape(key_count, head_width)
+    value_full = received[:, key_at + tokens :].reshape(key_count, head_width)
     ends = jnp.cumsum(lengths).astype(jnp.int32)
     taken = lax.dynamic_index_in_dim(inverse, own_index, 1, keepdims=False)
-    head_count = width // head_width
     dquery, terms = attend_kernel(
-        query_sent.reshape(tokens * head_count, head_width),
-        grad_sent.reshape(tokens * head_count, head_width),
+        flat_query,
+        flat_grad,
         key_full,
         value_full,
         ends,

time: 131 us -> 129 us (0.985)
  local copies, waits for them, and re-layouts: 9.85 us -> 4.88 us
  Pallas kernels: 16.9 us -> 20.5 us
    pallas_call x1, Pallas kernels: 16.9 us -> 20.5 us  [attend_kernel(): pl.pallas_call(functools.partial(_attend_kernel, heads, kb_size, sub), ou...]
    reshape x4 -> x2, local copies, waits for them, and re-layouts: 3.11 us -> 0.48 us  [as_heads(): return reorder(rows).reshape(shards, piece, head_width)]
    another operation x2 -> x0, local copies, waits for them, and re-layouts: 1.56 us -> none  [the longest x1 0.78 us: body(): key[0].reshape(key_rows, width)]
where the time goes in v11:
time: 129 us
  waiting for transfers between devices  80.1 us (62%)
  Pallas kernels  20.5 us (16%)
  starting transfers between devices  18 us (14%)
  local copies, waits for them, and re-layouts  4.88 us (4%)
  other arithmetic  4.49 us (3%)
    all_to_all x1, waiting for transfers between devices, body(): lax.all_to_all(packed, 'cp', split_axis=0, concat_axis=0, tiled=True)  51.6 us
    all_to_all x1, waiting for transfers between devices, body(): lax.all_to_all(terms.astype(jnp.bfloat16).reshape(shards, tokens, 2 * hea...  26.1 us
    pallas_call x1, Pallas kernels, attend_kernel(): pl.pallas_call(functools.partial(_attend_kernel, heads, kb_size, sub), ou...  20.5 us
    all_to_all x1, starting transfers between devices, body(): lax.all_to_all(packed, 'cp', split_axis=0, concat_axis=0, tiled=True)  13 us
    all_to_all x1, starting transfers between devices, body(): lax.all_to_all(terms.astype(jnp.bfloat16).reshape(shards, tokens, 2 * hea...  3.65 us
  transfers between devices with their start and end apart: 3, of which 3 were waited for; matrix products, arithmetic and copies ran while one was open for 1% of the time, Pallas kernels for 0%

profile of v11, /device:TPU:56, one launch (start us, length us, event | category | flops | bytes accessed | tf_op | source)
XLA Modules:
  0.0 128.7 jit_solution(15343460556900073503)
XLA Ops:
  0.6 0.0 copy-start
  0.6 1.1 select_reduce_fusion
  1.8 0.0 copy-done
  1.8 0.6 gather_fusion.1
  2.4 1.6 %gather_fusion = bf16[16,8,2048]{2,1,0:T(8,128)(2,1)S(1)} fusion(bf16[16,8,2048]{2,1,0:T(8,128)(2,1)} %bitcast.29, s32[1024]{0:T(1024)S(1)} %pad_clamp_fusion), kind=kCustom, calls=%fused_computation.clone | custom fusion | bytes 1048640 | tf_op jit(solution)/shard_map/jit(_take)/gather | solution.py:169
  4.0 0.0 copy-start.1
  4.0 0.0 copy-start.2
  4.0 0.2 broadcast_select_fusion.1
  4.2 0.2 reshape.64
  4.5 0.2 reshape.65
  4.7 0.1 copy-done.1
  4.8 0.0 copy-done.2
  4.8 0.2 broadcast_in_dim.33
  5.0 1.5 %pad_maximum_fusion = bf16[16,512,128]{2,1,0:T(8,128)(2,1)} fusion(bf16[16,256,128]{2,1,0:T(8,128)(2,1)S(1)} %broadcast_in_dim.33, bf16[16,128,128]{2,1,0:T(8,128)(2,1)S(1)} %reshape.65, bf16[16,128,128]{2,1,0:T(8,128)(2,1)S(1)} %reshape.64), kind=kLoop, calls=%fused_computation.2 | loop fusion | flops 6291456 | bytes 4194304 | tf_op jit(solution)/shard_map/concatenate | solution.py:178
  6.5 0.0 copy-start.3
  6.5 13.0 %all-to-all-start = ((bf16[16,512,128]{2,1,0:T(8,128)(2,1)}), bf16[16,512,128]{2,1,0:T(8,128)(2,1)S(1)}, u32[]{:S(2)}, u32[]{:S(2)}) async-start(bf16[16,512,128]{2,1,0:T(8,128)(2,1)} %pad_maximum_fusion), calls=%async_computation | async-start | bytes 4194304 | tf_op jit(solution)/shard_map/all_to_all | solution.py:186
  19.5 0.0 copy-done.3
  19.5 0.2 reduce-window.8
  19.7 0.2 multiply_reduce_fusion
  19.9 0.1 convert_reduce_fusion
  20.0 51.6 %all-to-all-done = bf16[16,512,128]{2,1,0:T(8,128)(2,1)S(1)} async-done(((bf16[16,512,128]{2,1,0:T(8,128)(2,1)}), bf16[16,512,128]{2,1,0:T(8,128)(2,1)S(1)}, u32[]{:S(2)}, u32[]{:S(2)}) %all-to-all-start) | async-done | bytes 2097184 | tf_op jit(solution)/shard_map/all_to_all | solution.py:186
  71.6 0.2 fusion
  71.8 20.5 %shard_map.85 = (bf16[2048,128]{1,0:T(8,128)(2,1)S(1)}, f32[2048,256]{1,0:T(8,128)S(1)}) custom-call(s32[6]{0:T(128)S(1)} %bitcast.27, s32[16]{0:T(128)S(1)} %multiply_add_fusion.start_ref, s32[1,2048]{1,0:T(1,128)S(1)} %bitcast.25, bf16[2048,128]{1,0:T(8,128)(2,1)S(1)} %bitcast.24, bf16[2048,128]{1,0:T(8,128)(2,1)S(1)} %bitcast.23, ...), custom_call_target="tpu_custom_call" | custom-call | flops 1879048192 | bytes 4718592 | tf_op jit(solution)/shard_map/pallas_call | solution.py:134
  92.3 1.1 convert_element_type.13
  93.4 3.7 %all-to-all-start.1 = ((bf16[16,128,256]{2,1,0:T(8,128)(2,1)}), bf16[16,128,256]{2,1,0:T(8,128)(2,1)S(1)}, u32[]{:S(2)}, u32[]{:S(2)}) async-start(bf16[16,128,256]{2,1,0:T(8,128)(2,1)} %bitcast.13), calls=%async_computation.1 | async-start | bytes 2097152 | tf_op jit(solution)/shard_map/all_to_all | solution.py:205
  97.1 0.2 reshape.70
  97.3 1.3 %collective-permute-start = (bf16[128,2048]{1,0:T(8,128)(2,1)S(1)}, bf16[128,2048]{1,0:T(8,128)(2,1)S(1)}, u32[]{:S(2)}, u32[]{:S(2)}) collective-permute-start(bf16[128,2048]{1,0:T(8,128)(2,1)S(1)} %reshape.70), channel_id=1, source_target_pairs={{128,0},{256,128},{384,256},{129,1},{257,129},{385,257},{130,2},{2... | collective-permute-start | bytes 1572872 | tf_op jit(solution)/shard_map/ppermute | solution.py:14
  98.6 2.5 %collective-permute-done = bf16[128,2048]{1,0:T(8,128)(2,1)S(1)} collective-permute-done((bf16[128,2048]{1,0:T(8,128)(2,1)S(1)}, bf16[128,2048]{1,0:T(8,128)(2,1)S(1)}, u32[]{:S(2)}, u32[]{:S(2)}) %collective-permute-start) | collective-permute-done | bytes 524320 | tf_op jit(solution)/shard_map/ppermute | solution.py:14
  101.1 26.1 %all-to-all-done.1 = bf16[16,128,256]{2,1,0:T(8,128)(2,1)S(1)} async-done(((bf16[16,128,256]{2,1,0:T(8,128)(2,1)}), bf16[16,128,256]{2,1,0:T(8,128)(2,1)S(1)}, u32[]{:S(2)}, u32[]{:S(2)}) %all-to-all-start.1) | async-done | bytes 1048608 | tf_op jit(solution)/shard_map/all_to_all | solution.py:205
  127.2 0.1 reduce
  127.3 0.6 slice_bitcast_fusion
  127.9 0.8 copy.10
  (4 shorter events, 0.0 us)
Async XLA Ops:
  0.6 1.2 copy-start
  4.0 0.8 copy-start.1
  4.0 0.8 copy-start.2
  6.5 13.0 %copy-start.3 = (s32[6]{0:T(128)S(1)}, s32[6]{0:T(128)}, u32[]{:S(2)}) copy-start(s32[6]{0:T(128)} %param.12) | copy-start | bytes 76
  6.5 65.1 %all-to-all-start = ((bf16[16,512,128]{2,1,0:T(8,128)(2,1)}), bf16[16,512,128]{2,1,0:T(8,128)(2,1)S(1)}, u32[]{:S(2)}, u32[]{:S(2)}) async-start(bf16[16,512,128]{2,1,0:T(8,128)(2,1)} %pad_maximum_fusion), calls=%async_computation | async-start | bytes 4194304 | tf_op jit(solution)/shard_map/all_to_all | solution.py:186
  93.4 33.8 %all-to-all-start.1 = ((bf16[16,128,256]{2,1,0:T(8,128)(2,1)}), bf16[16,128,256]{2,1,0:T(8,128)(2,1)S(1)}, u32[]{:S(2)}, u32[]{:S(2)}) async-start(bf16[16,128,256]{2,1,0:T(8,128)(2,1)} %bitcast.13), calls=%async_computation.1 | async-start | bytes 2097152 | tf_op jit(solution)/shard_map/all_to_all | solution.py:205
  97.3 3.8 %collective-permute-start = (bf16[128,2048]{1,0:T(8,128)(2,1)S(1)}, bf16[128,2048]{1,0:T(8,128)(2,1)S(1)}, u32[]{:S(2)}, u32[]{:S(2)}) collective-permute-start(bf16[128,2048]{1,0:T(8,128)(2,1)S(1)} %reshape.70), channel_id=1, source_target_pairs={{128,0},{256,128},{384,256},{129,1},{257,129},{385,257},{130,2},{2... | collective-permute-start | bytes 1572872 | tf_op jit(solution)/shard_map/ppermute | solution.py:14

commit v12 on v11

--- a/solution.py
+++ b/solution.py
@@ -21,7 +21,7 @@
     return doc
 
 
-def _attend_kernel(heads, kb_size, sub, ends_ref, start_ref, kdoc_ref, q_ref, g_ref, k_ref, v_ref, dq_ref, dkv_ref, top_ref, total_ref, weighted_ref, dq_acc):
+def _attend_kernel(heads, kb_size, sub, ends_ref, start_ref, kdoc_ref, q_ref, g_ref, k_ref, v_ref, dq_ref, dkv_ref, top_ref, total_ref, weighted_ref, dq_acc, s_keep, dp_keep):
     rows, head_width = q_ref.shape
     keys = k_ref.shape[0]
     piece = rows // start_ref.shape[0]
@@ -85,6 +85,8 @@
             @pl.when(seen(kb))
             def _():
                 _, _, s, dp = scores_of(kb)
+                s_keep[kb] = s
+                dp_keep[kb] = dp
                 top = top_ref[...]
                 new_top = jnp.maximum(top, jnp.max(s, axis=1, keepdims=True))
                 expo = jnp.exp(s - new_top)
@@ -103,7 +105,10 @@
         def second_pass(kb, c):
             @pl.when(seen(kb))
             def _():
-                k0, k, s, dp = scores_of(kb)
+                k0 = pl.multiple_of(kb * kb_size, kb_size)
+                k = k_ref[pl.ds(k0, kb_size), :]
+                s = s_keep[kb]
+                dp = dp_keep[kb]
                 probs = jnp.exp(s - top) * inverse_total
                 probs_low = probs.astype(jnp.bfloat16)
                 dscore = (probs * (dp - delta) * scale).astype(jnp.bfloat16)
@@ -144,6 +149,8 @@
             vmem((rb_size, 1), jnp.float32),
             vmem((rb_size, 1), jnp.float32),
             vmem((rb_size, head_width), jnp.float32),
+            vmem((keys // kb_size, rb_size, kb_size), jnp.float32),
+            vmem((keys // kb_size, rb_size, kb_size), jnp.float32),
         ],
         compiler_params=pltpu.CompilerParams(vmem_limit_bytes=48 * 1024 * 1024),
         cost_estimate=pl.CostEstimate(flops=flops // 4, transcendentals=rows * keys // 2, bytes_accessed=rows * head_width * 6 + keys * head_width * 4 + keys * head_width * 8),

time: 129 us -> 124 us (0.961); the launches traced: 129 us -> 126 us
  Pallas kernels: 20.5 us -> 17.3 us
    pallas_call x1, Pallas kernels: 20.5 us -> 17.3 us  [attend_kernel(): pl.pallas_call(functools.partial(_attend_kernel, heads, kb_size, sub), ou...]
where the time goes in v12:
time: 124 us; the launch traced here: 126 us
  waiting for transfers between devices  80.2 us (65%)
  starting transfers between devices  18 us (15%)
  Pallas kernels  17.3 us (14%)
  local copies, waits for them, and re-layouts  4.88 us (4%)
  other arithmetic  4.49 us (4%)
    all_to_all x1, waiting for transfers between devices, body(): lax.all_to_all(packed, 'cp', split_axis=0, concat_axis=0, tiled=True)  51.6 us
    all_to_all x1, waiting for transfers between devices, body(): lax.all_to_all(terms.astype(jnp.bfloat16).reshape(shards, tokens, 2 * hea...  26.1 us
    pallas_call x1, Pallas kernels, attend_kernel(): pl.pallas_call(functools.partial(_attend_kernel, heads, kb_size, sub), ou...  17.3 us
    all_to_all x1, starting transfers between devices, body(): lax.all_to_all(packed, 'cp', split_axis=0, concat_axis=0, tiled=True)  13 us
    all_to_all x1, starting transfers between devices, body(): lax.all_to_all(terms.astype(jnp.bfloat16).reshape(shards, tokens, 2 * hea...  3.65 us
    ppermute x1, waiting for transfers between devices, passed_along(): return lax.ppermute(array, axis, pairs)  2.5 us
  transfers between devices with their start and end apart: 3, of which 3 were waited for; matrix products, arithmetic and copies ran while one was open for 1% of the time, Pallas kernels for 0%

profile of v12, /device:TPU:56, one launch (start us, length us, event | category | flops | bytes accessed | tf_op | source)
XLA Modules:
  0.0 125.5 jit_solution(5263264303983623057)
XLA Ops:
  0.6 0.0 copy-start
  0.6 1.1 select_reduce_fusion
  1.8 0.0 copy-done
  1.8 0.6 gather_fusion.1
  2.4 1.6 %gather_fusion = bf16[16,8,2048]{2,1,0:T(8,128)(2,1)S(1)} fusion(bf16[16,8,2048]{2,1,0:T(8,128)(2,1)} %bitcast.29, s32[1024]{0:T(1024)S(1)} %pad_clamp_fusion), kind=kCustom, calls=%fused_computation.clone | custom fusion | bytes 1048640 | tf_op jit(solution)/shard_map/jit(_take)/gather | solution.py:176
  4.0 0.0 copy-start.1
  4.0 0.0 copy-start.2
  4.0 0.2 broadcast_select_fusion.1
  4.2 0.2 reshape.64
  4.5 0.2 reshape.65
  4.7 0.1 copy-done.1
  4.8 0.0 copy-done.2
  4.8 0.2 broadcast_in_dim.33
  5.0 1.5 %pad_maximum_fusion = bf16[16,512,128]{2,1,0:T(8,128)(2,1)} fusion(bf16[16,256,128]{2,1,0:T(8,128)(2,1)S(1)} %broadcast_in_dim.33, bf16[16,128,128]{2,1,0:T(8,128)(2,1)S(1)} %reshape.65, bf16[16,128,128]{2,1,0:T(8,128)(2,1)S(1)} %reshape.64), kind=kLoop, calls=%fused_computation.2 | loop fusion | flops 6291456 | bytes 4194304 | tf_op jit(solution)/shard_map/concatenate | solution.py:185
  6.5 0.0 copy-start.3
  6.5 13.0 %all-to-all-start = ((bf16[16,512,128]{2,1,0:T(8,128)(2,1)}), bf16[16,512,128]{2,1,0:T(8,128)(2,1)S(1)}, u32[]{:S(2)}, u32[]{:S(2)}) async-start(bf16[16,512,128]{2,1,0:T(8,128)(2,1)} %pad_maximum_fusion), calls=%async_computation | async-start | bytes 4194304 | tf_op jit(solution)/shard_map/all_to_all | solution.py:193
  19.5 0.0 copy-done.3
  19.5 0.2 reduce-window.8
  19.7 0.2 multiply_reduce_fusion
  19.9 0.1 convert_reduce_fusion
  20.0 51.6 %all-to-all-done = bf16[16,512,128]{2,1,0:T(8,128)(2,1)S(1)} async-done(((bf16[16,512,128]{2,1,0:T(8,128)(2,1)}), bf16[16,512,128]{2,1,0:T(8,128)(2,1)S(1)}, u32[]{:S(2)}, u32[]{:S(2)}) %all-to-all-start) | async-done | bytes 2097184 | tf_op jit(solution)/shard_map/all_to_all | solution.py:193
  71.6 0.2 fusion
  71.8 17.3 %shard_map.85 = (bf16[2048,128]{1,0:T(8,128)(2,1)S(1)}, f32[2048,256]{1,0:T(8,128)S(1)}) custom-call(s32[6]{0:T(128)S(1)} %bitcast.27, s32[16]{0:T(128)S(1)} %multiply_add_fusion.start_ref, s32[1,2048]{1,0:T(1,128)S(1)} %bitcast.25, bf16[2048,128]{1,0:T(8,128)(2,1)S(1)} %bitcast.24, bf16[2048,128]{1,0:T(8,128)(2,1)S(1)} %bitcast.23, ...), custom_call_target="tpu_custom_call" | custom-call | flops 1879048192 | bytes 4718592 | tf_op jit(solution)/shard_map/pallas_call | solution.py:139
  89.1 1.1 convert_element_type.13
  90.2 3.7 %all-to-all-start.1 = ((bf16[16,128,256]{2,1,0:T(8,128)(2,1)}), bf16[16,128,256]{2,1,0:T(8,128)(2,1)S(1)}, u32[]{:S(2)}, u32[]{:S(2)}) async-start(bf16[16,128,256]{2,1,0:T(8,128)(2,1)} %bitcast.13), calls=%async_computation.1 | async-start | bytes 2097152 | tf_op jit(solution)/shard_map/all_to_all | solution.py:212
  93.9 0.2 reshape.70
  94.1 1.3 %collective-permute-start = (bf16[128,2048]{1,0:T(8,128)(2,1)S(1)}, bf16[128,2048]{1,0:T(8,128)(2,1)S(1)}, u32[]{:S(2)}, u32[]{:S(2)}) collective-permute-start(bf16[128,2048]{1,0:T(8,128)(2,1)S(1)} %reshape.70), channel_id=1, source_target_pairs={{128,0},{256,128},{384,256},{129,1},{257,129},{385,257},{130,2},{2... | collective-permute-start | bytes 1572872 | tf_op jit(solution)/shard_map/ppermute | solution.py:14
  95.4 2.5 %collective-permute-done = bf16[128,2048]{1,0:T(8,128)(2,1)S(1)} collective-permute-done((bf16[128,2048]{1,0:T(8,128)(2,1)S(1)}, bf16[128,2048]{1,0:T(8,128)(2,1)S(1)}, u32[]{:S(2)}, u32[]{:S(2)}) %collective-permute-start) | collective-permute-done | bytes 524320 | tf_op jit(solution)/shard_map/ppermute | solution.py:14
  97.9 26.1 %all-to-all-done.1 = bf16[16,128,256]{2,1,0:T(8,128)(2,1)S(1)} async-done(((bf16[16,128,256]{2,1,0:T(8,128)(2,1)}), bf16[16,128,256]{2,1,0:T(8,128)(2,1)S(1)}, u32[]{:S(2)}, u32[]{:S(2)}) %all-to-all-start.1) | async-done | bytes 1048608 | tf_op jit(solution)/shard_map/all_to_all | solution.py:212
  124.0 0.1 reduce
  124.1 0.6 slice_bitcast_fusion
  124.8 0.8 copy.10
  (4 shorter events, 0.0 us)
Async XLA Ops:
  0.6 1.2 copy-start
  4.0 0.8 copy-start.1
  4.0 0.8 copy-start.2
  6.5 13.0 %copy-start.3 = (s32[6]{0:T(128)S(1)}, s32[6]{0:T(128)}, u32[]{:S(2)}) copy-start(s32[6]{0:T(128)} %param.12) | copy-start | bytes 76
  6.5 65.1 %all-to-all-start = ((bf16[16,512,128]{2,1,0:T(8,128)(2,1)}), bf16[16,512,128]{2,1,0:T(8,128)(2,1)S(1)}, u32[]{:S(2)}, u32[]{:S(2)}) async-start(bf16[16,512,128]{2,1,0:T(8,128)(2,1)} %pad_maximum_fusion), calls=%async_computation | async-start | bytes 4194304 | tf_op jit(solution)/shard_map/all_to_all | solution.py:193
  90.2 33.8 %all-to-all-start.1 = ((bf16[16,128,256]{2,1,0:T(8,128)(2,1)}), bf16[16,128,256]{2,1,0:T(8,128)(2,1)S(1)}, u32[]{:S(2)}, u32[]{:S(2)}) async-start(bf16[16,128,256]{2,1,0:T(8,128)(2,1)} %bitcast.13), calls=%async_computation.1 | async-start | bytes 2097152 | tf_op jit(solution)/shard_map/all_to_all | solution.py:212
  94.1 3.8 %collective-permute-start = (bf16[128,2048]{1,0:T(8,128)(2,1)S(1)}, bf16[128,2048]{1,0:T(8,128)(2,1)S(1)}, u32[]{:S(2)}, u32[]{:S(2)}) collective-permute-start(bf16[128,2048]{1,0:T(8,128)(2,1)S(1)} %reshape.70), channel_id=1, source_target_pairs={{128,0},{256,128},{384,256},{129,1},{257,129},{385,257},{130,2},{2... | collective-permute-start | bytes 1572872 | tf_op jit(solution)/shard_map/ppermute | solution.py:14

commit v13 on v12

--- a/solution.py
+++ b/solution.py
@@ -21,7 +21,7 @@
     return doc
 
 
-def _attend_kernel(heads, kb_size, sub, ends_ref, start_ref, kdoc_ref, q_ref, g_ref, k_ref, v_ref, dq_ref, dkv_ref, top_ref, total_ref, weighted_ref, dq_acc, s_keep, dp_keep):
+def _attend_kernel(heads, kb_size, sub, ends_ref, start_ref, kdoc_ref, q_ref, g_ref, k_ref, v_ref, dq_ref, dkv_ref, top_ref, total_ref, weighted_ref, dq_acc, s_keep, dp_keep, m_keep, dkv_acc):
     rows, head_width = q_ref.shape
     keys = k_ref.shape[0]
     piece = rows // start_ref.shape[0]
@@ -30,7 +30,7 @@
     key_blocks = keys // kb_size
     tokens_per_block = piece // heads
     scale = head_width ** (-0.5)
-    dkv_ref[...] = jnp.zeros_like(dkv_ref)
+    dkv_acc[...] = jnp.zeros_like(dkv_acc)
     row_raw = lax.broadcasted_iota(jnp.int32, (rb_size, kb_size), 0)
     row_iota = (row_raw % piece) // heads
     row_part = row_raw // piece
@@ -85,11 +85,12 @@
             @pl.when(seen(kb))
             def _():
                 _, _, s, dp = scores_of(kb)
-                s_keep[kb] = s
                 dp_keep[kb] = dp
                 top = top_ref[...]
                 new_top = jnp.maximum(top, jnp.max(s, axis=1, keepdims=True))
                 expo = jnp.exp(s - new_top)
+                s_keep[kb] = expo
+                m_keep[kb] = new_top
                 shrink = jnp.exp(top - new_top)
                 total_ref[...] = total_ref[...] * shrink + jnp.sum(expo, axis=1, keepdims=True)
                 weighted_ref[...] = weighted_ref[...] * shrink + jnp.sum(expo * dp, axis=1, keepdims=True)
@@ -107,15 +108,14 @@
             def _():
                 k0 = pl.multiple_of(kb * kb_size, kb_size)
                 k = k_ref[pl.ds(k0, kb_size), :]
-                s = s_keep[kb]
                 dp = dp_keep[kb]
-                probs = jnp.exp(s - top) * inverse_total
+                probs = s_keep[kb] * (jnp.exp(m_keep[kb] - top) * inverse_total)
                 probs_low = probs.astype(jnp.bfloat16)
                 dscore = (probs * (dp - delta) * scale).astype(jnp.bfloat16)
                 dv = lax.dot_general(probs_low, g, (((0,), (0,)), ((), ())), preferred_element_type=jnp.float32)
                 dk = lax.dot_general(dscore, q, (((0,), (0,)), ((), ())), preferred_element_type=jnp.float32)
-                dkv_ref[pl.ds(k0, kb_size), pl.ds(0, head_width)] += dk
-                dkv_ref[pl.ds(k0, kb_size), pl.ds(head_width, head_width)] += dv
+                dkv_acc[pl.ds(k0, kb_size), pl.ds(0, head_width)] += dk
+                dkv_acc[pl.ds(k0, kb_size), pl.ds(head_width, head_width)] += dv
                 dq_acc[...] += jnp.dot(dscore, k, preferred_element_type=jnp.float32)
             return c
 
@@ -124,6 +124,7 @@
         return carry
 
     lax.fori_loop(0, row_blocks, row_block, 0)
+    dkv_ref[...] = dkv_acc[...].astype(dkv_ref.dtype)
 
 
 def attend_kernel(flat_query, flat_grad, key_full, value_full, ends, block_start, heads, kb_size=1024, sub=4):
@@ -140,7 +141,7 @@
         functools.partial(_attend_kernel, heads, kb_size, sub),
         out_shape=(
             jax.ShapeDtypeStruct((rows, head_width), jnp.bfloat16),
-            jax.ShapeDtypeStruct((keys, 2 * head_width), jnp.float32),
+            jax.ShapeDtypeStruct((keys, 2 * head_width), jnp.bfloat16),
         ),
         in_specs=[smem, smem, whole, whole, whole, whole, whole],
         out_specs=(whole, whole),
@@ -151,6 +152,8 @@
             vmem((rb_size, head_width), jnp.float32),
             vmem((keys // kb_size, rb_size, kb_size), jnp.float32),
             vmem((keys // kb_size, rb_size, kb_size), jnp.float32),
+            vmem((keys // kb_size, rb_size, 1), jnp.float32),
+            vmem((keys, 2 * head_width), jnp.float32),
         ],
         compiler_params=pltpu.CompilerParams(vmem_limit_bytes=48 * 1024 * 1024),
         cost_estimate=pl.CostEstimate(flops=flops // 4, transcendentals=rows * keys // 2, bytes_accessed=rows * head_width * 6 + keys * head_width * 4 + keys * head_width * 8),
@@ -166,10 +169,9 @@
     block_rows = tokens // shards
     key_count = shards * tokens
     iota = jnp.arange(shards, dtype=jnp.int32)
-    inverse = jnp.sum(
-        (plan[:, None, :] == iota[None, :, None]).astype(jnp.int32) * iota[None, None, :], axis=2
-    )
-    send_order = lax.dynamic_index_in_dim(inverse, own_index, 0, keepdims=False)
+    own_plan = lax.dynamic_index_in_dim(plan, own_index, 0, keepdims=False)
+    send_order = jnp.sum((own_plan[None, :] == iota[:, None]).astype(jnp.int32) * iota[None, :], axis=1)
+    taken = jnp.sum((plan == own_index).astype(jnp.int32) * iota[None, :], axis=1)
 
     def reorder(rows):
         grouped = rows.reshape(shards, block_rows, rows.shape[1])
@@ -197,7 +199,6 @@
     key_full = received[:, key_at : key_at + tokens].reshape(key_count, head_width)
     value_full = received[:, key_at + tokens :].reshape(key_count, head_width)
     ends = jnp.cumsum(lengths).astype(jnp.int32)
-    taken = lax.dynamic_index_in_dim(inverse, own_index, 1, keepdims=False)
     dquery, terms = attend_kernel(
         flat_query,
         flat_grad,
@@ -210,7 +211,7 @@
     dquery = dquery.reshape(tokens, width)
     handed = passed_along(dquery, "pp", -1)
     partials = lax.all_to_all(
-        terms.astype(jnp.bfloat16).reshape(shards, tokens, 2 * head_width), "cp", split_axis=0, concat_axis=0, tiled=True
+        terms.reshape(shards, tokens, 2 * head_width), "cp", split_axis=0, concat_axis=0, tiled=True
     )
     summed = jnp.sum(partials.astype(jnp.float32), axis=0)
     key_grad = summed[:, :head_width].astype(jnp.bfloat16)

time: 124 us -> 123 us (level); the launches traced: 126 us -> 122 us
  other arithmetic: 4.49 us -> 2.34 us
  Pallas kernels: 17.3 us -> 15.2 us
    pallas_call x1, Pallas kernels: 17.3 us -> 15.2 us  [attend_kernel(): pl.pallas_call(functools.partial(_attend_kernel, heads, kb_size, sub), ou...]
where the time goes in v13:
time: 123 us; the launch traced here: 122 us
  waiting for transfers between devices  80.2 us (65%)
  starting transfers between devices  18 us (15%)
  Pallas kernels  15.2 us (12%)
  local copies, waits for them, and re-layouts  5.77 us (5%)
  other arithmetic  2.34 us (2%)
    all_to_all x1, waiting for transfers between devices, body(): lax.all_to_all(packed, 'cp', split_axis=0, concat_axis=0, tiled=True)  51.6 us
    all_to_all x1, waiting for transfers between devices, body(): lax.all_to_all(terms.reshape(shards, tokens, 2 * head_width), 'cp', split...  26.1 us
    pallas_call x1, Pallas kernels, attend_kernel(): pl.pallas_call(functools.partial(_attend_kernel, heads, kb_size, sub), ou...  15.2 us
    all_to_all x1, starting transfers between devices, body(): lax.all_to_all(packed, 'cp', split_axis=0, concat_axis=0, tiled=True)  13 us
    all_to_all x1, starting transfers between devices, body(): lax.all_to_all(terms.reshape(shards, tokens, 2 * head_width), 'cp', split...  3.65 us
    ppermute x1, waiting for transfers between devices, passed_along(): return lax.ppermute(array, axis, pairs)  2.5 us
  transfers between devices with their start and end apart: 3, of which 3 were waited for; matrix products, arithmetic and copies ran while one was open for 1% of the time, Pallas kernels for 0%

profile of v13, /device:TPU:56, one launch (start us, length us, event | category | flops | bytes accessed | tf_op | source)
XLA Modules:
  0.0 122.3 jit_solution(8088146152984571401)
XLA Ops:
  0.6 0.0 copy-start
  0.6 0.8 dynamic-slice_bitcast_fusion
  1.4 0.1 select_reduce_fusion
  1.6 0.1 copy-done
  1.7 0.6 gather_fusion
  2.3 1.6 %gather_fusion.1 = bf16[16,8,2048]{2,1,0:T(8,128)(2,1)S(1)} fusion(bf16[16,8,2048]{2,1,0:T(8,128)(2,1)} %bitcast.28, s32[1024]{0:T(1024)S(1)} %pad_clamp_fusion), kind=kCustom, calls=%fused_computation.1.clone | custom fusion | bytes 1048640 | tf_op jit(solution)/shard_map/jit(_take)/gather | solution.py:178
  3.9 0.0 copy-start.1
  3.9 0.0 copy-start.2
  3.9 0.2 broadcast_select_fusion.1
  4.1 0.2 reshape.61
  4.4 0.2 reshape.62
  4.6 0.1 copy-done.1
  4.7 0.0 copy-done.2
  4.7 0.2 broadcast_in_dim.34
  4.9 1.5 %pad_maximum_fusion = bf16[16,512,128]{2,1,0:T(8,128)(2,1)} fusion(bf16[16,256,128]{2,1,0:T(8,128)(2,1)S(1)} %broadcast_in_dim.34, bf16[16,128,128]{2,1,0:T(8,128)(2,1)S(1)} %reshape.62, bf16[16,128,128]{2,1,0:T(8,128)(2,1)S(1)} %reshape.61), kind=kLoop, calls=%fused_computation.2 | loop fusion | flops 6291456 | bytes 4194304 | tf_op jit(solution)/shard_map/concatenate | solution.py:187
  6.4 0.0 copy-start.4
  6.4 0.0 copy-start.3
  6.4 13.0 %all-to-all-start = ((bf16[16,512,128]{2,1,0:T(8,128)(2,1)}), bf16[16,512,128]{2,1,0:T(8,128)(2,1)S(1)}, u32[]{:S(2)}, u32[]{:S(2)}) async-start(bf16[16,512,128]{2,1,0:T(8,128)(2,1)} %pad_maximum_fusion), calls=%async_computation | async-start | bytes 4194304 | tf_op jit(solution)/shard_map/all_to_all | solution.py:195
  19.4 0.0 copy-done.4
  19.4 0.2 reduce-window.8
  19.6 0.0 copy-done.3
  19.6 0.1 select_reduce_fusion.1
  19.7 0.1 convert_reduce_fusion
  19.8 51.6 %all-to-all-done = bf16[16,512,128]{2,1,0:T(8,128)(2,1)S(1)} async-done(((bf16[16,512,128]{2,1,0:T(8,128)(2,1)}), bf16[16,512,128]{2,1,0:T(8,128)(2,1)S(1)}, u32[]{:S(2)}, u32[]{:S(2)}) %all-to-all-start) | async-done | bytes 2097184 | tf_op jit(solution)/shard_map/all_to_all | solution.py:195
  71.5 0.2 fusion
  71.7 15.2 %shard_map.85 = (bf16[2048,128]{1,0:T(8,128)(2,1)S(1)}, bf16[2048,256]{1,0:T(8,128)(2,1)}) custom-call(s32[6]{0:T(128)S(1)} %bitcast.26, s32[16]{0:T(128)S(1)} %multiply_add_fusion.start_ref, s32[1,2048]{1,0:T(1,128)S(1)} %bitcast.24, bf16[2048,128]{1,0:T(8,128)(2,1)S(1)} %bitcast.23, bf16[2048,128]{1,0:T(8,128)(2,1)S(1)} %bitcast.22, ...), custom_call_target="tpu_custom_call" | custom-call | flops 1879048192 | bytes 4718592 | tf_op jit(solution)/shard_map/pallas_call | solution.py:140
  87.0 3.7 %all-to-all-start.1 = ((bf16[16,128,256]{2,1,0:T(8,128)(2,1)}), bf16[16,128,256]{2,1,0:T(8,128)(2,1)S(1)}, u32[]{:S(2)}, u32[]{:S(2)}) async-start(bf16[16,128,256]{2,1,0:T(8,128)(2,1)} %bitcast.13), calls=%async_computation.1 | async-start | bytes 2097152 | tf_op jit(solution)/shard_map/all_to_all | solution.py:213
  90.6 0.2 reshape.67
  90.9 1.3 %collective-permute-start = (bf16[128,2048]{1,0:T(8,128)(2,1)S(1)}, bf16[128,2048]{1,0:T(8,128)(2,1)S(1)}, u32[]{:S(2)}, u32[]{:S(2)}) collective-permute-start(bf16[128,2048]{1,0:T(8,128)(2,1)S(1)} %reshape.67), channel_id=1, source_target_pairs={{128,0},{256,128},{384,256},{129,1},{257,129},{385,257},{130,2},{2... | collective-permute-start | bytes 1572872 | tf_op jit(solution)/shard_map/ppermute | solution.py:14
  92.2 2.5 %collective-permute-done = bf16[128,2048]{1,0:T(8,128)(2,1)S(1)} collective-permute-done((bf16[128,2048]{1,0:T(8,128)(2,1)S(1)}, bf16[128,2048]{1,0:T(8,128)(2,1)S(1)}, u32[]{:S(2)}, u32[]{:S(2)}) %collective-permute-start) | collective-permute-done | bytes 524320 | tf_op jit(solution)/shard_map/ppermute | solution.py:14
  94.7 26.1 %all-to-all-done.1 = bf16[16,128,256]{2,1,0:T(8,128)(2,1)S(1)} async-done(((bf16[16,128,256]{2,1,0:T(8,128)(2,1)}), bf16[16,128,256]{2,1,0:T(8,128)(2,1)S(1)}, u32[]{:S(2)}, u32[]{:S(2)}) %all-to-all-start.1) | async-done | bytes 1048608 | tf_op jit(solution)/shard_map/all_to_all | solution.py:213
  120.7 0.1 reduce
  120.9 0.6 slice_bitcast_fusion
  121.5 0.8 copy.10
  (5 shorter events, 0.0 us)
Async XLA Ops:
  0.6 1.1 copy-start
  3.9 0.8 copy-start.1
  3.9 0.8 copy-start.2
  6.4 13.0 %copy-start.4 = (s32[6]{0:T(128)S(1)}, s32[6]{0:T(128)}, u32[]{:S(2)}) copy-start(s32[6]{0:T(128)} %param.12) | copy-start | bytes 76
  6.4 13.2 %copy-start.3 = (s32[16,16]{1,0:T(8,128)S(1)}, s32[16,16]{1,0:T(8,128)}, u32[]{:S(2)}) copy-start(s32[16,16]{1,0:T(8,128)} %param.13) | copy-start | bytes 3076
  6.4 65.1 %all-to-all-start = ((bf16[16,512,128]{2,1,0:T(8,128)(2,1)}), bf16[16,512,128]{2,1,0:T(8,128)(2,1)S(1)}, u32[]{:S(2)}, u32[]{:S(2)}) async-start(bf16[16,512,128]{2,1,0:T(8,128)(2,1)} %pad_maximum_fusion), calls=%async_computation | async-start | bytes 4194304 | tf_op jit(solution)/shard_map/all_to_all | solution.py:195
  87.0 33.8 %all-to-all-start.1 = ((bf16[16,128,256]{2,1,0:T(8,128)(2,1)}), bf16[16,128,256]{2,1,0:T(8,128)(2,1)S(1)}, u32[]{:S(2)}, u32[]{:S(2)}) async-start(bf16[16,128,256]{2,1,0:T(8,128)(2,1)} %bitcast.13), calls=%async_computation.1 | async-start | bytes 2097152 | tf_op jit(solution)/shard_map/all_to_all | solution.py:213
  90.9 3.8 %collective-permute-start = (bf16[128,2048]{1,0:T(8,128)(2,1)S(1)}, bf16[128,2048]{1,0:T(8,128)(2,1)S(1)}, u32[]{:S(2)}, u32[]{:S(2)}) collective-permute-start(bf16[128,2048]{1,0:T(8,128)(2,1)S(1)} %reshape.67), channel_id=1, source_target_pairs={{128,0},{256,128},{384,256},{129,1},{257,129},{385,257},{130,2},{2... | collective-permute-start | bytes 1572872 | tf_op jit(solution)/shard_map/ppermute | solution.py:14

commit v14 on v12

--- a/solution.py
+++ b/solution.py
@@ -21,7 +21,7 @@
     return doc
 
 
-def _attend_kernel(heads, kb_size, sub, ends_ref, start_ref, kdoc_ref, q_ref, g_ref, k_ref, v_ref, dq_ref, dkv_ref, top_ref, total_ref, weighted_ref, dq_acc, s_keep, dp_keep):
+def _attend_kernel(heads, kb_size, sub, ends_ref, start_ref, kdoc_ref, q_ref, g_ref, k_ref, v_ref, dq_ref, dkv_ref, top_ref, total_ref, weighted_ref, dq_acc, s_keep, dp_keep, dkv_acc):
     rows, head_width = q_ref.shape
     keys = k_ref.shape[0]
     piece = rows // start_ref.shape[0]
@@ -30,7 +30,7 @@
     key_blocks = keys // kb_size
     tokens_per_block = piece // heads
     scale = head_width ** (-0.5)
-    dkv_ref[...] = jnp.zeros_like(dkv_ref)
+    dkv_acc[...] = jnp.zeros_like(dkv_acc)
     row_raw = lax.broadcasted_iota(jnp.int32, (rb_size, kb_size), 0)
     row_iota = (row_raw % piece) // heads
     row_part = row_raw // piece
@@ -114,8 +114,8 @@
                 dscore = (probs * (dp - delta) * scale).astype(jnp.bfloat16)
                 dv = lax.dot_general(probs_low, g, (((0,), (0,)), ((), ())), preferred_element_type=jnp.float32)
                 dk = lax.dot_general(dscore, q, (((0,), (0,)), ((), ())), preferred_element_type=jnp.float32)
-                dkv_ref[pl.ds(k0, kb_size), pl.ds(0, head_width)] += dk
-                dkv_ref[pl.ds(k0, kb_size), pl.ds(head_width, head_width)] += dv
+                dkv_acc[pl.ds(k0, kb_size), pl.ds(0, head_width)] += dk
+                dkv_acc[pl.ds(k0, kb_size), pl.ds(head_width, head_width)] += dv
                 dq_acc[...] += jnp.dot(dscore, k, preferred_element_type=jnp.float32)
             return c
 
@@ -124,6 +124,7 @@
         return carry
 
     lax.fori_loop(0, row_blocks, row_block, 0)
+    dkv_ref[...] = dkv_acc[...].astype(dkv_ref.dtype)
 
 
 def attend_kernel(flat_query, flat_grad, key_full, value_full, ends, block_start, heads, kb_size=1024, sub=4):
@@ -140,7 +141,7 @@
         functools.partial(_attend_kernel, heads, kb_size, sub),
         out_shape=(
             jax.ShapeDtypeStruct((rows, head_width), jnp.bfloat16),
-            jax.ShapeDtypeStruct((keys, 2 * head_width), jnp.float32),
+            jax.ShapeDtypeStruct((keys, 2 * head_width), jnp.bfloat16),
         ),
         in_specs=[smem, smem, whole, whole, whole, whole, whole],
         out_specs=(whole, whole),
@@ -151,6 +152,7 @@
             vmem((rb_size, head_width), jnp.float32),
             vmem((keys // kb_size, rb_size, kb_size), jnp.float32),
             vmem((keys // kb_size, rb_size, kb_size), jnp.float32),
+            vmem((keys, 2 * head_width), jnp.float32),
         ],
         compiler_params=pltpu.CompilerParams(vmem_limit_bytes=48 * 1024 * 1024),
         cost_estimate=pl.CostEstimate(flops=flops // 4, transcendentals=rows * keys // 2, bytes_accessed=rows * head_width * 6 + keys * head_width * 4 + keys * head_width * 8),
@@ -207,15 +209,13 @@
         iota * tokens + taken * block_rows,
         head_count,
     )
-    dquery = dquery.reshape(tokens, width)
-    handed = passed_along(dquery, "pp", -1)
+    handed = passed_along(dquery.reshape(1, tokens, width), "pp", -1)
     partials = lax.all_to_all(
-        terms.astype(jnp.bfloat16).reshape(shards, tokens, 2 * head_width), "cp", split_axis=0, concat_axis=0, tiled=True
-    )
-    summed = jnp.sum(partials.astype(jnp.float32), axis=0)
-    key_grad = summed[:, :head_width].astype(jnp.bfloat16)
-    value_grad = summed[:, head_width:].astype(jnp.bfloat16)
-    return (handed[None], key_grad[None], value_grad[None])
+        terms.reshape(shards, tokens, 2 * head_width), "cp", split_axis=0, concat_axis=0, tiled=True
+    )
+    key_grad = jnp.sum(partials[:, :, :head_width].astype(jnp.float32), axis=0).astype(jnp.bfloat16)
+    value_grad = jnp.sum(partials[:, :, head_width:].astype(jnp.float32), axis=0).astype(jnp.bfloat16)
+    return (handed, key_grad[None], value_grad[None])
 
 
 def solution(mesh):

time: 124 us -> 126 us (1.016); the launches traced: 126 us -> 126 us
  no operation moved by 1% of the time
where the time goes in v14:
time: 126 us
  waiting for transfers between devices  80.2 us (64%)
  Pallas kernels  18.3 us (15%)
  starting transfers between devices  18 us (14%)
  local copies, waits for them, and re-layouts  4.24 us (3%)
  other arithmetic  4.01 us (3%)
    all_to_all x1, waiting for transfers between devices, body(): lax.all_to_all(packed, 'cp', split_axis=0, concat_axis=0, tiled=True)  51.6 us
    all_to_all x1, waiting for transfers between devices, body(): lax.all_to_all(terms.reshape(shards, tokens, 2 * head_width), 'cp', split...  26.1 us
    pallas_call x1, Pallas kernels, attend_kernel(): pl.pallas_call(functools.partial(_attend_kernel, heads, kb_size, sub), ou...  18.3 us
    all_to_all x1, starting transfers between devices, body(): lax.all_to_all(packed, 'cp', split_axis=0, concat_axis=0, tiled=True)  13 us
    all_to_all x1, starting transfers between devices, body(): lax.all_to_all(terms.reshape(shards, tokens, 2 * head_width), 'cp', split...  3.65 us
  transfers between devices with their start and end apart: 3, of which 3 were waited for; matrix products, arithmetic and copies ran while one was open for 1% of the time, Pallas kernels for 0%

profile of v14, /device:TPU:56, one launch (start us, length us, event | category | flops | bytes accessed | tf_op | source)
XLA Modules:
  0.0 125.5 jit_solution(9839910586067429212)
XLA Ops:
  0.6 0.0 copy-start
  0.6 1.1 select_reduce_fusion
  1.8 0.0 copy-done
  1.8 0.6 gather_fusion
  2.4 1.6 %gather_fusion.1 = bf16[16,8,2048]{2,1,0:T(8,128)(2,1)S(1)} fusion(bf16[16,8,2048]{2,1,0:T(8,128)(2,1)} %bitcast.25, s32[1024]{0:T(1024)S(1)} %pad_clamp_fusion), kind=kCustom, calls=%fused_computation.1.clone | custom fusion | bytes 1048640 | tf_op jit(solution)/shard_map/jit(_take)/gather | solution.py:178
  4.0 0.0 copy-start.1
  4.0 0.0 copy-start.2
  4.0 0.2 broadcast_select_fusion.1
  4.2 0.2 reshape.64
  4.5 0.2 reshape.65
  4.7 0.1 copy-done.1
  4.8 0.0 copy-done.2
  4.8 0.2 broadcast_in_dim.30
  5.0 1.5 %pad_maximum_fusion = bf16[16,512,128]{2,1,0:T(8,128)(2,1)} fusion(bf16[16,256,128]{2,1,0:T(8,128)(2,1)S(1)} %broadcast_in_dim.30, bf16[16,128,128]{2,1,0:T(8,128)(2,1)S(1)} %reshape.65, bf16[16,128,128]{2,1,0:T(8,128)(2,1)S(1)} %reshape.64), kind=kLoop, calls=%fused_computation.2 | loop fusion | flops 6291456 | bytes 4194304 | tf_op jit(solution)/shard_map/concatenate | solution.py:187
  6.5 0.0 copy-start.3
  6.5 13.0 %all-to-all-start = ((bf16[16,512,128]{2,1,0:T(8,128)(2,1)}), bf16[16,512,128]{2,1,0:T(8,128)(2,1)S(1)}, u32[]{:S(2)}, u32[]{:S(2)}) async-start(bf16[16,512,128]{2,1,0:T(8,128)(2,1)} %pad_maximum_fusion), calls=%async_computation | async-start | bytes 4194304 | tf_op jit(solution)/shard_map/all_to_all | solution.py:195
  19.5 0.0 copy-done.3
  19.5 0.2 reduce-window.8
  19.7 0.2 multiply_reduce_fusion
  19.9 0.1 convert_reduce_fusion
  20.0 51.6 %all-to-all-done = bf16[16,512,128]{2,1,0:T(8,128)(2,1)S(1)} async-done(((bf16[16,512,128]{2,1,0:T(8,128)(2,1)}), bf16[16,512,128]{2,1,0:T(8,128)(2,1)S(1)}, u32[]{:S(2)}, u32[]{:S(2)}) %all-to-all-start) | async-done | bytes 2097184 | tf_op jit(solution)/shard_map/all_to_all | solution.py:195
  71.6 0.2 fusion
  71.8 18.3 %shard_map.85 = (bf16[2048,128]{1,0:T(8,128)(2,1)S(1)}, bf16[2048,256]{1,0:T(8,128)(2,1)}) custom-call(s32[6]{0:T(128)S(1)} %bitcast.24, s32[16]{0:T(128)S(1)} %multiply_add_fusion.start_ref, s32[1,2048]{1,0:T(1,128)S(1)} %bitcast.22, bf16[2048,128]{1,0:T(8,128)(2,1)S(1)} %bitcast.21, bf16[2048,128]{1,0:T(8,128)(2,1)S(1)} %bitcast.20, ...), custom_call_target="tpu_custom_call" | custom-call | flops 1879048192 | bytes 4718592 | tf_op jit(solution)/shard_map/pallas_call | solution.py:140
  90.2 3.7 %all-to-all-start.1 = ((bf16[16,128,256]{2,1,0:T(8,128)(2,1)}), bf16[16,128,256]{2,1,0:T(8,128)(2,1)S(1)}, u32[]{:S(2)}, u32[]{:S(2)}) async-start(bf16[16,128,256]{2,1,0:T(8,128)(2,1)} %bitcast.12), calls=%async_computation.1 | async-start | bytes 2097152 | tf_op jit(solution)/shard_map/all_to_all | solution.py:213
  93.8 0.2 reshape.70
  94.1 1.3 %collective-permute-start = (bf16[1,128,2048]{2,1,0:T(8,128)(2,1)S(1)}, bf16[1,128,2048]{2,1,0:T(8,128)(2,1)S(1)}, u32[]{:S(2)}, u32[]{:S(2)}) collective-permute-start(bf16[1,128,2048]{2,1,0:T(8,128)(2,1)S(1)} %reshape.70), channel_id=1, source_target_pairs={{128,0},{256,128},{384,256},{129,1},{257,129},{385,257},{130,2},{2... | collective-permute-start | bytes 1572872 | tf_op jit(solution)/shard_map/ppermute | solution.py:14
  95.4 2.5 %collective-permute-done = bf16[1,128,2048]{2,1,0:T(8,128)(2,1)S(1)} collective-permute-done((bf16[1,128,2048]{2,1,0:T(8,128)(2,1)S(1)}, bf16[1,128,2048]{2,1,0:T(8,128)(2,1)S(1)}, u32[]{:S(2)}, u32[]{:S(2)}) %collective-permute-start) | collective-permute-done | bytes 524320 | tf_op jit(solution)/shard_map/ppermute | solution.py:14
  97.9 26.1 %all-to-all-done.1 = bf16[16,128,256]{2,1,0:T(8,128)(2,1)S(1)} async-done(((bf16[16,128,256]{2,1,0:T(8,128)(2,1)}), bf16[16,128,256]{2,1,0:T(8,128)(2,1)S(1)}, u32[]{:S(2)}, u32[]{:S(2)}) %all-to-all-start.1) | async-done | bytes 1048608 | tf_op jit(solution)/shard_map/all_to_all | solution.py:213
  123.9 0.8 slice_reduce_fusion
  124.7 0.8 copy.10
  (4 shorter events, 0.0 us)
Async XLA Ops:
  0.6 1.2 copy-start
  4.0 0.8 copy-start.1
  4.0 0.8 copy-start.2
  6.5 13.0 %copy-start.3 = (s32[6]{0:T(128)S(1)}, s32[6]{0:T(128)}, u32[]{:S(2)}) copy-start(s32[6]{0:T(128)} %param.12) | copy-start | bytes 76
  6.5 65.1 %all-to-all-start = ((bf16[16,512,128]{2,1,0:T(8,128)(2,1)}), bf16[16,512,128]{2,1,0:T(8,128)(2,1)S(1)}, u32[]{:S(2)}, u32[]{:S(2)}) async-start(bf16[16,512,128]{2,1,0:T(8,128)(2,1)} %pad_maximum_fusion), calls=%async_computation | async-start | bytes 4194304 | tf_op jit(solution)/shard_map/all_to_all | solution.py:195
  90.2 33.8 %all-to-all-start.1 = ((bf16[16,128,256]{2,1,0:T(8,128)(2,1)}), bf16[16,128,256]{2,1,0:T(8,128)(2,1)S(1)}, u32[]{:S(2)}, u32[]{:S(2)}) async-start(bf16[16,128,256]{2,1,0:T(8,128)(2,1)} %bitcast.12), calls=%async_computation.1 | async-start | bytes 2097152 | tf_op jit(solution)/shard_map/all_to_all | solution.py:213
  94.1 3.8 %collective-permute-start = (bf16[1,128,2048]{2,1,0:T(8,128)(2,1)S(1)}, bf16[1,128,2048]{2,1,0:T(8,128)(2,1)S(1)}, u32[]{:S(2)}, u32[]{:S(2)}) collective-permute-start(bf16[1,128,2048]{2,1,0:T(8,128)(2,1)S(1)} %reshape.70), channel_id=1, source_target_pairs={{128,0},{256,128},{384,256},{129,1},{257,129},{385,257},{130,2},{2... | collective-permute-start | bytes 1572872 | tf_op jit(solution)/shard_map/ppermute | solution.py:14
